TPU v7x, 32 devices: a whole 2x2x4 slice. The times are simulated.
32 devices in a mesh: grp: 8 (over y, x, core), rep: 4 (over z).
Axes of the slice: x: 2, y: 2, z: 4, core: 2. Of those that a mesh axis runs over, the one named last changes fastest.
Arguments:
- features: bfloat16 [4096, 256], P(('grp', 'rep')), may hold values from -0.0625 to 0.0625
- weight: bfloat16 [256, 256], replicated, may hold values from -0.375 to 0.375
- preact: bfloat16 [4096, 256], P(('grp', 'rep')), may hold values from -6 to 6
- grad_out: bfloat16 [4096, 256], P(('grp', 'rep')), may hold values from -1.5 to 1.5
- degree: int32 [4096], P(('grp', 'rep')), may hold values from 1 to 64
- tile_values: bfloat16 [256, 4, 128, 128], P(('grp', 'rep')), may hold values from 0 to 1
- tile_rows: int32 [256, 4], P(('grp', 'rep')), may hold values from -1 to 3, as said below
Outputs:
- input_grad: float32 [4096, 256], P(('grp', 'rep'))
- weight_grad: float32 [256, 256], replicated
Inputs may be any that keep to these rules, and one draw needn't show every extreme that they name: `tile_rows`: each of the 8 rows of one device (aligned blocks) has up to 4 live slots; in every such block some row has all 4 slots live.
All inputs are finite; a program needn't handle non-finite values.
Results may differ from a plain program's by a relative error of at most 0.013.
Values may be sent and summed in bfloat16 or wider, within the bound.
No kernel may reach another device: no remote copies, remote signals or barrier semaphores. Data moves between devices by JAX's collectives and lax.ppermute only.
A program may use at most 128 MiB of HBM per device.

v0:
```python
import jax
import jax.numpy as jnp
from jax import lax
from jax.sharding import PartitionSpec as P


def tile_masks(tile_rows):
    tile_live = tile_rows >= 0
    clipped = jnp.where(tile_live, tile_rows, 0)
    return (tile_live, clipped)


def per_device(features, weight, preact, grad_out, degree, tile_values, tile_rows):
    rows_here = features.shape[0]
    feature_width = features.shape[1]
    tile_edge = tile_values.shape[2]
    slot_count = tile_values.shape[1]
    row_tiles = lax.axis_size("rep") * rows_here // tile_edge
    inverse = lax.rsqrt(degree.astype(jnp.float32))[:, None]
    grad_pre = jnp.where(preact > 0, grad_out, jnp.zeros_like(grad_out))
    tile_live, clipped = tile_masks(tile_rows)
    scaled = (features.astype(jnp.float32) * inverse).astype(jnp.bfloat16)
    gathered = lax.all_gather(scaled, "grp", axis=0, tiled=True)
    columns = gathered.reshape(-1, tile_edge, feature_width)
    target = jnp.where(tile_live, tile_rows, row_tiles)
    partial_value = jnp.zeros((row_tiles + 1, tile_edge, feature_width), jnp.float32)
    for slot in range(slot_count):
        product = jnp.einsum(
            "cij,cjf->cif", tile_values[:, slot], columns, preferred_element_type=jnp.float32
        )
        partial_value = partial_value.at[target[:, slot]].add(product)
    partial_value = partial_value[:row_tiles]
    summed = lax.psum_scatter(
        partial_value.reshape(row_tiles * tile_edge, feature_width).astype(jnp.bfloat16),
        "rep",
        scatter_dimension=0,
        tiled=True,
    ).astype(jnp.float32)
    aggregated = (summed * inverse).astype(jnp.bfloat16)
    weight_local = lax.dot_general(
        aggregated, grad_pre, (((0,), (0,)), ((), ())), preferred_element_type=jnp.float32
    )
    projected = (
        lax.dot_general(
            grad_pre, weight, (((1,), (1,)), ((), ())), preferred_element_type=jnp.float32
        )
        * inverse
    ).astype(jnp.bfloat16)
    block_rows = lax.all_gather(projected, "rep", axis=0, tiled=True)
    blocks = block_rows.reshape(row_tiles, tile_edge, feature_width)
    picked = jnp.take(blocks, clipped, axis=0)
    picked = jnp.where(tile_live[:, :, None, None], picked, jnp.zeros_like(picked))
    result = jnp.einsum("csij,csif->cjf", tile_values, picked, preferred_element_type=jnp.float32)
    input_grad = (
        lax.psum_scatter(
            result.reshape(rows_here * lax.axis_size("grp"), feature_width),
            "grp",
            scatter_dimension=0,
            tiled=True,
        )
        * inverse
    )
    weight_grad = lax.psum(weight_local, ("grp", "rep"))
    return (input_grad, weight_grad)


def solution(mesh):
    return jax.shard_map(
        per_device,
        mesh=mesh,
        in_specs=(
            P(("grp", "rep"), None),
            P(),
            P(("grp", "rep"), None),
            P(("grp", "rep"), None),
            P(("grp", "rep")),
            P(("grp", "rep"), None, None, None),
            P(("grp", "rep"), None),
        ),
        out_specs=(P(("grp", "rep"), None), P()),
        check_vma=False,
    )
```

profile of v0, /device:TPU:0, one launch (start us, length us, event | category | flops | bytes accessed | tf_op | source)
XLA Modules:
  0.0 254.4 jit_solution(7141739193772190387)
XLA Ops:
  7.2 0.0 copy-start
  7.2 0.0 reduce-scatter.3.cloned.1.call-start
  7.2 0.7 broadcast_select_fusion
  7.9 0.7 broadcast_compare_fusion
  8.6 0.7 convert_rsqrt_fusion
  9.3 0.0 copy-done
  9.3 1.1 fusion.5
  10.4 15.6 %all_gather.6 = bf16[512,256]{1,0:T(8,128)(2,1)S(1)} all-gather(bf16[128,256]{1,0:T(8,128)(2,1)S(1)} %fusion.5), channel_id=1, replica_groups=mesh['grp'=8,'rep'=4] {'rep'}, dimensions={0}, use_global_device_ids=true | all-gather | bytes 327680 | tf_op jit(solution)/shard_map/all_gather | solution.py:49
  26.0 0.1 copy.27
  26.1 0.1 reshape.27
  26.2 0.1 copy.25
  26.3 0.7 copy.26
  26.9 0.0 copy-start.1
  26.9 0.7 gather_fusion
  27.6 0.5 copy-done.1
  28.1 0.0 copy-start.4
  28.1 2.4 fusion
  30.5 0.0 reduce-scatter.3.cloned.1.call-update
  30.5 0.0 reduce-scatter.5.cloned.1.call-start
  30.6 0.5 fusion.21
  31.1 37.1 %reduce-scatter.3.cloned.1.call-done = f32[128,256]{1,0:T(8,128)} async-done(((f32[1024,256]{1,0:T(8,128)}), f32[128,256]{1,0:T(8,128)}) %reduce-scatter.3.cloned.1.call-update) | async-done | bytes 131088 | tf_op jit(solution)/shard_map/reduce_scatter | solution.py:55
  68.2 0.0 copy-done.4
  68.3 1.6 multiply_convert_fusion.1
  69.9 9.8 %all_gather.7 = bf16[1024,256]{1,0:T(8,128)(2,1)S(1)} all-gather(bf16[128,256]{1,0:T(8,128)(2,1)S(1)} %get-tuple-element.10), channel_id=1, replica_groups=mesh['grp'=8,'rep'=4] {'grp'}, dimensions={0}, use_global_device_ids=true | all-gather | bytes 589824 | tf_op jit(solution)/shard_map/all_gather | solution.py:23
  79.7 1.4 convolution_bitcast_fusion.3
  81.1 0.3 convolution_bitcast_fusion.2
  81.4 0.3 convolution_bitcast_fusion.1
  81.8 1.3 convolution_bitcast_fusion
  83.1 2.6 %copy.31 = f32[8,128,256]{2,1,0:T(8,128)} copy(f32[8,128,256]{1,2,0:T(8,128)} %convolution_bitcast_fusion.3) | data formatting | bytes 2097152 | tf_op jit(solution)/shard_map/cij,cjf->cif/dot_general | solution.py:28
  85.6 1.4 copy.34
  87.0 0.0 copy-start.6
  87.0 0.3 copy.37
  87.3 0.3 copy.40
  87.7 0.0 copy-start.5
  87.7 0.0 copy-done.6
  87.7 2.5 scatter_fusion
  90.2 0.0 copy-done.5
  90.2 2.5 scatter_fusion.1
  92.7 1.3 scatter_fusion.2
  94.0 0.0 copy-start.2
  94.0 0.0 copy-start.3
  94.0 1.3 scatter_fusion.3
  95.4 0.7 slice.61
  96.1 0.0 reduce-scatter.5.cloned.1.call-update
  96.1 0.0 all-reduce.2.cloned.1.call-start
  96.2 19.7 %reduce-scatter.5.cloned.1.call-done = bf16[128,256]{1,0:T(8,128)(2,1)} async-done(((bf16[512,256]{1,0:T(8,128)(2,1)}), bf16[128,256]{1,0:T(8,128)(2,1)}) %reduce-scatter.5.cloned.1.call-update) | async-done | bytes 65552 | tf_op jit(solution)/shard_map/reduce_scatter | solution.py:33
  115.9 0.0 copy-done.2
  115.9 0.0 copy-done.3
  115.9 1.8 fusion.16
  117.7 0.0 all-reduce.2.cloned.1.call-update
  117.8 128.5 %all-reduce.2.cloned.1.call-done = f32[256,256]{1,0:T(8,128)} async-done(((f32[256,256]{1,0:T(8,128)}), f32[256,256]{1,0:T(8,128)}) %all-reduce.2.cloned.1.call-update) | async-done | bytes 262160 | tf_op jit(solution)/shard_map/psum | solution.py:63
  246.2 1.7 copy.56
  (2 shorter events, 0.1 us)
Async XLA Ops:
  7.2 2.1 copy-start
  7.2 61.1 %reduce-scatter.3.cloned.1.call-start = ((), (), s32[]{:S(2)}) async-start(), calls=%async_computation.2 | async-start | bytes 1179648 | tf_op jit(solution)/shard_map/reduce_scatter | solution.py:55
  26.9 1.2 copy-start.1
  28.1 40.1 %copy-start.4 = (bf16[128,256]{1,0:T(8,128)(2,1)S(1)}, bf16[128,256]{1,0:T(8,128)(2,1)}, u32[]{:S(2)}) copy-start(bf16[128,256]{1,0:T(8,128)(2,1)} %param.7) | copy-start | bytes 196612
  30.5 85.4 %reduce-scatter.5.cloned.1.call-start = ((), (), s32[]{:S(2)}) async-start(), calls=%async_computation.3 | async-start | bytes 327680 | tf_op jit(solution)/shard_map/reduce_scatter | solution.py:33
  87.0 0.8 copy-start.6
  87.7 2.5 %copy-start.5 = (s32[8]{0:T(128)S(1)}, s32[8]{0:T(128)}, u32[]{:S(2)}) copy-start(s32[8]{0:T(128)} %get-tuple-element.4) | copy-start | bytes 100
  94.0 21.9 %copy-start.2 = (bf16[128,256]{1,0:T(8,128)(2,1)S(1)}, bf16[128,256]{1,0:T(8,128)(2,1)}, u32[]{:S(2)}) copy-start(bf16[128,256]{1,0:T(8,128)(2,1)} %param.10) | copy-start | bytes 196612
  94.0 21.9 %copy-start.3 = (bf16[128,256]{1,0:T(8,128)(2,1)S(1)}, bf16[128,256]{1,0:T(8,128)(2,1)}, u32[]{:S(2)}) copy-start(bf16[128,256]{1,0:T(8,128)(2,1)} %param.9) | copy-start | bytes 196612
  96.1 150.1 %all-reduce.2.cloned.1.call-start = ((), (), s32[]{:S(2)}) async-start(), calls=%async_computation.4 | async-start | bytes 524288 | tf_op jit(solution)/shard_map/psum | solution.py:63
Sparse Core Ops, SparseCore 0:
  30.7 37.5 reduce-scatter.2
  96.2 19.6 reduce-scatter.4
  122.9 123.2 all-reduce.1
where the time goes:
time: 255 us; the launch traced here: 254 us
  waiting for transfers between devices  185 us (73%)
  blocking collectives  25.4 us (10%)
  between operations  13.9 us (5%)
  other arithmetic  11.8 us (5%)
  local copies, waits for them, and re-layouts  9.19 us (4%)
  matrix products  8.63 us (3%)
    psum x1, waiting for transfers between devices, per_device(): weight_grad = lax.psum(weight_local, ('grp', 'rep'))  128 us
    reduce_scatter x1, waiting for transfers between devices, per_device(): lax.psum_scatter(result.reshape(rows_here * lax.axis_size('grp'), feature...  37.1 us
    reduce_scatter x1, waiting for transfers between devices, per_device(): lax.psum_scatter(partial_value.reshape(row_tiles * tile_edge, feature_wid...  19.7 us
    all_gather x1, blocking collectives, per_device(): block_rows = lax.all_gather(projected, 'rep', axis=0, tiled=True)  15.6 us
    all_gather x1, blocking collectives, per_device(): gathered = lax.all_gather(scaled, 'grp', axis=0, tiled=True)  9.77 us
    scatter-add x4, other arithmetic, per_device(): partial_value = partial_value.at[target[:, slot]].add(product)  7.55 us
  transfers between devices with their start and end apart: 3, of which 3 were waited for; matrix products, arithmetic and copies ran while one was open for 0% of the time, Pallas kernels for 0%

commit v1 on v0

v1 whole, which is shorter than its diff:
```python
import jax
import jax.numpy as jnp
from jax import lax
from jax.sharding import PartitionSpec as P

HIGHEST = lax.Precision.HIGHEST


def gather_rep(x):
    reps = lax.axis_size("rep")
    me = lax.axis_index("rep")
    parts = [x]
    for shift in range(1, reps):
        parts.append(lax.ppermute(x, "rep", [((i + shift) % reps, i) for i in range(reps)]))
    stacked = jnp.stack(parts)
    return jnp.roll(stacked, me, axis=0)


def all_reduce_a2a(w, axes):
    count = 1
    for name in axes:
        count *= lax.axis_size(name)
    chunks = w.reshape(count, -1)
    owned = lax.all_to_all(chunks, axes, 0, 0, tiled=True).reshape(count, -1).sum(0)
    spread = jnp.broadcast_to(owned[None], (count, owned.shape[0]))
    return lax.all_to_all(spread, axes, 0, 0, tiled=True).reshape(w.shape)


def per_device(features, weight, preact, grad_out, degree, tile_values, tile_rows):
    rows_here, width = features.shape
    col_tiles, slots, edge, _ = tile_values.shape
    reps = lax.axis_size("rep")
    row_tiles = reps * rows_here // edge
    inverse = lax.rsqrt(degree.astype(jnp.float32))[:, None]
    grad_pre = jnp.where(preact > 0, grad_out, jnp.zeros_like(grad_out))
    scaled = (features.astype(jnp.float32) * inverse).astype(jnp.bfloat16)
    projected = (
        lax.dot_general(
            grad_pre, weight, (((1,), (1,)), ((), ())), preferred_element_type=jnp.float32
        )
        * inverse
    ).astype(jnp.bfloat16)

    columns = lax.all_gather(scaled, "grp", axis=0, tiled=True).reshape(col_tiles, edge, width)
    degree_lanes = jnp.broadcast_to(degree.astype(jnp.bfloat16)[:, None], (rows_here, 128))
    packed = jnp.concatenate([projected, grad_pre, degree_lanes], axis=1)
    block = gather_rep(packed).reshape(reps * rows_here, -1)
    block_proj = block[:, :width].reshape(row_tiles, edge, width)
    block_grad = block[:, width : 2 * width].astype(jnp.float32)
    block_inverse = lax.rsqrt(block[:, 2 * width : 2 * width + 1].astype(jnp.float32))

    tile_live = tile_rows >= 0
    clipped = jnp.where(tile_live, tile_rows, 0)
    onehot = (
        (clipped[..., None] == jnp.arange(row_tiles, dtype=jnp.int32)) & tile_live[..., None]
    ).astype(jnp.float32)

    product = jnp.einsum(
        "csij,cjf->csif", tile_values, columns, preferred_element_type=jnp.float32
    )
    partial = jnp.einsum("csh,csif->hif", onehot, product, precision=HIGHEST)
    partial = partial.reshape(row_tiles * edge, width) * block_inverse
    weight_local = lax.dot_general(
        partial, block_grad, (((0,), (0,)), ((), ())), precision=HIGHEST,
        preferred_element_type=jnp.float32,
    )

    picked = jnp.take(block_proj, clipped, axis=0)
    picked = jnp.where(tile_live[:, :, None, None], picked, jnp.zeros_like(picked))
    result = jnp.einsum("csij,csif->cjf", tile_values, picked, preferred_element_type=jnp.float32)

    terms = lax.all_to_all(result, "grp", 0, 0, tiled=True)
    input_grad = terms.sum(0) * inverse
    weight_grad = all_reduce_a2a(weight_local, ("grp", "rep"))
    return (input_grad, weight_grad)


def solution(mesh):
    return jax.shard_map(
        per_device,
        mesh=mesh,
        in_specs=(
            P(("grp", "rep"), None),
            P(),
            P(("grp", "rep"), None),
            P(("grp", "rep"), None),
            P(("grp", "rep")),
            P(("grp", "rep"), None, None, None),
            P(("grp", "rep"), None),
        ),
        out_specs=(P(("grp", "rep"), None), P()),
        check_vma=False,
    )
```

time: 255 us -> 102 us (0.40)
  waiting for transfers between devices: 185 us -> 26.3 us
  between operations: 13.9 us -> 0.85 us
  blocking collectives: 25.4 us -> 35.7 us
  starting transfers between devices: 0.12 us -> 9.98 us
  other arithmetic: 11.8 us -> 5.58 us
  matrix products: 8.63 us -> 11.8 us
    psum x1 -> x0, waiting for transfers between devices: 128 us -> none  [per_device(): weight_grad = lax.psum(weight_local, ('grp', 'rep'))]
    reduce_scatter x2 -> x0, waiting for transfers between devices: 56.9 us -> none  [the longest x1 37.1 us: per_device(): lax.psum_scatter(result.reshape(rows_here * lax.axis_size('grp'), feature...]
    all_to_all x0 -> x2, blocking collectives: none -> 26.8 us  [the longest x1 14 us: all_reduce_a2a(): lax.all_to_all(chunks, axes, 0, 0, tiled=True).reshape(count, -1).sum(0)]
    all_gather x2 -> x1, blocking collectives: 25.4 us -> 8.89 us  [per_device(): lax.all_gather(scaled, 'grp', axis=0, tiled=True)]
    all_to_all x0 -> x1, waiting for transfers between devices: none -> 15.2 us  [per_device(): terms = lax.all_to_all(result, 'grp', 0, 0, tiled=True)]
    ppermute x0 -> x3, waiting for transfers between devices: none -> 11.1 us  [gather_rep(): lax.ppermute(x, 'rep', [((i + shift) % reps, i) for i in range(reps)])]
    scatter-add x4 -> x0, other arithmetic: 7.55 us -> none  [per_device(): partial_value = partial_value.at[target[:, slot]].add(product)]
    ppermute x0 -> x3, starting transfers between devices: none -> 6.12 us  [gather_rep(): lax.ppermute(x, 'rep', [((i + shift) % reps, i) for i in range(reps)])]
  transfers between devices with their start and end apart: 3 -> 4, of which waited for: 3 -> 3; matrix products, arithmetic and copies ran while one was open for 0% -> 2% of each run, Pallas kernels for 0% -> 0%
where the time goes in v1:
time: 102 us
  blocking collectives  35.7 us (35%)
  waiting for transfers between devices  26.3 us (26%)
  matrix products  11.8 us (12%)
  local copies, waits for them, and re-layouts  11.4 us (11%)
  starting transfers between devices  9.98 us (10%)
  other arithmetic  5.58 us (5%)
    all_to_all x1, waiting for transfers between devices, per_device(): terms = lax.all_to_all(result, 'grp', 0, 0, tiled=True)  15.2 us
    all_to_all x1, blocking collectives, all_reduce_a2a(): lax.all_to_all(chunks, axes, 0, 0, tiled=True).reshape(count, -1).sum(0)  14 us
    all_to_all x1, blocking collectives, all_reduce_a2a(): return lax.all_to_all(spread, axes, 0, 0, tiled=True).reshape(w.shape)  12.7 us
    ppermute x3, waiting for transfers between devices, gather_rep(): lax.ppermute(x, 'rep', [((i + shift) % reps, i) for i in range(reps)])  11.1 us
    all_gather x1, blocking collectives, per_device(): lax.all_gather(scaled, 'grp', axis=0, tiled=True)  8.89 us
    ppermute x3, starting transfers between devices, gather_rep(): lax.ppermute(x, 'rep', [((i + shift) % reps, i) for i in range(reps)])  6.12 us
    dot_general x1, local copies, waits for them, and re-layouts, per_device(): jnp.einsum('csij,cjf->csif', tile_values, columns, preferred_element_type...  5.51 us
    dot_general x1, matrix products, per_device(): partial = jnp.einsum('csh,csif->hif', onehot, product, precision=HIGHEST)  4.02 us
  transfers between devices with their start and end apart: 4, of which 3 were waited for; matrix products, arithmetic and copies ran while one was open for 2% of the time, Pallas kernels for 0%

profile of v1, /device:TPU:0, one launch (start us, length us, event | category | flops | bytes accessed | tf_op | source)
XLA Modules:
  0.0 101.6 jit_solution(6074562311005059718)
XLA Ops:
  0.6 0.0 copy-start
  0.6 0.7 convert_rsqrt_fusion
  1.4 0.7 convert_element_type.22
  2.1 0.9 compare_select_fusion
  2.9 1.1 %fusion.8 = bf16[128,256]{1,0:T(8,128)(2,1)S(1)} fusion(bf16[128,256]{1,0:T(8,128)(2,1)S(1)} %compare_select_fusion, bf16[256,256]{1,0:T(8,128)(2,1)} %param.8, f32[128]{0:T(128)S(1)} %convert_rsqrt_fusion), kind=kOutput, calls=%fused_computation.10 | convolution fusion | flops 16842752 | bytes 262656 | tf_op jit(solution)/shard_map/dot_general | solution.py:38
  4.0 0.1 broadcast_in_dim.44
  4.2 5.1 %collective-permute-start = (bf16[128,640]{1,0:T(8,128)(2,1)S(1)}, bf16[128,640]{1,0:T(8,128)(2,1)S(1)}, u32[]{:S(2)}, u32[]{:S(2)}) collective-permute-start(bf16[128,640]{1,0:T(8,128)(2,1)S(1)} %pad_maximum_fusion), channel_id=1, source_target_pairs={{1,0},{2,1},{3,2},{0,3},{5,4},{6,5},{7,6},{4,7},{9,8},{10,9},{11,1... | collective-permute-start | bytes 491528 | tf_op jit(solution)/shard_map/ppermute | solution.py:14
  9.3 0.0 collective-permute-start.1
  9.3 1.0 collective-permute-start.2
  10.3 0.7 broadcast_select_fusion
  11.0 0.7 broadcast_compare_fusion
  11.7 0.1 copy.27
  11.7 0.1 reshape.47
  11.8 0.1 copy.26
  11.9 0.1 copy.25
  12.1 1.9 %collective-permute-done = bf16[128,640]{1,0:T(8,128)(2,1)S(1)} collective-permute-done((bf16[128,640]{1,0:T(8,128)(2,1)S(1)}, bf16[128,640]{1,0:T(8,128)(2,1)S(1)}, u32[]{:S(2)}, u32[]{:S(2)}) %collective-permute-start) | collective-permute-done | bytes 163872 | tf_op jit(solution)/shard_map/ppermute | solution.py:14
  13.9 9.2 %collective-permute-done.1 = bf16[128,640]{1,0:T(8,128)(2,1)S(1)} collective-permute-done((bf16[128,640]{1,0:T(8,128)(2,1)S(1)}, bf16[128,640]{1,0:T(8,128)(2,1)S(1)}, u32[]{:S(2)}, u32[]{:S(2)}) %collective-permute-start.1) | collective-permute-done | bytes 163872 | tf_op jit(solution)/shard_map/ppermute | solution.py:14
  23.2 0.0 collective-permute-done.2
  23.3 0.1 constant_dynamic-slice_fusion
  23.4 0.0 copy-start.1
  23.4 0.8 copy-done.1
  24.3 0.7 gather_fusion
  24.9 2.4 %copy.28 = bf16[8,4,128,256]{2,3,1,0:T(8,128)(2,1)} copy(bf16[8,4,128,256]{3,2,1,0:T(8,128)(2,1)S(1)} %bitcast.43) | data formatting | bytes 4194304 | tf_op jit(solution)/shard_map/jit(_take)/gather | solution.py:68
  27.3 0.0 copy-done
  27.3 3.3 %fusion.5 = f32[8,128,256]{1,2,0:T(8,128)} fusion(bf16[8,4,128,128]{3,2,1,0:T(8,128)(2,1)S(1)} %copy-done, bf16[8,4,128,256]{2,3,1,0:T(8,128)(2,1)} %copy.28, pred[8,4]{1,0:T(8,128)(4,1)S(1)} %copy.26, pred[8,4]{1,0:T(8,128)(4,1)S(1)} %copy.25), kind=kOutput, calls=%fused_computation.7 | convolution fusion | flops 270532608 | bytes 4194368 | tf_op jit(solution)/shard_map/csij,csif->cjf/dot_general | solution.py:70
  30.7 0.0 copy-start.2
  30.7 3.9 %all-to-all-start = ((f32[8,128,256]{1,2,0:T(8,128)}), f32[8,128,256]{1,2,0:T(8,128)S(1)}, u32[]{:S(2)}, u32[]{:S(2)}) async-start(f32[8,128,256]{1,2,0:T(8,128)} %fusion.5), calls=%async_computation | async-start | bytes 2097152 | tf_op jit(solution)/shard_map/all_to_all | solution.py:72
  34.6 0.0 copy-done.2
  34.6 0.0 copy-start.3
  34.6 0.2 rsqrt_reduce_fusion
  34.7 15.2 %all-to-all-done = f32[8,128,256]{1,2,0:T(8,128)S(1)} async-done(((f32[8,128,256]{1,2,0:T(8,128)}), f32[8,128,256]{1,2,0:T(8,128)S(1)}, u32[]{:S(2)}, u32[]{:S(2)}) %all-to-all-start) | async-done | bytes 1048608 | tf_op jit(solution)/shard_map/all_to_all | solution.py:72
  50.0 0.1 reduce_sum.18
  50.0 0.1 copy.29
  50.1 0.0 copy-done.3
  50.1 0.7 multiply_convert_fusion
  50.9 8.9 %all_gather.3 = bf16[1024,256]{1,0:T(8,128)(2,1)S(1)} all-gather(bf16[128,256]{1,0:T(8,128)(2,1)S(1)} %get-tuple-element.6), channel_id=1, replica_groups=mesh['grp'=8,'rep'=4] {'grp'}, dimensions={0}, use_global_device_ids=true | all-gather | bytes 589824 | tf_op jit(solution)/shard_map/all_gather | solution.py:44
  59.8 2.7 %convolution_bitcast_fusion = f32[8,4,128,256]{2,3,1,0:T(8,128)} fusion(bf16[8,128,256,1]{2,1,3,0:T(8,128)(2,1)S(1)} %bitcast.47, bf16[8,4,128,128]{3,2,1,0:T(8,128)(2,1)S(1)} %copy-done), kind=kOutput, calls=%fused_computation.1 | convolution fusion | flops 268435456 | bytes 5767168 | tf_op jit(solution)/shard_map/csij,cjf->csif/dot_general | solution.py:58
  62.5 5.5 %copy.31 = f32[8,4,128,256]{3,0,1,2:T(8,128)} copy(f32[8,4,128,256]{2,3,1,0:T(8,128)} %convolution_bitcast_fusion) | data formatting | bytes 8388608 | tf_op jit(solution)/shard_map/csij,cjf->csif/dot_general | solution.py:58
  68.0 4.0 %convolution_bitcast_fusion.1 = f32[4,128,256]{2,0,1:T(4,128)S(1)} fusion(f32[8,4,128,256]{3,0,1,2:T(8,128)} %copy.31, s32[8,4]{0,1:T(4,128)S(1)} %get-tuple-element.2, pred[8,4]{0,1:T(4,128)(4,1)S(1)} %get-tuple-element.4), kind=kOutput, calls=%fused_computation.8 | convolution fusion | flops 50331904 | bytes 4718752 | tf_op jit(solution)/shard_map/csh,csif->hif/dot_general | solution.py:61
  72.0 0.1 copy.32
  72.1 0.1 bitcast_multiply_fusion
  72.2 0.6 fusion.11
  72.9 0.3 all_to_all.17
  73.1 14.0 %all_to_all.21 = f32[32,1,2048]{2,1,0:T(1,128)S(1)} all-to-all(f32[32,1,2048]{2,1,0:T(1,128)S(1)} %all_to_all.17), channel_id=1, replica_groups=mesh['grp'=8,'rep'=4] {'grp','rep'}, dimensions={0} | all-to-all | bytes 524288 | tf_op jit(solution)/shard_map/all_to_all | solution.py:24
  87.2 0.2 reduce_sum.19
  87.3 0.1 broadcast_in_dim.48
  87.5 12.7 %all_to_all.22 = f32[32,1,2048]{2,1,0:T(1,128)S(1)} all-to-all(f32[32,1,2048]{2,1,0:T(1,128)S(1)} %broadcast_in_dim.48), channel_id=1, replica_groups=mesh['grp'=8,'rep'=4] {'grp','rep'}, dimensions={0} | all-to-all | bytes 524288 | tf_op jit(solution)/shard_map/all_to_all | solution.py:26
  100.2 0.6 reduce.2
  100.8 0.7 reshape.44
  (11 shorter events, 0.2 us)
Async XLA Ops:
  0.6 26.7 %copy-start = (bf16[8,4,128,128]{3,2,1,0:T(8,128)(2,1)S(1)}, bf16[8,4,128,128]{3,2,1,0:T(8,128)(2,1)}, u32[]{:S(2)}) copy-start(bf16[8,4,128,128]{3,2,1,0:T(8,128)(2,1)} %param.12) | copy-start | bytes 3145732
  4.2 9.8 %collective-permute-start = (bf16[128,640]{1,0:T(8,128)(2,1)S(1)}, bf16[128,640]{1,0:T(8,128)(2,1)S(1)}, u32[]{:S(2)}, u32[]{:S(2)}) collective-permute-start(bf16[128,640]{1,0:T(8,128)(2,1)S(1)} %pad_maximum_fusion), channel_id=1, source_target_pairs={{1,0},{2,1},{3,2},{0,3},{5,4},{6,5},{7,6},{4,7},{9,8},{10,9},{11,1... | collective-permute-start | bytes 491528 | tf_op jit(solution)/shard_map/ppermute | solution.py:14
  9.3 13.9 %collective-permute-start.1 = (bf16[128,640]{1,0:T(8,128)(2,1)S(1)}, bf16[128,640]{1,0:T(8,128)(2,1)S(1)}, u32[]{:S(2)}, u32[]{:S(2)}) collective-permute-start(bf16[128,640]{1,0:T(8,128)(2,1)S(1)} %pad_maximum_fusion), channel_id=1, source_target_pairs={{2,0},{3,1},{0,2},{1,3},{6,4},{7,5},{4,6},{5,7},{10,8},{11,9},{8,1... | collective-permute-start | bytes 491528 | tf_op jit(solution)/shard_map/ppermute | solution.py:14
  9.3 13.9 %collective-permute-start.2 = (bf16[128,640]{1,0:T(8,128)(2,1)S(1)}, bf16[128,640]{1,0:T(8,128)(2,1)S(1)}, u32[]{:S(2)}, u32[]{:S(2)}) collective-permute-start(bf16[128,640]{1,0:T(8,128)(2,1)S(1)} %pad_maximum_fusion), channel_id=1, source_target_pairs={{3,0},{0,1},{1,2},{2,3},{7,4},{4,5},{5,6},{6,7},{11,8},{8,9},{9,10... | collective-permute-start | bytes 491528 | tf_op jit(solution)/shard_map/ppermute | solution.py:14
  23.4 0.8 copy-start.1
  30.7 3.9 %copy-start.2 = (bf16[4,128,640]{2,1,0:T(8,128)(2,1)S(1)}, bf16[4,128,640]{2,1,0:T(8,128)(2,1)}, u32[]{:S(2)}) copy-start(bf16[4,128,640]{2,1,0:T(8,128)(2,1)} %copy-done.1) | copy-start | bytes 1966084
  30.7 19.3 %all-to-all-start = ((f32[8,128,256]{1,2,0:T(8,128)}), f32[8,128,256]{1,2,0:T(8,128)S(1)}, u32[]{:S(2)}, u32[]{:S(2)}) async-start(f32[8,128,256]{1,2,0:T(8,128)} %fusion.5), calls=%async_computation | async-start | bytes 2097152 | tf_op jit(solution)/shard_map/all_to_all | solution.py:72
  34.6 15.6 %copy-start.3 = (bf16[128,256]{1,0:T(8,128)(2,1)S(1)}, bf16[128,256]{1,0:T(8,128)(2,1)}, u32[]{:S(2)}) copy-start(bf16[128,256]{1,0:T(8,128)(2,1)} %param.7) | copy-start | bytes 196612

commit v2 on v1

v2 whole, which is shorter than its diff:
```python
import jax
import jax.numpy as jnp
from jax import lax
from jax.sharding import PartitionSpec as P

HIGHEST = lax.Precision.HIGHEST


def all_reduce_a2a(w, axes):
    count = 1
    for name in axes:
        count *= lax.axis_size(name)
    chunks = w.reshape(count, -1)
    owned = lax.all_to_all(chunks, axes, 0, 0, tiled=True).reshape(count, -1).sum(0)
    spread = jnp.broadcast_to(owned[None], (count, owned.shape[0]))
    return lax.all_to_all(spread, axes, 0, 0, tiled=True).reshape(w.shape)


def gather_axis(x, axis):
    count = lax.axis_size(axis)
    me = lax.axis_index(axis)
    parts = [x]
    for shift in range(1, count):
        parts.append(lax.ppermute(x, axis, [((i + shift) % count, i) for i in range(count)]))
    stacked = jnp.stack(parts)
    return jnp.roll(stacked, me, axis=0)


def per_device(features, weight, preact, grad_out, degree, tile_values, tile_rows):
    rows_here, width = features.shape
    col_tiles, slots, edge, _ = tile_values.shape
    reps = lax.axis_size("rep")
    row_tiles = reps * rows_here // edge
    inverse = lax.rsqrt(degree.astype(jnp.float32))[:, None]
    grad_pre = jnp.where(preact > 0, grad_out, jnp.zeros_like(grad_out))
    scaled = (features.astype(jnp.float32) * inverse).astype(jnp.bfloat16)

    columns = gather_axis(scaled, "grp").reshape(col_tiles, edge, width)
    degree_row = jnp.zeros((16, width), jnp.bfloat16).at[0, :rows_here].set(
        degree.astype(jnp.bfloat16)
    )
    packed = jnp.concatenate([grad_pre, degree_row], axis=0)
    block = gather_axis(packed, "rep")
    block_grad = block[:, :rows_here].reshape(reps * rows_here, width)
    block_degree = block[:, rows_here, :rows_here].reshape(reps * rows_here, 1)
    block_inverse = lax.rsqrt(block_degree.astype(jnp.float32))
    block_proj = (
        lax.dot_general(
            block_grad, weight, (((1,), (1,)), ((), ())), preferred_element_type=jnp.float32
        )
        * block_inverse
    ).astype(jnp.bfloat16).reshape(row_tiles, edge, width)

    hit = tile_rows[None] == jnp.arange(row_tiles, dtype=jnp.int32)[:, None, None]
    masked = jnp.where(hit[..., None, None], tile_values[None], jnp.zeros_like(tile_values[None]))

    partial = jnp.einsum("hcsij,cjf->hif", masked, columns, preferred_element_type=jnp.float32)
    partial = partial.reshape(row_tiles * edge, width) * block_inverse
    weight_local = lax.dot_general(
        partial, block_grad.astype(jnp.float32), (((0,), (0,)), ((), ())), precision=HIGHEST,
        preferred_element_type=jnp.float32,
    )

    result = jnp.einsum("hcsij,hif->cjf", masked, block_proj, preferred_element_type=jnp.float32)

    terms = lax.all_to_all(result.astype(jnp.bfloat16), "grp", 0, 0, tiled=True)
    input_grad = terms.astype(jnp.float32).sum(0) * inverse
    weight_grad = all_reduce_a2a(weight_local, ("grp", "rep"))
    return (input_grad, weight_grad)


def solution(mesh):
    return jax.shard_map(
        per_device,
        mesh=mesh,
        in_specs=(
            P(("grp", "rep"), None),
            P(),
            P(("grp", "rep"), None),
            P(("grp", "rep"), None),
            P(("grp", "rep")),
            P(("grp", "rep"), None, None, None),
            P(("grp", "rep"), None),
        ),
        out_specs=(P(("grp", "rep"), None), P()),
        check_vma=False,
    )
```

time: 102 us -> 92.2 us (0.904)
  blocking collectives: 35.7 us -> 0 us
  starting transfers between devices: 9.98 us -> 25.1 us
  waiting for transfers between devices: 26.3 us -> 40.7 us
  matrix products: 11.8 us -> 2.59 us
  local copies, waits for them, and re-layouts: 11.4 us -> 14.5 us
  other arithmetic: 5.58 us -> 7.95 us
    all_to_all x2 -> x0, blocking collectives: 26.8 us -> none  [the longest x1 14 us: all_reduce_a2a(): lax.all_to_all(chunks, axes, 0, 0, tiled=True).reshape(count, -1).sum(0)]
    all_to_all x1 -> x3, waiting for transfers between devices: 15.2 us -> 27.5 us  [the longest x1 9.51 us: per_device(): terms = lax.all_to_all(result.astype(jnp.bfloat16), 'grp', 0, 0, tiled=True)]
    unnamed x13 -> x24, local copies, waits for them, and re-layouts: 0.94 us -> 10.6 us
    dot_general x5 -> x4, matrix products: 11.8 us -> 2.59 us  [the longest x1 1.28 us: per_device(): jnp.einsum('hcsij,hif->cjf', masked, block_proj, preferred_element_type=j...]
    all_gather x1 -> x0, blocking collectives: 8.89 us -> none  [per_device(): lax.all_gather(scaled, 'grp', axis=0, tiled=True)]
    ppermute x3 -> x10, starting transfers between devices: 6.12 us -> 14.4 us  [gather_axis(): lax.ppermute(x, axis, [((i + shift) % count, i) for i in range(count)])]
    all_to_all x1 -> x3, starting transfers between devices: 3.86 us -> 10.7 us  [the longest x1 4.59 us: all_reduce_a2a(): lax.all_to_all(chunks, axes, 0, 0, tiled=True).reshape(count, -1).sum(0)]
    dot_general x2 -> x1, local copies, waits for them, and re-layouts: 5.61 us -> 0.68 us  [per_device(): jnp.einsum('hcsij,cjf->hif', masked, columns, preferred_element_type=jnp....]
  transfers between devices with their start and end apart: 4 -> 13, of which waited for: 3 -> 8; matrix products, arithmetic and copies ran while one was open for 2% -> 20% of each run, Pallas kernels for 0% -> 0%
where the time goes in v2:
time: 92.2 us; the launch traced here: 91.7 us
  waiting for transfers between devices  40.7 us (44%)
  starting transfers between devices  25.1 us (27%)
  local copies, waits for them, and re-layouts  14.5 us (16%)
  other arithmetic  7.95 us (9%)
  matrix products  2.59 us (3%)
    ppermute x10, starting transfers between devices, gather_axis(): lax.ppermute(x, axis, [((i + shift) % count, i) for i in range(count)])  14.4 us
    ppermute x10, waiting for transfers between devices, gather_axis(): lax.ppermute(x, axis, [((i + shift) % count, i) for i in range(count)])  13.2 us
    unnamed x24, local copies, waits for them, and re-layouts  10.6 us
    all_to_all x1, waiting for transfers between devices, per_device(): terms = lax.all_to_all(result.astype(jnp.bfloat16), 'grp', 0, 0, tiled=True)  9.51 us
    all_to_all x1, waiting for transfers between devices, all_reduce_a2a(): return lax.all_to_all(spread, axes, 0, 0, tiled=True).reshape(w.shape)  9.38 us
    all_to_all x1, waiting for transfers between devices, all_reduce_a2a(): lax.all_to_all(chunks, axes, 0, 0, tiled=True).reshape(count, -1).sum(0)  8.64 us
    all_to_all x1, starting transfers between devices, all_reduce_a2a(): lax.all_to_all(chunks, axes, 0, 0, tiled=True).reshape(count, -1).sum(0)  4.59 us
    all_to_all x1, starting transfers between devices, per_device(): terms = lax.all_to_all(result.astype(jnp.bfloat16), 'grp', 0, 0, tiled=True)  3.49 us
  transfers between devices with their start and end apart: 13, of which 8 were waited for; matrix products, arithmetic and copies ran while one was open for 20% of the time, Pallas kernels for 0%

profile of v2, /device:TPU:0, one launch (start us, length us, event | category | flops | bytes accessed | tf_op | source)
XLA Modules:
  0.0 91.7 jit_solution(13890283898200614362)
XLA Ops:
  0.6 0.0 copy-start
  0.6 0.7 convert_bitcast_fusion
  1.3 0.9 compare_select_fusion
  2.2 4.1 %collective-permute-start.1 = (bf16[144,256]{1,0:T(8,128)(2,1)S(1)}, bf16[144,256]{1,0:T(8,128)(2,1)S(1)}, u32[]{:S(2)}, u32[]{:S(2)}) collective-permute-start(bf16[144,256]{1,0:T(8,128)(2,1)S(1)} %fusion.12), channel_id=1, source_target_pairs={{2,0},{3,1},{0,2},{1,3},{6,4},{7,5},{4,6},{5,7},{10,8},{11,9},{8,1... | collective-permute-start | bytes 221192 | tf_op jit(solution)/shard_map/ppermute | solution.py:24
  6.3 1.3 %collective-permute-start = (bf16[144,256]{1,0:T(8,128)(2,1)S(1)}, bf16[144,256]{1,0:T(8,128)(2,1)S(1)}, u32[]{:S(2)}, u32[]{:S(2)}) collective-permute-start(bf16[144,256]{1,0:T(8,128)(2,1)S(1)} %fusion.12), channel_id=1, source_target_pairs={{1,0},{2,1},{3,2},{0,3},{5,4},{6,5},{7,6},{4,7},{9,8},{10,9},{11,1... | collective-permute-start | bytes 221192 | tf_op jit(solution)/shard_map/ppermute | solution.py:24
  7.7 0.7 collective-permute-start.2
  8.4 0.7 convert_rsqrt_fusion
  9.0 1.5 %bitcast_dynamic-update-slice_fusion.22 = (bf16[16,128,256]{2,1,0:T(8,128)(2,1)}, bf16[128,256]{1,0:T(8,128)(2,1)S(1)}) fusion(f32[128]{0:T(128)S(1)} %convert_rsqrt_fusion, bf16[128,256]{1,0:T(8,128)(2,1)} %param.9), kind=kLoop, calls=%fused_computation.38 | loop fusion | flops 98303 | bytes 197120
  10.6 0.0 collective-permute-start.9
  10.6 2.6 %collective-permute-start.3 = (bf16[128,256]{1,0:T(8,128)(2,1)S(1)}, bf16[128,256]{1,0:T(8,128)(2,1)S(1)}, u32[]{:S(2)}, u32[]{:S(2)}) collective-permute-start(bf16[128,256]{1,0:T(8,128)(2,1)S(1)} %get-tuple-element.15), channel_id=1, source_target_pairs={{4,0},{8,4},{12,8},{16,12},{20,16},{24,20},{28,24},{0,28},{5,1},{9... | collective-permute-start | bytes 196616 | tf_op jit(solution)/shard_map/ppermute | solution.py:24
  13.2 0.8 copy.16
  14.0 2.5 %convert_reduce_fusion = bf16[4,8,128,128]{3,2,1,0:T(8,128)(2,1)S(1)} fusion(pred[4,8,4]{2,1,0:T(8,128)(4,1)S(1)} %iota_compare_fusion.1, bf16[8,4,128,128]{3,2,1,0:T(8,128)(2,1)} %param.14), kind=kLoop, calls=%fused_computation | loop fusion | flops 5767168 | bytes 2097280 | tf_op jit(solution)/shard_map/hcsij,hif->cjf/reduce_sum | solution.py:64
  16.5 0.7 copy.18
  17.2 0.0 collective-permute-done.3
  17.2 1.6 %collective-permute-start.4 = (bf16[128,256]{1,0:T(8,128)(2,1)S(1)}, bf16[128,256]{1,0:T(8,128)(2,1)S(1)}, u32[]{:S(2)}, u32[]{:S(2)}) collective-permute-start(bf16[128,256]{1,0:T(8,128)(2,1)S(1)} %get-tuple-element.15), channel_id=1, source_target_pairs={{8,0},{12,4},{16,8},{20,12},{24,16},{28,20},{0,24},{4,28},{9,1},{1... | collective-permute-start | bytes 196616 | tf_op jit(solution)/shard_map/ppermute | solution.py:24
  18.8 0.6 bitcast_dynamic-update-slice_fusion.20
  19.5 2.1 %collective-permute-done.4 = bf16[128,256]{1,0:T(8,128)(2,1)S(1)} collective-permute-done((bf16[128,256]{1,0:T(8,128)(2,1)S(1)}, bf16[128,256]{1,0:T(8,128)(2,1)S(1)}, u32[]{:S(2)}, u32[]{:S(2)}) %collective-permute-start.4) | collective-permute-done | bytes 65568 | tf_op jit(solution)/shard_map/ppermute | solution.py:24
  21.6 0.0 collective-permute-start.5
  21.6 0.6 bitcast_dynamic-update-slice_fusion.18
  22.2 3.1 %collective-permute-done.5 = bf16[128,256]{1,0:T(8,128)(2,1)S(1)} collective-permute-done((bf16[128,256]{1,0:T(8,128)(2,1)S(1)}, bf16[128,256]{1,0:T(8,128)(2,1)S(1)}, u32[]{:S(2)}, u32[]{:S(2)}) %collective-permute-start.5) | collective-permute-done | bytes 65568 | tf_op jit(solution)/shard_map/ppermute | solution.py:24
  25.3 1.5 %collective-permute-start.6 = (bf16[128,256]{1,0:T(8,128)(2,1)S(1)}, bf16[128,256]{1,0:T(8,128)(2,1)S(1)}, u32[]{:S(2)}, u32[]{:S(2)}) collective-permute-start(bf16[128,256]{1,0:T(8,128)(2,1)S(1)} %get-tuple-element.15), channel_id=1, source_target_pairs={{16,0},{20,4},{24,8},{28,12},{0,16},{4,20},{8,24},{12,28},{17,1},{... | collective-permute-start | bytes 196616 | tf_op jit(solution)/shard_map/ppermute | solution.py:24
  26.8 0.6 bitcast_dynamic-update-slice_fusion.16
  27.4 2.1 %collective-permute-done.6 = bf16[128,256]{1,0:T(8,128)(2,1)S(1)} collective-permute-done((bf16[128,256]{1,0:T(8,128)(2,1)S(1)}, bf16[128,256]{1,0:T(8,128)(2,1)S(1)}, u32[]{:S(2)}, u32[]{:S(2)}) %collective-permute-start.6) | collective-permute-done | bytes 65568 | tf_op jit(solution)/shard_map/ppermute | solution.py:24
  29.5 0.0 collective-permute-start.7
  29.5 0.6 bitcast_dynamic-update-slice_fusion.14
  30.1 3.1 %collective-permute-done.7 = bf16[128,256]{1,0:T(8,128)(2,1)S(1)} collective-permute-done((bf16[128,256]{1,0:T(8,128)(2,1)S(1)}, bf16[128,256]{1,0:T(8,128)(2,1)S(1)}, u32[]{:S(2)}, u32[]{:S(2)}) %collective-permute-start.7) | collective-permute-done | bytes 65568 | tf_op jit(solution)/shard_map/ppermute | solution.py:24
  33.2 2.5 %collective-permute-start.8 = (bf16[128,256]{1,0:T(8,128)(2,1)S(1)}, bf16[128,256]{1,0:T(8,128)(2,1)S(1)}, u32[]{:S(2)}, u32[]{:S(2)}) collective-permute-start(bf16[128,256]{1,0:T(8,128)(2,1)S(1)} %get-tuple-element.15), channel_id=1, source_target_pairs={{24,0},{28,4},{0,8},{4,12},{8,16},{12,20},{16,24},{20,28},{25,1},{... | collective-permute-start | bytes 196616 | tf_op jit(solution)/shard_map/ppermute | solution.py:24
  35.7 0.6 bitcast_dynamic-update-slice_fusion.12
  36.3 2.8 %collective-permute-done.8 = bf16[128,256]{1,0:T(8,128)(2,1)S(1)} collective-permute-done((bf16[128,256]{1,0:T(8,128)(2,1)S(1)}, bf16[128,256]{1,0:T(8,128)(2,1)S(1)}, u32[]{:S(2)}, u32[]{:S(2)}) %collective-permute-start.8) | collective-permute-done | bytes 65568 | tf_op jit(solution)/shard_map/ppermute | solution.py:24
  39.2 0.6 bitcast_dynamic-update-slice_fusion.10
  39.8 0.0 collective-permute-done.9
  39.8 0.6 bitcast_dynamic-update-slice_fusion.8
  40.4 0.6 bitcast_dynamic-update-slice_fusion.23
  41.0 0.6 bitcast_dynamic-update-slice_fusion.21
  41.7 0.6 bitcast_dynamic-update-slice_fusion.19
  42.3 0.6 bitcast_dynamic-update-slice_fusion.17
  42.9 0.6 bitcast_dynamic-update-slice_fusion.15
  43.5 0.6 bitcast_dynamic-update-slice_fusion.13
  44.2 0.6 bitcast_dynamic-update-slice_fusion.11
  44.8 0.6 bitcast_dynamic-update-slice_fusion.9
  45.4 0.0 copy-start.1
  45.4 0.0 collective-permute-done
  45.4 0.0 collective-permute-done.1
  45.5 0.0 collective-permute-done.2
  45.6 1.0 %copy-done.1 = bf16[16,128,256]{2,1,0:T(8,128)(2,1)S(1)} copy-done((bf16[16,128,256]{2,1,0:T(8,128)(2,1)S(1)}, bf16[16,128,256]{2,1,0:T(8,128)(2,1)}, u32[]{:S(2)}) %copy-start.1) | copy-done | bytes 1048600
  46.6 0.4 fusion.6
  47.1 0.6 fusion.15
  47.7 1.0 %all_to_all.17 = f32[32,1,2048]{2,1,0:T(1,128)} reshape(f32[256,256]{1,0:T(8,128)S(1)} %fusion.15) | data formatting | bytes 524288 | tf_op jit(solution)/shard_map/all_to_all | solution.py:14
  48.7 4.6 %all-to-all-start.1 = ((f32[32,1,2048]{2,1,0:T(1,128)}), f32[32,1,2048]{2,1,0:T(1,128)S(1)}, u32[]{:S(2)}, u32[]{:S(2)}) async-start(f32[32,1,2048]{2,1,0:T(1,128)} %all_to_all.17), calls=%async_computation.1 | async-start | bytes 524288 | tf_op jit(solution)/shard_map/all_to_all | solution.py:14
  53.3 0.0 copy-done
  53.3 0.3 fusion.9
  53.6 1.3 %fusion.2 = bf16[8,128,256]{2,1,0:T(8,128)(2,1)} fusion(bf16[4,8,128,128]{3,2,1,0:T(8,128)(2,1)S(1)} %convert_reduce_fusion, bf16[4,128,256,1]{2,1,3,0:T(8,128)(2,1)S(1)} %bitcast.64), kind=kOutput, calls=%fused_computation.4 | convolution fusion | flops 268435456 | bytes 1835008 | tf_op jit(solution)/shard_map/hcsij,hif->cjf/dot_general | solution.py:64
  54.8 8.6 %all-to-all-done.1 = f32[32,1,2048]{2,1,0:T(1,128)S(1)} async-done(((f32[32,1,2048]{2,1,0:T(1,128)}), f32[32,1,2048]{2,1,0:T(1,128)S(1)}, u32[]{:S(2)}, u32[]{:S(2)}) %all-to-all-start.1) | async-done | bytes 262176 | tf_op jit(solution)/shard_map/all_to_all | solution.py:14
  63.5 3.5 %all-to-all-start = ((bf16[8,128,256]{2,1,0:T(8,128)(2,1)}), bf16[8,128,256]{2,1,0:T(8,128)(2,1)S(1)}, u32[]{:S(2)}, u32[]{:S(2)}) async-start(bf16[8,128,256]{2,1,0:T(8,128)(2,1)} %fusion.2), calls=%async_computation | async-start | bytes 1048576 | tf_op jit(solution)/shard_map/all_to_all | solution.py:66
  67.0 0.2 reduce_sum.33
  67.1 9.5 %all-to-all-done = bf16[8,128,256]{2,1,0:T(8,128)(2,1)S(1)} async-done(((bf16[8,128,256]{2,1,0:T(8,128)(2,1)}), bf16[8,128,256]{2,1,0:T(8,128)(2,1)S(1)}, u32[]{:S(2)}, u32[]{:S(2)}) %all-to-all-start) | async-done | bytes 524320 | tf_op jit(solution)/shard_map/all_to_all | solution.py:66
  76.7 0.8 broadcast_in_dim.40
  77.5 2.6 %all-to-all-start.2 = ((f32[32,1,2048]{2,1,0:T(1,128)}), f32[32,1,2048]{2,1,0:T(1,128)S(1)}, u32[]{:S(2)}, u32[]{:S(2)}) async-start(f32[32,1,2048]{2,1,0:T(1,128)} %broadcast_in_dim.40), calls=%async_computation.2 | async-start | bytes 524288 | tf_op jit(solution)/shard_map/all_to_all | solution.py:16
  80.1 0.1 convert_reduce_fusion.1
  80.2 0.7 broadcast_multiply_fusion
  80.9 9.4 %all-to-all-done.2 = f32[32,1,2048]{2,1,0:T(1,128)S(1)} async-done(((f32[32,1,2048]{2,1,0:T(1,128)}), f32[32,1,2048]{2,1,0:T(1,128)S(1)}, u32[]{:S(2)}, u32[]{:S(2)}) %all-to-all-start.2) | async-done | bytes 262176 | tf_op jit(solution)/shard_map/all_to_all | solution.py:16
  90.3 0.6 reduce.3
  90.9 0.7 reshape.76
  (12 shorter events, 0.1 us)
Async XLA Ops:
  0.6 52.6 %copy-start = (bf16[256,256]{1,0:T(8,128)(2,1)S(1)}, bf16[256,256]{1,0:T(8,128)(2,1)}, u32[]{:S(2)}) copy-start(bf16[256,256]{1,0:T(8,128)(2,1)} %param.10) | copy-start | bytes 393220
  2.2 43.2 %collective-permute-start.1 = (bf16[144,256]{1,0:T(8,128)(2,1)S(1)}, bf16[144,256]{1,0:T(8,128)(2,1)S(1)}, u32[]{:S(2)}, u32[]{:S(2)}) collective-permute-start(bf16[144,256]{1,0:T(8,128)(2,1)S(1)} %fusion.12), channel_id=1, source_target_pairs={{2,0},{3,1},{0,2},{1,3},{6,4},{7,5},{4,6},{5,7},{10,8},{11,9},{8,1... | collective-permute-start | bytes 221192 | tf_op jit(solution)/shard_map/ppermute | solution.py:24
  6.3 39.1 %collective-permute-start = (bf16[144,256]{1,0:T(8,128)(2,1)S(1)}, bf16[144,256]{1,0:T(8,128)(2,1)S(1)}, u32[]{:S(2)}, u32[]{:S(2)}) collective-permute-start(bf16[144,256]{1,0:T(8,128)(2,1)S(1)} %fusion.12), channel_id=1, source_target_pairs={{1,0},{2,1},{3,2},{0,3},{5,4},{6,5},{7,6},{4,7},{9,8},{10,9},{11,1... | collective-permute-start | bytes 221192 | tf_op jit(solution)/shard_map/ppermute | solution.py:24
  7.7 37.8 %collective-permute-start.2 = (bf16[144,256]{1,0:T(8,128)(2,1)S(1)}, bf16[144,256]{1,0:T(8,128)(2,1)S(1)}, u32[]{:S(2)}, u32[]{:S(2)}) collective-permute-start(bf16[144,256]{1,0:T(8,128)(2,1)S(1)} %fusion.12), channel_id=1, source_target_pairs={{3,0},{0,1},{1,2},{2,3},{7,4},{4,5},{5,6},{6,7},{11,8},{8,9},{9,10... | collective-permute-start | bytes 221192 | tf_op jit(solution)/shard_map/ppermute | solution.py:24
  10.6 29.2 %collective-permute-start.9 = (bf16[128,256]{1,0:T(8,128)(2,1)S(1)}, bf16[128,256]{1,0:T(8,128)(2,1)S(1)}, u32[]{:S(2)}, u32[]{:S(2)}) collective-permute-start(bf16[128,256]{1,0:T(8,128)(2,1)S(1)} %get-tuple-element.15), channel_id=1, source_target_pairs={{28,0},{0,4},{4,8},{8,12},{12,16},{16,20},{20,24},{24,28},{29,1},{... | collective-permute-start | bytes 196616 | tf_op jit(solution)/shard_map/ppermute | solution.py:24
  10.6 6.7 %collective-permute-start.3 = (bf16[128,256]{1,0:T(8,128)(2,1)S(1)}, bf16[128,256]{1,0:T(8,128)(2,1)S(1)}, u32[]{:S(2)}, u32[]{:S(2)}) collective-permute-start(bf16[128,256]{1,0:T(8,128)(2,1)S(1)} %get-tuple-element.15), channel_id=1, source_target_pairs={{4,0},{8,4},{12,8},{16,12},{20,16},{24,20},{28,24},{0,28},{5,1},{9... | collective-permute-start | bytes 196616 | tf_op jit(solution)/shard_map/ppermute | solution.py:24
  17.2 4.3 %collective-permute-start.4 = (bf16[128,256]{1,0:T(8,128)(2,1)S(1)}, bf16[128,256]{1,0:T(8,128)(2,1)S(1)}, u32[]{:S(2)}, u32[]{:S(2)}) collective-permute-start(bf16[128,256]{1,0:T(8,128)(2,1)S(1)} %get-tuple-element.15), channel_id=1, source_target_pairs={{8,0},{12,4},{16,8},{20,12},{24,16},{28,20},{0,24},{4,28},{9,1},{1... | collective-permute-start | bytes 196616 | tf_op jit(solution)/shard_map/ppermute | solution.py:24
  21.6 3.7 %collective-permute-start.5 = (bf16[128,256]{1,0:T(8,128)(2,1)S(1)}, bf16[128,256]{1,0:T(8,128)(2,1)S(1)}, u32[]{:S(2)}, u32[]{:S(2)}) collective-permute-start(bf16[128,256]{1,0:T(8,128)(2,1)S(1)} %get-tuple-element.15), channel_id=1, source_target_pairs={{12,0},{16,4},{20,8},{24,12},{28,16},{0,20},{4,24},{8,28},{13,1},{... | collective-permute-start | bytes 196616 | tf_op jit(solution)/shard_map/ppermute | solution.py:24
  25.3 4.3 %collective-permute-start.6 = (bf16[128,256]{1,0:T(8,128)(2,1)S(1)}, bf16[128,256]{1,0:T(8,128)(2,1)S(1)}, u32[]{:S(2)}, u32[]{:S(2)}) collective-permute-start(bf16[128,256]{1,0:T(8,128)(2,1)S(1)} %get-tuple-element.15), channel_id=1, source_target_pairs={{16,0},{20,4},{24,8},{28,12},{0,16},{4,20},{8,24},{12,28},{17,1},{... | collective-permute-start | bytes 196616 | tf_op jit(solution)/shard_map/ppermute | solution.py:24
  29.5 3.7 %collective-permute-start.7 = (bf16[128,256]{1,0:T(8,128)(2,1)S(1)}, bf16[128,256]{1,0:T(8,128)(2,1)S(1)}, u32[]{:S(2)}, u32[]{:S(2)}) collective-permute-start(bf16[128,256]{1,0:T(8,128)(2,1)S(1)} %get-tuple-element.15), channel_id=1, source_target_pairs={{20,0},{24,4},{28,8},{0,12},{4,16},{8,20},{12,24},{16,28},{21,1},{... | collective-permute-start | bytes 196616 | tf_op jit(solution)/shard_map/ppermute | solution.py:24
  33.2 6.0 %collective-permute-start.8 = (bf16[128,256]{1,0:T(8,128)(2,1)S(1)}, bf16[128,256]{1,0:T(8,128)(2,1)S(1)}, u32[]{:S(2)}, u32[]{:S(2)}) collective-permute-start(bf16[128,256]{1,0:T(8,128)(2,1)S(1)} %get-tuple-element.15), channel_id=1, source_target_pairs={{24,0},{28,4},{0,8},{4,12},{8,16},{12,20},{16,24},{20,28},{25,1},{... | collective-permute-start | bytes 196616 | tf_op jit(solution)/shard_map/ppermute | solution.py:24
  45.4 1.2 %copy-start.1 = (bf16[16,128,256]{2,1,0:T(8,128)(2,1)S(1)}, bf16[16,128,256]{2,1,0:T(8,128)(2,1)}, u32[]{:S(2)}) copy-start(bf16[16,128,256]{2,1,0:T(8,128)(2,1)} %bitcast_dynamic-update-slice_fusion.9) | copy-start | bytes 3145732
  48.7 14.8 %all-to-all-start.1 = ((f32[32,1,2048]{2,1,0:T(1,128)}), f32[32,1,2048]{2,1,0:T(1,128)S(1)}, u32[]{:S(2)}, u32[]{:S(2)}) async-start(f32[32,1,2048]{2,1,0:T(1,128)} %all_to_all.17), calls=%async_computation.1 | async-start | bytes 524288 | tf_op jit(solution)/shard_map/all_to_all | solution.py:14
  63.5 13.2 %all-to-all-start = ((bf16[8,128,256]{2,1,0:T(8,128)(2,1)}), bf16[8,128,256]{2,1,0:T(8,128)(2,1)S(1)}, u32[]{:S(2)}, u32[]{:S(2)}) async-start(bf16[8,128,256]{2,1,0:T(8,128)(2,1)} %fusion.2), calls=%async_computation | async-start | bytes 1048576 | tf_op jit(solution)/shard_map/all_to_all | solution.py:66
  77.5 12.8 %all-to-all-start.2 = ((f32[32,1,2048]{2,1,0:T(1,128)}), f32[32,1,2048]{2,1,0:T(1,128)S(1)}, u32[]{:S(2)}, u32[]{:S(2)}) async-start(f32[32,1,2048]{2,1,0:T(1,128)} %broadcast_in_dim.40), calls=%async_computation.2 | async-start | bytes 524288 | tf_op jit(solution)/shard_map/all_to_all | solution.py:16

commit v3 on v2

v3 whole, which is shorter than its diff:
```python
import jax
import jax.numpy as jnp
from jax import lax
from jax.sharding import PartitionSpec as P

HIGHEST = lax.Precision.HIGHEST


def all_reduce_a2a(w, axes):
    count = 1
    for name in axes:
        count *= lax.axis_size(name)
    chunks = w.reshape(count, -1)
    owned = lax.all_to_all(chunks, axes, 0, 0, tiled=True).reshape(count, -1).sum(0)
    spread = jnp.broadcast_to(owned[None], (count, owned.shape[0]))
    return lax.all_to_all(spread, axes, 0, 0, tiled=True).reshape(w.shape)


def per_device(features, weight, preact, grad_out, degree, tile_values, tile_rows):
    rows_here, width = features.shape
    col_tiles, slots, edge, _ = tile_values.shape
    reps = lax.axis_size("rep")
    row_tiles = reps * rows_here // edge
    inverse = lax.rsqrt(degree.astype(jnp.float32))[:, None]
    grad_pre = jnp.where(preact > 0, grad_out, jnp.zeros_like(grad_out))
    scaled = (features.astype(jnp.float32) * inverse).astype(jnp.bfloat16)

    degree_row = jnp.zeros((16, width), jnp.bfloat16).at[0, :rows_here].set(
        degree.astype(jnp.bfloat16)
    )
    packed = jnp.concatenate([grad_pre, degree_row], axis=0)
    block = lax.all_gather(packed, "rep", axis=0, tiled=False)
    block_grad = block[:, :rows_here].reshape(reps * rows_here, width)
    block_degree = block[:, rows_here, :rows_here].reshape(reps * rows_here, 1)
    block_inverse = lax.rsqrt(block_degree.astype(jnp.float32))
    block_scaled_grad = (block_grad.astype(jnp.float32) * block_inverse).astype(jnp.bfloat16)
    block_scaled_grad = block_scaled_grad.reshape(row_tiles, edge, width)

    hit = tile_rows[None] == jnp.arange(row_tiles, dtype=jnp.int32)[:, None, None]
    masked = jnp.where(hit[..., None, None], tile_values[None], jnp.zeros_like(tile_values[None]))
    terms = jnp.einsum(
        "hcsij,hif->cjf", masked, block_scaled_grad, preferred_element_type=jnp.float32
    )

    arrived = lax.all_to_all(terms.astype(jnp.bfloat16), "grp", 0, 0, tiled=True)
    pulled = arrived.astype(jnp.float32).sum(0)

    input_grad = inverse * lax.dot_general(
        pulled, weight.astype(jnp.float32), (((1,), (1,)), ((), ())), precision=HIGHEST,
        preferred_element_type=jnp.float32,
    )
    weight_local = lax.dot_general(
        scaled.astype(jnp.float32), pulled, (((0,), (0,)), ((), ())), precision=HIGHEST,
        preferred_element_type=jnp.float32,
    )
    weight_grad = all_reduce_a2a(weight_local, ("grp", "rep"))
    return (input_grad, weight_grad)


def solution(mesh):
    return jax.shard_map(
        per_device,
        mesh=mesh,
        in_specs=(
            P(("grp", "rep"), None),
            P(),
            P(("grp", "rep"), None),
            P(("grp", "rep"), None),
            P(("grp", "rep")),
            P(("grp", "rep"), None, None, None),
            P(("grp", "rep"), None),
        ),
        out_specs=(P(("grp", "rep"), None), P()),
        check_vma=False,
    )
```

time: 92.2 us -> 67.1 us (0.73)
  blocking collectives: 0 us -> 30.1 us
  waiting for transfers between devices: 40.7 us -> 19 us
  starting transfers between devices: 25.1 us -> 6.58 us
  local copies, waits for them, and re-layouts: 14.5 us -> 2.63 us
  other arithmetic: 7.95 us -> 4.97 us
    all_gather x0 -> x1, blocking collectives: none -> 15.6 us  [per_device(): block = lax.all_gather(packed, 'rep', axis=0, tiled=False)]
    all_to_all x0 -> x1, blocking collectives: none -> 14.5 us  [all_reduce_a2a(): lax.all_to_all(chunks, axes, 0, 0, tiled=True).reshape(count, -1).sum(0)]
    ppermute x10 -> x0, starting transfers between devices: 14.4 us -> none  [gather_axis(): lax.ppermute(x, axis, [((i + shift) % count, i) for i in range(count)])]
    ppermute x10 -> x0, waiting for transfers between devices: 13.2 us -> none  [gather_axis(): lax.ppermute(x, axis, [((i + shift) % count, i) for i in range(count)])]
    unnamed x24 -> x7, local copies, waits for them, and re-layouts: 10.6 us -> 0.78 us
    all_to_all x2 -> x1, waiting for transfers between devices: 18.1 us -> 9.73 us  [per_device(): lax.all_to_all(terms.astype(jnp.bfloat16), 'grp', 0, 0, tiled=True)]
    all_to_all x2 -> x1, starting transfers between devices: 8.09 us -> 3.86 us  [per_device(): lax.all_to_all(terms.astype(jnp.bfloat16), 'grp', 0, 0, tiled=True)]
    unnamed x3 -> x0, other arithmetic: 1.56 us -> none
  transfers between devices with their start and end apart: 13 -> 2, of which waited for: 8 -> 2; matrix products, arithmetic and copies ran while one was open for 20% -> 1% of each run, Pallas kernels for 0% -> 0%
where the time goes in v3:
time: 67.1 us; the launch traced here: 66.7 us
  blocking collectives  30.1 us (45%)
  waiting for transfers between devices  19 us (28%)
  starting transfers between devices  6.58 us (10%)
  other arithmetic  4.97 us (7%)
  matrix products  2.7 us (4%)
  local copies, waits for them, and re-layouts  2.63 us (4%)
  between operations  0.73 us (1%)
    all_gather x1, blocking collectives, per_device(): block = lax.all_gather(packed, 'rep', axis=0, tiled=False)  15.6 us
    all_to_all x1, blocking collectives, all_reduce_a2a(): lax.all_to_all(chunks, axes, 0, 0, tiled=True).reshape(count, -1).sum(0)  14.5 us
    all_to_all x1, waiting for transfers between devices, per_device(): lax.all_to_all(terms.astype(jnp.bfloat16), 'grp', 0, 0, tiled=True)  9.73 us
    all_to_all x1, waiting for transfers between devices, all_reduce_a2a(): return lax.all_to_all(spread, axes, 0, 0, tiled=True).reshape(w.shape)  9.23 us
    all_to_all x1, starting transfers between devices, per_device(): lax.all_to_all(terms.astype(jnp.bfloat16), 'grp', 0, 0, tiled=True)  3.86 us
    all_to_all x1, starting transfers between devices, all_reduce_a2a(): return lax.all_to_all(spread, axes, 0, 0, tiled=True).reshape(w.shape)  2.72 us
    reduce_sum x1, other arithmetic, per_device(): jnp.einsum('hcsij,hif->cjf', masked, block_scaled_grad, preferred_element...  2.52 us
    dot_general x1, matrix products, per_device(): jnp.einsum('hcsij,hif->cjf', masked, block_scaled_grad, preferred_element...  1.36 us
  transfers between devices with their start and end apart: 2, of which 2 were waited for; matrix products, arithmetic and copies ran while one was open for 1% of the time, Pallas kernels for 0%

profile of v3, /device:TPU:0, one launch (start us, length us, event | category | flops | bytes accessed | tf_op | source)
XLA Modules:
  0.0 66.7 jit_solution(2666336555936048201)
XLA Ops:
  0.6 0.0 copy-start
  0.6 0.7 %convert_bitcast_fusion = bf16[1,128]{1,0:T(2,128)(2,1)S(1)} fusion(s32[128]{0:T(128)} %param.13), kind=kLoop, calls=%fused_computation.19 | loop fusion | flops 128 | bytes 768 | tf_op jit(solution)/shard_map/reshape.37
  1.3 0.9 %compare_select_fusion = bf16[128,256]{1,0:T(8,128)(2,1)S(1)} fusion(bf16[128,256]{1,0:T(8,128)(2,1)} %param.12, bf16[128,256]{1,0:T(8,128)(2,1)} %param.11), kind=kLoop, calls=%fused_computation.12 | loop fusion | flops 65536 | bytes 196608 | tf_op jit(solution)/shard_map/jit(_where)/select_n | solution.py:25
  2.2 15.6 %all-gather = bf16[576,256]{1,0:T(8,128)(2,1)S(1)} all-gather(bf16[144,256]{1,0:T(8,128)(2,1)S(1)} %fusion.6), channel_id=2, replica_groups=mesh['grp'=8,'rep'=4] {'rep'}, dimensions={0}, use_global_device_ids=true | all-gather | bytes 368640 | tf_op jit(solution)/shard_map/all_gather | solution.py:32
  17.9 0.8 %copy.12 = s32[8,4]{1,0:T(8,128)S(1)} copy(s32[8,4]{0,1:T(4,128)} %param.15) | data formatting | bytes 256 | tf_op args[6]
  18.7 2.5 %convert_reduce_fusion = bf16[4,8,128,128]{3,2,1,0:T(8,128)(2,1)S(1)} fusion(pred[4,8,4]{2,1,0:T(8,128)(4,1)S(1)} %iota_compare_fusion.1, bf16[8,4,128,128]{3,2,1,0:T(8,128)(2,1)} %param.14), kind=kLoop, calls=%fused_computation | loop fusion | flops 5767168 | bytes 2097280 | tf_op jit(solution)/shard_map/hcsij,hif->cjf/reduce_sum | solution.py:41
  21.2 0.0 copy-start.2
  21.2 1.4 %fusion = bf16[8,128,256]{2,1,0:T(8,128)(2,1)} fusion(bf16[4,8,128,128]{3,2,1,0:T(8,128)(2,1)S(1)} %convert_reduce_fusion, bf16[4,144,256]{2,1,0:T(8,128)(2,1)S(1)} %bitcast.18, f32[4,128]{1,0:T(4,128)S(1)} %bitcast.19), kind=kOutput, calls=%fused_computation.2 | convolution fusion | flops 268828672 | bytes 1837056 | tf_op jit(solution)/shard_map/hcsij,hif->cjf/dot_general | solution.py:41
  22.6 0.0 copy-start.1
  22.6 3.9 %all-to-all-start = ((bf16[8,128,256]{2,1,0:T(8,128)(2,1)}), bf16[8,128,256]{2,1,0:T(8,128)(2,1)S(1)}, u32[]{:S(2)}, u32[]{:S(2)}) async-start(bf16[8,128,256]{2,1,0:T(8,128)(2,1)} %fusion), calls=%async_computation | async-start | bytes 1048576 | tf_op jit(solution)/shard_map/all_to_all | solution.py:45
  26.4 0.0 copy-done.2
  26.4 9.7 %all-to-all-done = bf16[8,128,256]{2,1,0:T(8,128)(2,1)S(1)} async-done(((bf16[8,128,256]{2,1,0:T(8,128)(2,1)}), bf16[8,128,256]{2,1,0:T(8,128)(2,1)S(1)}, u32[]{:S(2)}, u32[]{:S(2)}) %all-to-all-start) | async-done | bytes 524320 | tf_op jit(solution)/shard_map/all_to_all | solution.py:45
  36.2 0.1 convert_reduce_fusion.1
  36.2 0.0 copy-done.1
  36.2 0.4 fusion.7
  36.6 0.3 all_to_all.17
  36.9 14.5 %all_to_all.21 = f32[32,1,2048]{2,1,0:T(1,128)S(1)} all-to-all(f32[32,1,2048]{2,1,0:T(1,128)S(1)} %all_to_all.17), channel_id=1, replica_groups=mesh['grp'=8,'rep'=4] {'grp','rep'}, dimensions={0} | all-to-all | bytes 524288 | tf_op jit(solution)/shard_map/all_to_all | solution.py:14
  51.4 0.2 reduce_sum.29
  51.5 0.8 %broadcast_in_dim.40 = f32[32,1,2048]{2,1,0:T(1,128)} broadcast(f32[2048]{0:T(1024)S(1)} %reduce_sum.29), dimensions={2} | broadcast | bytes 270336 | tf_op jit(solution)/shard_map/broadcast_in_dim | solution.py:15
  52.4 2.7 %all-to-all-start.2 = ((f32[32,1,2048]{2,1,0:T(1,128)}), f32[32,1,2048]{2,1,0:T(1,128)S(1)}, u32[]{:S(2)}, u32[]{:S(2)}) async-start(f32[32,1,2048]{2,1,0:T(1,128)} %broadcast_in_dim.40), calls=%async_computation.2 | async-start | bytes 524288 | tf_op jit(solution)/shard_map/all_to_all | solution.py:16
  55.1 0.0 copy-done
  55.1 1.0 %convolution_multiply_fusion = f32[128,256]{1,0:T(8,128)} fusion(f32[128,256]{1,0:T(8,128)S(1)} %convert_reduce_fusion.1, bf16[256,256]{1,0:T(8,128)(2,1)S(1)} %copy-done, f32[128]{0:T(128)S(1)} %convert_rsqrt_fusion), kind=kOutput, calls=%fused_computation.3 | convolution fusion | flops 100696064 | bytes 393728 | tf_op jit(solution)/shard_map/dot_general | solution.py:48
  56.1 9.2 %all-to-all-done.2 = f32[32,1,2048]{2,1,0:T(1,128)S(1)} async-done(((f32[32,1,2048]{2,1,0:T(1,128)}), f32[32,1,2048]{2,1,0:T(1,128)S(1)}, u32[]{:S(2)}, u32[]{:S(2)}) %all-to-all-start.2) | async-done | bytes 262176 | tf_op jit(solution)/shard_map/all_to_all | solution.py:16
  65.3 0.6 reduce.3
  65.9 0.7 %reshape.73 = f32[256,256]{1,0:T(8,128)} reshape(f32[32,2048]{1,0:T(8,128)S(1)} %reduce.3) | data formatting | bytes 524288 | tf_op jit(solution)/shard_map/reshape | solution.py:16
  (4 shorter events, 0.0 us)
Async XLA Ops:
  0.6 54.5 %copy-start = (bf16[256,256]{1,0:T(8,128)(2,1)S(1)}, bf16[256,256]{1,0:T(8,128)(2,1)}, u32[]{:S(2)}) copy-start(bf16[256,256]{1,0:T(8,128)(2,1)} %param.10) | copy-start | bytes 393220
  21.2 5.2 %copy-start.2 = (s32[128]{0:T(128)S(1)}, s32[128]{0:T(128)}, u32[]{:S(2)}) copy-start(s32[128]{0:T(128)} %param.13) | copy-start | bytes 1540
  22.6 13.7 %copy-start.1 = (bf16[128,256]{1,0:T(8,128)(2,1)S(1)}, bf16[128,256]{1,0:T(8,128)(2,1)}, u32[]{:S(2)}) copy-start(bf16[128,256]{1,0:T(8,128)(2,1)} %param.9) | copy-start | bytes 196612
  22.6 13.6 %all-to-all-start = ((bf16[8,128,256]{2,1,0:T(8,128)(2,1)}), bf16[8,128,256]{2,1,0:T(8,128)(2,1)S(1)}, u32[]{:S(2)}, u32[]{:S(2)}) async-start(bf16[8,128,256]{2,1,0:T(8,128)(2,1)} %fusion), calls=%async_computation | async-start | bytes 1048576 | tf_op jit(solution)/shard_map/all_to_all | solution.py:45
  52.4 12.9 %all-to-all-start.2 = ((f32[32,1,2048]{2,1,0:T(1,128)}), f32[32,1,2048]{2,1,0:T(1,128)S(1)}, u32[]{:S(2)}, u32[]{:S(2)}) async-start(f32[32,1,2048]{2,1,0:T(1,128)} %broadcast_in_dim.40), calls=%async_computation.2 | async-start | bytes 524288 | tf_op jit(solution)/shard_map/all_to_all | solution.py:16

commit v4 on v3

--- a/solution.py
+++ b/solution.py
@@ -29,14 +29,19 @@
         degree.astype(jnp.bfloat16)
     )
     packed = jnp.concatenate([grad_pre, degree_row], axis=0)
-    block = lax.all_gather(packed, "rep", axis=0, tiled=False)
+    me = lax.axis_index("rep")
+    parts = [packed]
+    for shift in range(1, reps):
+        parts.append(lax.ppermute(packed, "rep", [((i + shift) % reps, i) for i in range(reps)]))
+    block = jnp.stack(parts)
     block_grad = block[:, :rows_here].reshape(reps * rows_here, width)
     block_degree = block[:, rows_here, :rows_here].reshape(reps * rows_here, 1)
     block_inverse = lax.rsqrt(block_degree.astype(jnp.float32))
     block_scaled_grad = (block_grad.astype(jnp.float32) * block_inverse).astype(jnp.bfloat16)
     block_scaled_grad = block_scaled_grad.reshape(row_tiles, edge, width)
 
-    hit = tile_rows[None] == jnp.arange(row_tiles, dtype=jnp.int32)[:, None, None]
+    arrival = jnp.where(tile_rows >= 0, (tile_rows - me + reps) % reps, -1)
+    hit = arrival[None] == jnp.arange(row_tiles, dtype=jnp.int32)[:, None, None]
     masked = jnp.where(hit[..., None, None], tile_values[None], jnp.zeros_like(tile_values[None]))
     terms = jnp.einsum(
         "hcsij,hif->cjf", masked, block_scaled_grad, preferred_element_type=jnp.float32

time: 67.1 us -> 58.2 us (0.87)
  blocking collectives: 30.1 us -> 12.4 us
  starting transfers between devices: 6.58 us -> 12.7 us
  waiting for transfers between devices: 19 us -> 21.6 us
  other arithmetic: 4.97 us -> 5.7 us
  local copies, waits for them, and re-layouts: 2.63 us -> 1.95 us
    all_gather x1 -> x0, blocking collectives: 15.6 us -> none  [per_device(): block = lax.all_gather(packed, 'rep', axis=0, tiled=False)]
    ppermute x0 -> x3, starting transfers between devices: none -> 6.11 us  [per_device(): lax.ppermute(packed, 'rep', [((i + shift) % reps, i) for i in range(reps)])]
    ppermute x0 -> x3, waiting for transfers between devices: none -> 2.66 us  [per_device(): lax.ppermute(packed, 'rep', [((i + shift) % reps, i) for i in range(reps)])]
    all_to_all x1, blocking collectives: 14.5 us -> 12.4 us  [all_reduce_a2a(): lax.all_to_all(chunks, axes, 0, 0, tiled=True).reshape(count, -1).sum(0)]
    unnamed x7 -> x6, local copies, waits for them, and re-layouts: 0.78 us -> 0.02 us
    select_n x0 -> x1, other arithmetic: none -> 0.69 us  [per_device(): arrival = jnp.where(tile_rows >= 0, (tile_rows - me + reps) % reps, -1)]
  transfers between devices with their start and end apart: 2 -> 5, of which waited for: 2 -> 3; matrix products, arithmetic and copies ran while one was open for 1% -> 7% of each run, Pallas kernels for 0% -> 0%
where the time goes in v4:
time: 58.2 us; the launch traced here: 57.8 us
  waiting for transfers between devices  21.6 us (37%)
  starting transfers between devices  12.7 us (22%)
  blocking collectives  12.4 us (21%)
  other arithmetic  5.7 us (10%)
  matrix products  2.69 us (5%)
  local copies, waits for them, and re-layouts  1.95 us (3%)
  between operations  0.75 us (1%)
    all_to_all x1, blocking collectives, all_reduce_a2a(): lax.all_to_all(chunks, axes, 0, 0, tiled=True).reshape(count, -1).sum(0)  12.4 us
    all_to_all x1, waiting for transfers between devices, per_device(): lax.all_to_all(terms.astype(jnp.bfloat16), 'grp', 0, 0, tiled=True)  9.73 us
    all_to_all x1, waiting for transfers between devices, all_reduce_a2a(): return lax.all_to_all(spread, axes, 0, 0, tiled=True).reshape(w.shape)  9.23 us
    ppermute x3, starting transfers between devices, per_device(): lax.ppermute(packed, 'rep', [((i + shift) % reps, i) for i in range(reps)])  6.11 us
    all_to_all x1, starting transfers between devices, per_device(): lax.all_to_all(terms.astype(jnp.bfloat16), 'grp', 0, 0, tiled=True)  3.86 us
    all_to_all x1, starting transfers between devices, all_reduce_a2a(): return lax.all_to_all(spread, axes, 0, 0, tiled=True).reshape(w.shape)  2.72 us
    ppermute x3, waiting for transfers between devices, per_device(): lax.ppermute(packed, 'rep', [((i + shift) % reps, i) for i in range(reps)])  2.66 us
    reduce_sum x1, other arithmetic, per_device(): jnp.einsum('hcsij,hif->cjf', masked, block_scaled_grad, preferred_element...  2.52 us
  transfers between devices with their start and end apart: 5, of which 3 were waited for; matrix products, arithmetic and copies ran while one was open for 7% of the time, Pallas kernels for 0%

profile of v4, /device:TPU:0, one launch (start us, length us, event | category | flops | bytes accessed | tf_op | source)
XLA Modules:
  0.0 57.8 jit_solution(13135498213714705274)
XLA Ops:
  0.6 0.0 copy-start
  0.6 0.7 %convert_bitcast_fusion = bf16[1,128]{1,0:T(2,128)(2,1)S(1)} fusion(s32[128]{0:T(128)} %param.13), kind=kLoop, calls=%fused_computation.25 | loop fusion | flops 128 | bytes 768 | tf_op jit(solution)/shard_map/reshape.37
  1.3 0.9 %compare_select_fusion = bf16[128,256]{1,0:T(8,128)(2,1)S(1)} fusion(bf16[128,256]{1,0:T(8,128)(2,1)} %param.12, bf16[128,256]{1,0:T(8,128)(2,1)} %param.11), kind=kLoop, calls=%fused_computation.13 | loop fusion | flops 65536 | bytes 196608 | tf_op jit(solution)/shard_map/jit(_where)/select_n | solution.py:25
  2.2 5.1 %collective-permute-start = (bf16[144,256]{1,0:T(8,128)(2,1)S(1)}, bf16[144,256]{1,0:T(8,128)(2,1)S(1)}, u32[]{:S(2)}, u32[]{:S(2)}) collective-permute-start(bf16[144,256]{1,0:T(8,128)(2,1)S(1)} %get-tuple-element.15), channel_id=1, source_target_pairs={{1,0},{2,1},{3,2},{0,3},{5,4},{6,5},{7,6},{4,7},{9,8},{10,9},{11,1... | collective-permute-start | bytes 221192 | tf_op jit(solution)/shard_map/ppermute | solution.py:35
  7.3 0.0 collective-permute-start.1
  7.3 1.0 %collective-permute-start.2 = (bf16[144,256]{1,0:T(8,128)(2,1)S(1)}, bf16[144,256]{1,0:T(8,128)(2,1)S(1)}, u32[]{:S(2)}, u32[]{:S(2)}) collective-permute-start(bf16[144,256]{1,0:T(8,128)(2,1)S(1)} %get-tuple-element.15), channel_id=1, source_target_pairs={{3,0},{0,1},{1,2},{2,3},{7,4},{4,5},{5,6},{6,7},{11,8},{8,9},{9,10... | collective-permute-start | bytes 221192 | tf_op jit(solution)/shard_map/ppermute | solution.py:35
  8.4 0.7 %fusion.10 = s32[8,4]{0,1:T(4,128)S(1)} fusion(s32[8,4]{0,1:T(4,128)} %param.15, s32[]{:T(128)S(6)} %axis_index.12), kind=kLoop, calls=%fused_computation.22 | loop fusion | flops 480 | bytes 260 | tf_op jit(solution)/shard_map/jit(_where)/select_n | solution.py:43
  9.1 0.1 copy.12
  9.1 2.5 %convert_reduce_fusion = bf16[4,8,128,128]{3,2,1,0:T(8,128)(2,1)S(1)} fusion(pred[4,8,4]{2,1,0:T(8,128)(4,1)S(1)} %iota_compare_fusion.1, bf16[8,4,128,128]{3,2,1,0:T(8,128)(2,1)} %param.14), kind=kLoop, calls=%fused_computation | loop fusion | flops 5767168 | bytes 2097280 | tf_op jit(solution)/shard_map/hcsij,hif->cjf/reduce_sum | solution.py:46
  11.7 0.0 collective-permute-done
  11.7 2.7 %collective-permute-done.1 = bf16[144,256]{1,0:T(8,128)(2,1)S(1)} collective-permute-done((bf16[144,256]{1,0:T(8,128)(2,1)S(1)}, bf16[144,256]{1,0:T(8,128)(2,1)S(1)}, u32[]{:S(2)}, u32[]{:S(2)}) %collective-permute-start.1) | collective-permute-done | bytes 73760 | tf_op jit(solution)/shard_map/ppermute | solution.py:35
  14.3 0.0 collective-permute-done.2
  14.4 0.0 copy-start.2
  14.4 1.4 %fusion = bf16[8,128,256]{2,1,0:T(8,128)(2,1)} fusion(bf16[4,8,128,128]{3,2,1,0:T(8,128)(2,1)S(1)} %convert_reduce_fusion, bf16[4,144,256]{2,1,0:T(8,128)(2,1)S(1)} %pad_maximum_fusion, f32[4,128]{1,0:T(4,128)S(1)} %bitcast.27), kind=kOutput, calls=%fused_computation.2 | convolution fusion | flops 268828672 | bytes 1837056 | tf_op jit(solution)/shard_map/hcsij,hif->cjf/dot_general | solution.py:46
  15.8 0.0 copy-start.1
  15.8 3.9 %all-to-all-start = ((bf16[8,128,256]{2,1,0:T(8,128)(2,1)}), bf16[8,128,256]{2,1,0:T(8,128)(2,1)S(1)}, u32[]{:S(2)}, u32[]{:S(2)}) async-start(bf16[8,128,256]{2,1,0:T(8,128)(2,1)} %fusion), calls=%async_computation | async-start | bytes 1048576 | tf_op jit(solution)/shard_map/all_to_all | solution.py:50
  19.6 0.0 copy-done.2
  19.7 9.7 %all-to-all-done = bf16[8,128,256]{2,1,0:T(8,128)(2,1)S(1)} async-done(((bf16[8,128,256]{2,1,0:T(8,128)(2,1)}), bf16[8,128,256]{2,1,0:T(8,128)(2,1)S(1)}, u32[]{:S(2)}, u32[]{:S(2)}) %all-to-all-start) | async-done | bytes 524320 | tf_op jit(solution)/shard_map/all_to_all | solution.py:50
  29.4 0.1 convert_reduce_fusion.1
  29.5 0.0 copy-done.1
  29.5 0.4 fusion.7
  29.8 0.3 all_to_all.17
  30.1 12.4 %all_to_all.21 = f32[32,1,2048]{2,1,0:T(1,128)S(1)} all-to-all(f32[32,1,2048]{2,1,0:T(1,128)S(1)} %all_to_all.17), channel_id=1, replica_groups=mesh['grp'=8,'rep'=4] {'grp','rep'}, dimensions={0} | all-to-all | bytes 524288 | tf_op jit(solution)/shard_map/all_to_all | solution.py:14
  42.5 0.2 reduce_sum.29
  42.6 0.8 %broadcast_in_dim.45 = f32[32,1,2048]{2,1,0:T(1,128)} broadcast(f32[2048]{0:T(1024)S(1)} %reduce_sum.29), dimensions={2} | broadcast | bytes 270336 | tf_op jit(solution)/shard_map/broadcast_in_dim | solution.py:15
  43.5 2.7 %all-to-all-start.2 = ((f32[32,1,2048]{2,1,0:T(1,128)}), f32[32,1,2048]{2,1,0:T(1,128)S(1)}, u32[]{:S(2)}, u32[]{:S(2)}) async-start(f32[32,1,2048]{2,1,0:T(1,128)} %broadcast_in_dim.45), calls=%async_computation.2 | async-start | bytes 524288 | tf_op jit(solution)/shard_map/all_to_all | solution.py:16
  46.2 0.0 copy-done
  46.2 1.0 %convolution_multiply_fusion = f32[128,256]{1,0:T(8,128)} fusion(f32[128,256]{1,0:T(8,128)S(1)} %convert_reduce_fusion.1, bf16[256,256]{1,0:T(8,128)(2,1)S(1)} %copy-done, f32[128]{0:T(128)S(1)} %convert_rsqrt_fusion), kind=kOutput, calls=%fused_computation.3 | convolution fusion | flops 100696064 | bytes 393728 | tf_op jit(solution)/shard_map/dot_general | solution.py:53
  47.2 9.2 %all-to-all-done.2 = f32[32,1,2048]{2,1,0:T(1,128)S(1)} async-done(((f32[32,1,2048]{2,1,0:T(1,128)}), f32[32,1,2048]{2,1,0:T(1,128)S(1)}, u32[]{:S(2)}, u32[]{:S(2)}) %all-to-all-start.2) | async-done | bytes 262176 | tf_op jit(solution)/shard_map/all_to_all | solution.py:16
  56.4 0.6 %reduce.3 = f32[32,2048]{1,0:T(8,128)S(1)} reduce(f32[32,1,2048]{2,1,0:T(1,128)S(1)} %all-to-all-done.2, f32[]{:T(128)} %constant.58), dimensions={1}, to_apply=%all_to_all.16.reduce_sub_computation | reduce | bytes 524292 | tf_op jit(solution)/shard_map/all_to_all | solution.py:16
  57.0 0.7 %reshape.73 = f32[256,256]{1,0:T(8,128)} reshape(f32[32,2048]{1,0:T(8,128)S(1)} %reduce.3) | data formatting | bytes 524288 | tf_op jit(solution)/shard_map/reshape | solution.py:16
  (5 shorter events, 0.1 us)
Async XLA Ops:
  0.6 45.6 %copy-start = (bf16[256,256]{1,0:T(8,128)(2,1)S(1)}, bf16[256,256]{1,0:T(8,128)(2,1)}, u32[]{:S(2)}) copy-start(bf16[256,256]{1,0:T(8,128)(2,1)} %param.10) | copy-start | bytes 393220
  2.2 9.4 %collective-permute-start = (bf16[144,256]{1,0:T(8,128)(2,1)S(1)}, bf16[144,256]{1,0:T(8,128)(2,1)S(1)}, u32[]{:S(2)}, u32[]{:S(2)}) collective-permute-start(bf16[144,256]{1,0:T(8,128)(2,1)S(1)} %get-tuple-element.15), channel_id=1, source_target_pairs={{1,0},{2,1},{3,2},{0,3},{5,4},{6,5},{7,6},{4,7},{9,8},{10,9},{11,1... | collective-permute-start | bytes 221192 | tf_op jit(solution)/shard_map/ppermute | solution.py:35
  7.3 7.0 %collective-permute-start.1 = (bf16[144,256]{1,0:T(8,128)(2,1)S(1)}, bf16[144,256]{1,0:T(8,128)(2,1)S(1)}, u32[]{:S(2)}, u32[]{:S(2)}) collective-permute-start(bf16[144,256]{1,0:T(8,128)(2,1)S(1)} %get-tuple-element.15), channel_id=1, source_target_pairs={{2,0},{3,1},{0,2},{1,3},{6,4},{7,5},{4,6},{5,7},{10,8},{11,9},{8,1... | collective-permute-start | bytes 221192 | tf_op jit(solution)/shard_map/ppermute | solution.py:35
  7.3 7.0 %collective-permute-start.2 = (bf16[144,256]{1,0:T(8,128)(2,1)S(1)}, bf16[144,256]{1,0:T(8,128)(2,1)S(1)}, u32[]{:S(2)}, u32[]{:S(2)}) collective-permute-start(bf16[144,256]{1,0:T(8,128)(2,1)S(1)} %get-tuple-element.15), channel_id=1, source_target_pairs={{3,0},{0,1},{1,2},{2,3},{7,4},{4,5},{5,6},{6,7},{11,8},{8,9},{9,10... | collective-permute-start | bytes 221192 | tf_op jit(solution)/shard_map/ppermute | solution.py:35
  14.4 5.2 %copy-start.2 = (s32[128]{0:T(128)S(1)}, s32[128]{0:T(128)}, u32[]{:S(2)}) copy-start(s32[128]{0:T(128)} %param.13) | copy-start | bytes 1540
  15.8 13.7 %copy-start.1 = (bf16[128,256]{1,0:T(8,128)(2,1)S(1)}, bf16[128,256]{1,0:T(8,128)(2,1)}, u32[]{:S(2)}) copy-start(bf16[128,256]{1,0:T(8,128)(2,1)} %param.9) | copy-start | bytes 196612
  15.8 13.6 %all-to-all-start = ((bf16[8,128,256]{2,1,0:T(8,128)(2,1)}), bf16[8,128,256]{2,1,0:T(8,128)(2,1)S(1)}, u32[]{:S(2)}, u32[]{:S(2)}) async-start(bf16[8,128,256]{2,1,0:T(8,128)(2,1)} %fusion), calls=%async_computation | async-start | bytes 1048576 | tf_op jit(solution)/shard_map/all_to_all | solution.py:50
  43.5 12.9 %all-to-all-start.2 = ((f32[32,1,2048]{2,1,0:T(1,128)}), f32[32,1,2048]{2,1,0:T(1,128)S(1)}, u32[]{:S(2)}, u32[]{:S(2)}) async-start(f32[32,1,2048]{2,1,0:T(1,128)} %broadcast_in_dim.45), calls=%async_computation.2 | async-start | bytes 524288 | tf_op jit(solution)/shard_map/all_to_all | solution.py:16

commit v5 on v4

--- a/solution.py
+++ b/solution.py
@@ -10,9 +10,9 @@
     count = 1
     for name in axes:
         count *= lax.axis_size(name)
-    chunks = w.reshape(count, -1)
-    owned = lax.all_to_all(chunks, axes, 0, 0, tiled=True).reshape(count, -1).sum(0)
-    spread = jnp.broadcast_to(owned[None], (count, owned.shape[0]))
+    chunks = w.reshape(count, w.shape[0] // count, w.shape[1])
+    owned = lax.all_to_all(chunks, axes, 0, 0, tiled=True).sum(0)
+    spread = jnp.broadcast_to(owned[None], chunks.shape)
     return lax.all_to_all(spread, axes, 0, 0, tiled=True).reshape(w.shape)
 
 

time: 58.2 us -> 56.8 us (0.976)
  other arithmetic: 5.7 us -> 5.05 us
    reshape x1 -> x0, local copies, waits for them, and re-layouts: 0.75 us -> none  [all_reduce_a2a(): return lax.all_to_all(spread, axes, 0, 0, tiled=True).reshape(w.shape)]
    unnamed x6 -> x7, local copies, waits for them, and re-layouts: 0.02 us -> 0.72 us
    all_to_all x1 -> x0, other arithmetic: 0.61 us -> none  [all_reduce_a2a(): return lax.all_to_all(spread, axes, 0, 0, tiled=True).reshape(w.shape)]
  transfers between devices with their start and end apart: 5 -> 5, of which waited for: 3 -> 3; matrix products, arithmetic and copies ran while one was open for 7% -> 8% of each run, Pallas kernels for 0% -> 0%
where the time goes in v5:
time: 56.8 us; the launch traced here: 56.4 us
  waiting for transfers between devices  21.4 us (38%)
  starting transfers between devices  12.6 us (22%)
  blocking collectives  12.4 us (22%)
  other arithmetic  5.05 us (9%)
  matrix products  2.59 us (5%)
  local copies, waits for them, and re-layouts  1.64 us (3%)
  between operations  0.76 us (1%)
    all_to_all x1, blocking collectives, all_reduce_a2a(): owned = lax.all_to_all(chunks, axes, 0, 0, tiled=True).sum(0)  12.4 us
    all_to_all x1, waiting for transfers between devices, per_device(): lax.all_to_all(terms.astype(jnp.bfloat16), 'grp', 0, 0, tiled=True)  9.51 us
    all_to_all x1, waiting for transfers between devices, all_reduce_a2a(): return lax.all_to_all(spread, axes, 0, 0, tiled=True).reshape(w.shape)  9.23 us
    ppermute x3, starting transfers between devices, per_device(): lax.ppermute(packed, 'rep', [((i + shift) % reps, i) for i in range(reps)])  6.11 us
    all_to_all x1, starting transfers between devices, per_device(): lax.all_to_all(terms.astype(jnp.bfloat16), 'grp', 0, 0, tiled=True)  3.72 us
    all_to_all x1, starting transfers between devices, all_reduce_a2a(): return lax.all_to_all(spread, axes, 0, 0, tiled=True).reshape(w.shape)  2.72 us
    ppermute x3, waiting for transfers between devices, per_device(): lax.ppermute(packed, 'rep', [((i + shift) % reps, i) for i in range(reps)])  2.66 us
    reduce_sum x1, other arithmetic, per_device(): jnp.einsum('hcsij,hif->cjf', masked, block_scaled_grad, preferred_element...  2.52 us
  transfers between devices with their start and end apart: 5, of which 3 were waited for; matrix products, arithmetic and copies ran while one was open for 8% of the time, Pallas kernels for 0%

profile of v5, /device:TPU:0, one launch (start us, length us, event | category | flops | bytes accessed | tf_op | source)
XLA Modules:
  0.0 56.4 jit_solution(7493381448680168804)
XLA Ops:
  0.6 0.0 copy-start
  0.6 0.7 %convert_bitcast_fusion = bf16[1,128]{1,0:T(2,128)(2,1)S(1)} fusion(s32[128]{0:T(128)} %param.13), kind=kLoop, calls=%fused_computation.27 | loop fusion | flops 128 | bytes 768 | tf_op jit(solution)/shard_map/reshape.33
  1.3 0.9 %compare_select_fusion = bf16[128,256]{1,0:T(8,128)(2,1)S(1)} fusion(bf16[128,256]{1,0:T(8,128)(2,1)} %param.12, bf16[128,256]{1,0:T(8,128)(2,1)} %param.11), kind=kLoop, calls=%fused_computation.15 | loop fusion | flops 65536 | bytes 196608 | tf_op jit(solution)/shard_map/jit(_where)/select_n | solution.py:25
  2.2 5.1 %collective-permute-start = (bf16[144,256]{1,0:T(8,128)(2,1)S(1)}, bf16[144,256]{1,0:T(8,128)(2,1)S(1)}, u32[]{:S(2)}, u32[]{:S(2)}) collective-permute-start(bf16[144,256]{1,0:T(8,128)(2,1)S(1)} %get-tuple-element.15), channel_id=1, source_target_pairs={{1,0},{2,1},{3,2},{0,3},{5,4},{6,5},{7,6},{4,7},{9,8},{10,9},{11,1... | collective-permute-start | bytes 221192 | tf_op jit(solution)/shard_map/ppermute | solution.py:35
  7.3 0.0 collective-permute-start.1
  7.3 1.0 %collective-permute-start.2 = (bf16[144,256]{1,0:T(8,128)(2,1)S(1)}, bf16[144,256]{1,0:T(8,128)(2,1)S(1)}, u32[]{:S(2)}, u32[]{:S(2)}) collective-permute-start(bf16[144,256]{1,0:T(8,128)(2,1)S(1)} %get-tuple-element.15), channel_id=1, source_target_pairs={{3,0},{0,1},{1,2},{2,3},{7,4},{4,5},{5,6},{6,7},{11,8},{8,9},{9,10... | collective-permute-start | bytes 221192 | tf_op jit(solution)/shard_map/ppermute | solution.py:35
  8.4 0.7 %fusion.12 = s32[8,4]{0,1:T(4,128)S(1)} fusion(s32[8,4]{0,1:T(4,128)} %param.15, s32[]{:T(128)S(6)} %axis_index.12), kind=kLoop, calls=%fused_computation.24 | loop fusion | flops 480 | bytes 260 | tf_op jit(solution)/shard_map/jit(_where)/select_n | solution.py:43
  9.1 0.1 copy.13
  9.1 2.5 %convert_reduce_fusion = bf16[4,8,128,128]{3,2,1,0:T(8,128)(2,1)S(1)} fusion(pred[4,8,4]{2,1,0:T(8,128)(4,1)S(1)} %iota_compare_fusion.1, bf16[8,4,128,128]{3,2,1,0:T(8,128)(2,1)} %param.14), kind=kLoop, calls=%fused_computation | loop fusion | flops 5767168 | bytes 2097280 | tf_op jit(solution)/shard_map/hcsij,hif->cjf/reduce_sum | solution.py:46
  11.7 0.0 collective-permute-done
  11.7 2.7 %collective-permute-done.1 = bf16[144,256]{1,0:T(8,128)(2,1)S(1)} collective-permute-done((bf16[144,256]{1,0:T(8,128)(2,1)S(1)}, bf16[144,256]{1,0:T(8,128)(2,1)S(1)}, u32[]{:S(2)}, u32[]{:S(2)}) %collective-permute-start.1) | collective-permute-done | bytes 73760 | tf_op jit(solution)/shard_map/ppermute | solution.py:35
  14.3 0.0 collective-permute-done.2
  14.4 0.0 copy-start.2
  14.4 0.0 copy-start.1
  14.4 1.4 %fusion = bf16[8,128,256]{2,1,0:T(8,128)(2,1)} fusion(bf16[4,8,128,128]{3,2,1,0:T(8,128)(2,1)S(1)} %convert_reduce_fusion, bf16[4,144,256]{2,1,0:T(8,128)(2,1)S(1)} %pad_maximum_fusion, f32[4,128]{1,0:T(4,128)S(1)} %bitcast.36), kind=kOutput, calls=%fused_computation.2 | convolution fusion | flops 268828672 | bytes 1837056 | tf_op jit(solution)/shard_map/hcsij,hif->cjf/dot_general | solution.py:46
  15.8 3.7 %all-to-all-start = ((bf16[8,128,256]{2,1,0:T(8,128)(2,1)}), bf16[8,128,256]{2,1,0:T(8,128)(2,1)S(1)}, u32[]{:S(2)}, u32[]{:S(2)}) async-start(bf16[8,128,256]{2,1,0:T(8,128)(2,1)} %fusion), calls=%async_computation | async-start | bytes 1048576 | tf_op jit(solution)/shard_map/all_to_all | solution.py:50
  19.5 0.0 copy-done.2
  19.5 0.0 copy-done.1
  19.5 0.1 fusion.9
  19.6 0.1 copy.15
  19.8 9.5 %all-to-all-done = bf16[8,128,256]{2,1,0:T(8,128)(2,1)S(1)} async-done(((bf16[8,128,256]{2,1,0:T(8,128)(2,1)}), bf16[8,128,256]{2,1,0:T(8,128)(2,1)S(1)}, u32[]{:S(2)}, u32[]{:S(2)}) %all-to-all-start) | async-done | bytes 524320 | tf_op jit(solution)/shard_map/all_to_all | solution.py:50
  29.3 0.1 convert_reduce_fusion.1
  29.3 0.3 fusion.6
  29.6 12.4 %all_to_all.15 = f32[32,8,256]{2,1,0:T(8,128)S(1)} all-to-all(f32[32,8,256]{2,1,0:T(8,128)S(1)} %fusion.6), channel_id=1, replica_groups=mesh['grp'=8,'rep'=4] {'grp','rep'}, dimensions={0} | all-to-all | bytes 524288 | tf_op jit(solution)/shard_map/all_to_all | solution.py:14
  42.0 0.7 %broadcast_in_dim.45 = f32[32,8,256]{2,1,0:T(8,128)} broadcast(f32[8,256]{1,0:T(8,128)S(1)} %reduce_sum.29), dimensions={1,2} | broadcast | bytes 270336 | tf_op jit(solution)/shard_map/broadcast_in_dim | solution.py:15
  42.7 2.7 %all-to-all-start.2 = ((f32[32,8,256]{2,1,0:T(8,128)}), f32[32,8,256]{2,1,0:T(8,128)S(1)}, u32[]{:S(2)}, u32[]{:S(2)}) async-start(f32[32,8,256]{2,1,0:T(8,128)} %broadcast_in_dim.45), calls=%async_computation.2 | async-start | bytes 524288 | tf_op jit(solution)/shard_map/all_to_all | solution.py:16
  45.5 0.0 copy-done
  45.5 1.0 %convolution_multiply_fusion = f32[128,256]{1,0:T(8,128)} fusion(f32[128,256]{1,0:T(8,128)S(1)} %convert_reduce_fusion.1, bf16[256,256]{1,0:T(8,128)(2,1)S(1)} %copy-done, f32[128]{0:T(128)S(1)} %convert_rsqrt_fusion), kind=kOutput, calls=%fused_computation.3 | convolution fusion | flops 100696064 | bytes 393728 | tf_op jit(solution)/shard_map/dot_general | solution.py:53
  46.4 9.2 %all-to-all-done.2 = f32[32,8,256]{2,1,0:T(8,128)S(1)} async-done(((f32[32,8,256]{2,1,0:T(8,128)}), f32[32,8,256]{2,1,0:T(8,128)S(1)}, u32[]{:S(2)}, u32[]{:S(2)}) %all-to-all-start.2) | async-done | bytes 262176 | tf_op jit(solution)/shard_map/all_to_all | solution.py:16
  55.7 0.7 %copy.19 = f32[256,256]{1,0:T(8,128)} copy(f32[256,256]{1,0:T(8,128)S(1)} %bitcast.29) | data formatting | bytes 524288
  (6 shorter events, 0.1 us)
Async XLA Ops:
  0.6 44.8 %copy-start = (bf16[256,256]{1,0:T(8,128)(2,1)S(1)}, bf16[256,256]{1,0:T(8,128)(2,1)}, u32[]{:S(2)}) copy-start(bf16[256,256]{1,0:T(8,128)(2,1)} %param.10) | copy-start | bytes 393220
  2.2 9.4 %collective-permute-start = (bf16[144,256]{1,0:T(8,128)(2,1)S(1)}, bf16[144,256]{1,0:T(8,128)(2,1)S(1)}, u32[]{:S(2)}, u32[]{:S(2)}) collective-permute-start(bf16[144,256]{1,0:T(8,128)(2,1)S(1)} %get-tuple-element.15), channel_id=1, source_target_pairs={{1,0},{2,1},{3,2},{0,3},{5,4},{6,5},{7,6},{4,7},{9,8},{10,9},{11,1... | collective-permute-start | bytes 221192 | tf_op jit(solution)/shard_map/ppermute | solution.py:35
  7.3 7.0 %collective-permute-start.1 = (bf16[144,256]{1,0:T(8,128)(2,1)S(1)}, bf16[144,256]{1,0:T(8,128)(2,1)S(1)}, u32[]{:S(2)}, u32[]{:S(2)}) collective-permute-start(bf16[144,256]{1,0:T(8,128)(2,1)S(1)} %get-tuple-element.15), channel_id=1, source_target_pairs={{2,0},{3,1},{0,2},{1,3},{6,4},{7,5},{4,6},{5,7},{10,8},{11,9},{8,1... | collective-permute-start | bytes 221192 | tf_op jit(solution)/shard_map/ppermute | solution.py:35
  7.3 7.0 %collective-permute-start.2 = (bf16[144,256]{1,0:T(8,128)(2,1)S(1)}, bf16[144,256]{1,0:T(8,128)(2,1)S(1)}, u32[]{:S(2)}, u32[]{:S(2)}) collective-permute-start(bf16[144,256]{1,0:T(8,128)(2,1)S(1)} %get-tuple-element.15), channel_id=1, source_target_pairs={{3,0},{0,1},{1,2},{2,3},{7,4},{4,5},{5,6},{6,7},{11,8},{8,9},{9,10... | collective-permute-start | bytes 221192 | tf_op jit(solution)/shard_map/ppermute | solution.py:35
  14.4 5.1 %copy-start.2 = (s32[128]{0:T(128)S(1)}, s32[128]{0:T(128)}, u32[]{:S(2)}) copy-start(s32[128]{0:T(128)} %param.13) | copy-start | bytes 1540
  14.4 5.1 %copy-start.1 = (bf16[128,256]{1,0:T(8,128)(2,1)S(1)}, bf16[128,256]{1,0:T(8,128)(2,1)}, u32[]{:S(2)}) copy-start(bf16[128,256]{1,0:T(8,128)(2,1)} %param.9) | copy-start | bytes 196612
  15.8 13.5 %all-to-all-start = ((bf16[8,128,256]{2,1,0:T(8,128)(2,1)}), bf16[8,128,256]{2,1,0:T(8,128)(2,1)S(1)}, u32[]{:S(2)}, u32[]{:S(2)}) async-start(bf16[8,128,256]{2,1,0:T(8,128)(2,1)} %fusion), calls=%async_computation | async-start | bytes 1048576 | tf_op jit(solution)/shard_map/all_to_all | solution.py:50
  42.7 12.9 %all-to-all-start.2 = ((f32[32,8,256]{2,1,0:T(8,128)}), f32[32,8,256]{2,1,0:T(8,128)S(1)}, u32[]{:S(2)}, u32[]{:S(2)}) async-start(f32[32,8,256]{2,1,0:T(8,128)} %broadcast_in_dim.45), calls=%async_computation.2 | async-start | bytes 524288 | tf_op jit(solution)/shard_map/all_to_all | solution.py:16

commit v6 on v5

--- a/solution.py
+++ b/solution.py
@@ -25,19 +25,12 @@
     grad_pre = jnp.where(preact > 0, grad_out, jnp.zeros_like(grad_out))
     scaled = (features.astype(jnp.float32) * inverse).astype(jnp.bfloat16)
 
-    degree_row = jnp.zeros((16, width), jnp.bfloat16).at[0, :rows_here].set(
-        degree.astype(jnp.bfloat16)
-    )
-    packed = jnp.concatenate([grad_pre, degree_row], axis=0)
+    scaled_grad = (grad_pre.astype(jnp.float32) * inverse).astype(jnp.bfloat16)
     me = lax.axis_index("rep")
-    parts = [packed]
+    parts = [scaled_grad]
     for shift in range(1, reps):
-        parts.append(lax.ppermute(packed, "rep", [((i + shift) % reps, i) for i in range(reps)]))
-    block = jnp.stack(parts)
-    block_grad = block[:, :rows_here].reshape(reps * rows_here, width)
-    block_degree = block[:, rows_here, :rows_here].reshape(reps * rows_here, 1)
-    block_inverse = lax.rsqrt(block_degree.astype(jnp.float32))
-    block_scaled_grad = (block_grad.astype(jnp.float32) * block_inverse).astype(jnp.bfloat16)
+        parts.append(lax.ppermute(scaled_grad, "rep", [((i + shift) % reps, i) for i in range(reps)]))
+    block_scaled_grad = jnp.stack(parts)
     block_scaled_grad = block_scaled_grad.reshape(row_tiles, edge, width)
 
     arrival = jnp.where(tile_rows >= 0, (tile_rows - me + reps) % reps, -1)

time: 56.8 us -> 56 us (0.986)
  waiting for transfers between devices: 21.4 us -> 18.9 us
  blocking collectives: 12.4 us -> 13.4 us
  starting transfers between devices: 12.6 us -> 13.5 us
    ppermute x3, waiting for transfers between devices: 2.66 us -> 0.04 us  [per_device(): lax.ppermute(scaled_grad, 'rep', [((i + shift) % reps, i) for i in range(...]
    all_to_all x1, blocking collectives: 12.4 us -> 13.4 us  [all_reduce_a2a(): owned = lax.all_to_all(chunks, axes, 0, 0, tiled=True).sum(0)]
    dot_general x1, other arithmetic: 0.08 us -> 0.99 us  [per_device(): lax.dot_general(scaled.astype(jnp.float32), pulled, (((0,), (0,)), ((), (...]
    ppermute x3, starting transfers between devices: 6.11 us -> 7.01 us  [per_device(): lax.ppermute(scaled_grad, 'rep', [((i + shift) % reps, i) for i in range(...]
    select_n x1 -> x0, other arithmetic: 0.88 us -> none  [per_device(): grad_pre = jnp.where(preact > 0, grad_out, jnp.zeros_like(grad_out))]
    another operation x3 -> x0, other arithmetic: 0.75 us -> none
    rsqrt x1, other arithmetic: 0.01 us -> 0.69 us  [per_device(): inverse = lax.rsqrt(degree.astype(jnp.float32))[:, None]]
  transfers between devices with their start and end apart: 5 -> 5, of which waited for: 3 -> 2; matrix products, arithmetic and copies ran while one was open for 8% -> 8% of each run, Pallas kernels for 0% -> 0%
where the time goes in v6:
time: 56 us; the launch traced here: 55.6 us
  waiting for transfers between devices  18.9 us (34%)
  starting transfers between devices  13.5 us (24%)
  blocking collectives  13.4 us (24%)
  other arithmetic  5.01 us (9%)
  matrix products  2.49 us (4%)
  local copies, waits for them, and re-layouts  1.63 us (3%)
  between operations  0.71 us (1%)
    all_to_all x1, blocking collectives, all_reduce_a2a(): owned = lax.all_to_all(chunks, axes, 0, 0, tiled=True).sum(0)  13.4 us
    all_to_all x1, waiting for transfers between devices, per_device(): lax.all_to_all(terms.astype(jnp.bfloat16), 'grp', 0, 0, tiled=True)  9.63 us
    all_to_all x1, waiting for transfers between devices, all_reduce_a2a(): return lax.all_to_all(spread, axes, 0, 0, tiled=True).reshape(w.shape)  9.23 us
    ppermute x3, starting transfers between devices, per_device(): lax.ppermute(scaled_grad, 'rep', [((i + shift) % reps, i) for i in range(...  7.01 us
    all_to_all x1, starting transfers between devices, per_device(): lax.all_to_all(terms.astype(jnp.bfloat16), 'grp', 0, 0, tiled=True)  3.77 us
    all_to_all x1, starting transfers between devices, all_reduce_a2a(): return lax.all_to_all(spread, axes, 0, 0, tiled=True).reshape(w.shape)  2.72 us
    reduce_sum x1, other arithmetic, per_device(): jnp.einsum('hcsij,hif->cjf', masked, block_scaled_grad, preferred_element...  2.52 us
    dot_general x1, matrix products, per_device(): jnp.einsum('hcsij,hif->cjf', masked, block_scaled_grad, preferred_element...  1.27 us
  transfers between devices with their start and end apart: 5, of which 2 were waited for; matrix products, arithmetic and copies ran while one was open for 8% of the time, Pallas kernels for 0%

profile of v6, /device:TPU:0, one launch (start us, length us, event | category | flops | bytes accessed | tf_op | source)
XLA Modules:
  0.0 55.6 jit_solution(2066305783501558194)
XLA Ops:
  0.6 0.0 copy-start
  0.6 0.7 %convert_rsqrt_fusion = f32[128]{0:T(128)S(1)} fusion(s32[128]{0:T(128)} %param.11), kind=kLoop, calls=%fused_computation.25 | loop fusion | flops 128 | bytes 1024 | tf_op jit(solution)/shard_map/rsqrt | solution.py:24
  1.3 1.0 %fusion.9 = (bf16[256,128]{0,1:T(8,128)(2,1)S(1)}, bf16[128,256]{1,0:T(8,128)(2,1)S(1)}) fusion(bf16[128,256]{1,0:T(8,128)(2,1)} %param.7, f32[128]{0:T(128)S(1)} %convert_rsqrt_fusion, bf16[128,256]{1,0:T(8,128)(2,1)} %param.10, bf16[128,256]{1,0:T(8,128)(2,1)} %param.9), kind=kLoop, calls=%fused_computation.17 | loop fusion | flops 262144 | bytes 328192 | tf_op jit(solution)/shard_map/dot_general | solution.py:50
  2.3 3.1 %collective-permute-start.2 = (bf16[128,256]{1,0:T(8,128)(2,1)S(1)}, bf16[128,256]{1,0:T(8,128)(2,1)S(1)}, u32[]{:S(2)}, u32[]{:S(2)}) collective-permute-start(bf16[128,256]{1,0:T(8,128)(2,1)S(1)} %get-tuple-element.3), channel_id=1, source_target_pairs={{3,0},{0,1},{1,2},{2,3},{7,4},{4,5},{5,6},{6,7},{11,8},{8,9},{9,10... | collective-permute-start | bytes 196616 | tf_op jit(solution)/shard_map/ppermute | solution.py:32
  5.4 2.6 %collective-permute-start.1 = (bf16[128,256]{1,0:T(8,128)(2,1)S(1)}, bf16[128,256]{1,0:T(8,128)(2,1)S(1)}, u32[]{:S(2)}, u32[]{:S(2)}) collective-permute-start(bf16[128,256]{1,0:T(8,128)(2,1)S(1)} %get-tuple-element.3), channel_id=1, source_target_pairs={{2,0},{3,1},{0,2},{1,3},{6,4},{7,5},{4,6},{5,7},{10,8},{11,9},{8,1... | collective-permute-start | bytes 196616 | tf_op jit(solution)/shard_map/ppermute | solution.py:32
  8.0 1.3 %collective-permute-start = (bf16[128,256]{1,0:T(8,128)(2,1)S(1)}, bf16[128,256]{1,0:T(8,128)(2,1)S(1)}, u32[]{:S(2)}, u32[]{:S(2)}) collective-permute-start(bf16[128,256]{1,0:T(8,128)(2,1)S(1)} %get-tuple-element.3), channel_id=1, source_target_pairs={{1,0},{2,1},{3,2},{0,3},{5,4},{6,5},{7,6},{4,7},{9,8},{10,9},{11,1... | collective-permute-start | bytes 196616 | tf_op jit(solution)/shard_map/ppermute | solution.py:32
  9.4 0.7 %fusion.12 = s32[8,4]{0,1:T(4,128)S(1)} fusion(s32[8,4]{0,1:T(4,128)} %param.13, s32[]{:T(128)S(6)} %axis_index.12), kind=kLoop, calls=%fused_computation.24 | loop fusion | flops 480 | bytes 260 | tf_op jit(solution)/shard_map/jit(_where)/select_n | solution.py:36
  10.0 0.1 copy.13
  10.1 2.5 %convert_reduce_fusion = bf16[4,8,128,128]{3,2,1,0:T(8,128)(2,1)S(1)} fusion(pred[4,8,4]{2,1,0:T(8,128)(4,1)S(1)} %iota_compare_fusion, bf16[8,4,128,128]{3,2,1,0:T(8,128)(2,1)} %param.12), kind=kLoop, calls=%fused_computation | loop fusion | flops 5767168 | bytes 2097280 | tf_op jit(solution)/shard_map/hcsij,hif->cjf/reduce_sum | solution.py:39
  12.7 0.0 collective-permute-done.2
  12.7 0.0 collective-permute-done.1
  12.7 0.0 collective-permute-done
  12.7 1.3 %fusion = bf16[8,128,256]{2,1,0:T(8,128)(2,1)} fusion(bf16[4,8,128,128]{3,2,1,0:T(8,128)(2,1)S(1)} %convert_reduce_fusion, bf16[1,128,256]{2,1,0:T(8,128)(2,1)S(1)} %bitcast.27, bf16[1,128,256]{2,1,0:T(8,128)(2,1)S(1)} %bitcast.28, bf16[1,128,256]{2,1,0:T(8,128)(2,1)S(1)} %bitcast.29, bf16[1,128,256]{2,1,0:T(8,128)(2,1)S(1)} %bitcast.26), kind=kOutput, calls=%fused_computation.2 | convolution fusion | flops 268828672 | bytes 1835008 | tf_op jit(solution)/shard_map/hcsij,hif->cjf/dot_general | solution.py:39
  14.0 3.8 %all-to-all-start = ((bf16[8,128,256]{2,1,0:T(8,128)(2,1)}), bf16[8,128,256]{2,1,0:T(8,128)(2,1)S(1)}, u32[]{:S(2)}, u32[]{:S(2)}) async-start(bf16[8,128,256]{2,1,0:T(8,128)(2,1)} %fusion), calls=%async_computation | async-start | bytes 1048576 | tf_op jit(solution)/shard_map/all_to_all | solution.py:43
  17.8 0.1 copy.15
  17.9 9.6 %all-to-all-done = bf16[8,128,256]{2,1,0:T(8,128)(2,1)S(1)} async-done(((bf16[8,128,256]{2,1,0:T(8,128)(2,1)}), bf16[8,128,256]{2,1,0:T(8,128)(2,1)S(1)}, u32[]{:S(2)}, u32[]{:S(2)}) %all-to-all-start) | async-done | bytes 524320 | tf_op jit(solution)/shard_map/all_to_all | solution.py:43
  27.5 0.1 convert_reduce_fusion.1
  27.6 0.3 fusion.7
  27.9 13.4 %all_to_all.15 = f32[32,8,256]{2,1,0:T(8,128)S(1)} all-to-all(f32[32,8,256]{2,1,0:T(8,128)S(1)} %fusion.7), channel_id=1, replica_groups=mesh['grp'=8,'rep'=4] {'grp','rep'}, dimensions={0} | all-to-all | bytes 524288 | tf_op jit(solution)/shard_map/all_to_all | solution.py:14
  41.3 0.7 %broadcast_in_dim.44 = f32[32,8,256]{2,1,0:T(8,128)} broadcast(f32[8,256]{1,0:T(8,128)S(1)} %reduce_sum.29), dimensions={1,2} | broadcast | bytes 270336 | tf_op jit(solution)/shard_map/broadcast_in_dim | solution.py:15
  42.0 2.7 %all-to-all-start.2 = ((f32[32,8,256]{2,1,0:T(8,128)}), f32[32,8,256]{2,1,0:T(8,128)S(1)}, u32[]{:S(2)}, u32[]{:S(2)}) async-start(f32[32,8,256]{2,1,0:T(8,128)} %broadcast_in_dim.44), calls=%async_computation.2 | async-start | bytes 524288 | tf_op jit(solution)/shard_map/all_to_all | solution.py:16
  44.7 0.0 copy-done
  44.7 1.0 %convolution_multiply_fusion = f32[128,256]{1,0:T(8,128)} fusion(f32[128,256]{1,0:T(8,128)S(1)} %convert_reduce_fusion.1, bf16[256,256]{1,0:T(8,128)(2,1)S(1)} %copy-done, f32[128]{0:T(128)S(1)} %convert_rsqrt_fusion), kind=kOutput, calls=%fused_computation.3 | convolution fusion | flops 100696064 | bytes 393728 | tf_op jit(solution)/shard_map/dot_general | solution.py:46
  45.7 9.2 %all-to-all-done.2 = f32[32,8,256]{2,1,0:T(8,128)S(1)} async-done(((f32[32,8,256]{2,1,0:T(8,128)}), f32[32,8,256]{2,1,0:T(8,128)S(1)}, u32[]{:S(2)}, u32[]{:S(2)}) %all-to-all-start.2) | async-done | bytes 262176 | tf_op jit(solution)/shard_map/all_to_all | solution.py:16
  54.9 0.7 %copy.19 = f32[256,256]{1,0:T(8,128)} copy(f32[256,256]{1,0:T(8,128)S(1)} %bitcast.25) | data formatting | bytes 524288
  (2 shorter events, 0.0 us)
Async XLA Ops:
  0.6 44.1 %copy-start = (bf16[256,256]{1,0:T(8,128)(2,1)S(1)}, bf16[256,256]{1,0:T(8,128)(2,1)}, u32[]{:S(2)}) copy-start(bf16[256,256]{1,0:T(8,128)(2,1)} %param.8) | copy-start | bytes 393220
  2.3 10.3 %collective-permute-start.2 = (bf16[128,256]{1,0:T(8,128)(2,1)S(1)}, bf16[128,256]{1,0:T(8,128)(2,1)S(1)}, u32[]{:S(2)}, u32[]{:S(2)}) collective-permute-start(bf16[128,256]{1,0:T(8,128)(2,1)S(1)} %get-tuple-element.3), channel_id=1, source_target_pairs={{3,0},{0,1},{1,2},{2,3},{7,4},{4,5},{5,6},{6,7},{11,8},{8,9},{9,10... | collective-permute-start | bytes 196616 | tf_op jit(solution)/shard_map/ppermute | solution.py:32
  5.4 7.3 %collective-permute-start.1 = (bf16[128,256]{1,0:T(8,128)(2,1)S(1)}, bf16[128,256]{1,0:T(8,128)(2,1)S(1)}, u32[]{:S(2)}, u32[]{:S(2)}) collective-permute-start(bf16[128,256]{1,0:T(8,128)(2,1)S(1)} %get-tuple-element.3), channel_id=1, source_target_pairs={{2,0},{3,1},{0,2},{1,3},{6,4},{7,5},{4,6},{5,7},{10,8},{11,9},{8,1... | collective-permute-start | bytes 196616 | tf_op jit(solution)/shard_map/ppermute | solution.py:32
  8.0 4.7 %collective-permute-start = (bf16[128,256]{1,0:T(8,128)(2,1)S(1)}, bf16[128,256]{1,0:T(8,128)(2,1)S(1)}, u32[]{:S(2)}, u32[]{:S(2)}) collective-permute-start(bf16[128,256]{1,0:T(8,128)(2,1)S(1)} %get-tuple-element.3), channel_id=1, source_target_pairs={{1,0},{2,1},{3,2},{0,3},{5,4},{6,5},{7,6},{4,7},{9,8},{10,9},{11,1... | collective-permute-start | bytes 196616 | tf_op jit(solution)/shard_map/ppermute | solution.py:32
  14.0 13.5 %all-to-all-start = ((bf16[8,128,256]{2,1,0:T(8,128)(2,1)}), bf16[8,128,256]{2,1,0:T(8,128)(2,1)S(1)}, u32[]{:S(2)}, u32[]{:S(2)}) async-start(bf16[8,128,256]{2,1,0:T(8,128)(2,1)} %fusion), calls=%async_computation | async-start | bytes 1048576 | tf_op jit(solution)/shard_map/all_to_all | solution.py:43
  42.0 12.9 %all-to-all-start.2 = ((f32[32,8,256]{2,1,0:T(8,128)}), f32[32,8,256]{2,1,0:T(8,128)S(1)}, u32[]{:S(2)}, u32[]{:S(2)}) async-start(f32[32,8,256]{2,1,0:T(8,128)} %broadcast_in_dim.44), calls=%async_computation.2 | async-start | bytes 524288 | tf_op jit(solution)/shard_map/all_to_all | solution.py:16

commit v7 on v6

--- a/solution.py
+++ b/solution.py
@@ -1,6 +1,8 @@
 import jax
 import jax.numpy as jnp
 from jax import lax
+from jax.experimental import pallas as pl
+from jax.experimental.pallas import tpu as pltpu
 from jax.sharding import PartitionSpec as P
 
 HIGHEST = lax.Precision.HIGHEST
@@ -14,6 +16,46 @@
     owned = lax.all_to_all(chunks, axes, 0, 0, tiled=True).sum(0)
     spread = jnp.broadcast_to(owned[None], chunks.shape)
     return lax.all_to_all(spread, axes, 0, 0, tiled=True).reshape(w.shape)
+
+
+def transposed_terms(arrival, tile_values, block):
+    col_tiles, slots, edge, _ = tile_values.shape
+    row_tiles, _, width = block.shape
+    per_step = min(col_tiles, 8)
+
+    def kernel(rows_ref, tiles_ref, block_ref, out_ref):
+        step = pl.program_id(0)
+        for c in range(per_step):
+            acc = jnp.zeros((edge, width), jnp.float32)
+            for s in range(slots):
+                row = rows_ref[(step * per_step + c) * slots + s]
+                picked = block_ref[jnp.clip(row, 0, row_tiles - 1)]
+                contrib = lax.dot_general(
+                    tiles_ref[c, s], picked, (((0,), (0,)), ((), ())),
+                    preferred_element_type=jnp.float32,
+                )
+                acc = acc + jnp.where(row >= 0, contrib, jnp.zeros_like(contrib))
+            out_ref[c] = acc.astype(out_ref.dtype)
+
+    grid_spec = pltpu.PrefetchScalarGridSpec(
+        num_scalar_prefetch=1,
+        grid=(col_tiles // per_step,),
+        in_specs=[
+            pl.BlockSpec((per_step, slots, edge, edge), lambda b, rows: (b, 0, 0, 0)),
+            pl.BlockSpec((row_tiles, edge, width), lambda b, rows: (0, 0, 0)),
+        ],
+        out_specs=pl.BlockSpec((per_step, edge, width), lambda b, rows: (b, 0, 0)),
+    )
+    return pl.pallas_call(
+        kernel,
+        out_shape=jax.ShapeDtypeStruct((col_tiles, edge, width), jnp.bfloat16),
+        grid_spec=grid_spec,
+        cost_estimate=pl.CostEstimate(
+            flops=2 * col_tiles * slots * edge * edge * width,
+            transcendentals=0,
+            bytes_accessed=2 * (tile_values.size + block.size + col_tiles * edge * width),
+        ),
+    )(arrival.reshape(-1), tile_values, block)
 
 
 def per_device(features, weight, preact, grad_out, degree, tile_values, tile_rows):
@@ -34,13 +76,9 @@
     block_scaled_grad = block_scaled_grad.reshape(row_tiles, edge, width)
 
     arrival = jnp.where(tile_rows >= 0, (tile_rows - me + reps) % reps, -1)
-    hit = arrival[None] == jnp.arange(row_tiles, dtype=jnp.int32)[:, None, None]
-    masked = jnp.where(hit[..., None, None], tile_values[None], jnp.zeros_like(tile_values[None]))
-    terms = jnp.einsum(
-        "hcsij,hif->cjf", masked, block_scaled_grad, preferred_element_type=jnp.float32
-    )
+    terms = transposed_terms(arrival, tile_values, block_scaled_grad)
 
-    arrived = lax.all_to_all(terms.astype(jnp.bfloat16), "grp", 0, 0, tiled=True)
+    arrived = lax.all_to_all(terms, "grp", 0, 0, tiled=True)
     pulled = arrived.astype(jnp.float32).sum(0)
 
     input_grad = inverse * lax.dot_general(

time: 56 us -> 58.9 us (1.052)
  Pallas kernels: 0 us -> 3.47 us
  other arithmetic: 5.01 us -> 2.54 us
  waiting for transfers between devices: 18.9 us -> 20.8 us
  matrix products: 2.49 us -> 1.22 us
  local copies, waits for them, and re-layouts: 1.63 us -> 2.9 us
    pallas_call x0 -> x1, Pallas kernels: none -> 3.47 us  [transposed_terms(): pl.pallas_call(kernel, out_shape=jax.ShapeDtypeStruct((col_tiles, edge, w...]
    reduce_sum x1 -> x0, other arithmetic: 2.52 us -> none  [per_device(): jnp.einsum('hcsij,hif->cjf', masked, block_scaled_grad, preferred_element...]
    ppermute x3, waiting for transfers between devices: 0.04 us -> 1.99 us  [per_device(): lax.ppermute(scaled_grad, 'rep', [((i + shift) % reps, i) for i in range(...]
    dot_general x1 -> x0, matrix products: 1.27 us -> none  [per_device(): jnp.einsum('hcsij,hif->cjf', masked, block_scaled_grad, preferred_element...]
    another operation x0 -> x1, other arithmetic: none -> 0.74 us  [per_device(): block_scaled_grad = jnp.stack(parts)]
    unnamed x3 -> x5, local copies, waits for them, and re-layouts: 0.71 us -> 1.39 us
    select_n x1, other arithmetic: 0.69 us -> 0.01 us  [per_device(): arrival = jnp.where(tile_rows >= 0, (tile_rows - me + reps) % reps, -1)]
    reshape x0 -> x1, local copies, waits for them, and re-layouts: none -> 0.59 us  [transposed_terms(): arrival.reshape(-1)]
  transfers between devices with their start and end apart: 5 -> 5, of which waited for: 2 -> 4; matrix products, arithmetic and copies ran while one was open for 8% -> 3% of each run, Pallas kernels for 0% -> 0%
where the time goes in v7:
time: 58.9 us; the launch traced here: 58.5 us
  waiting for transfers between devices  20.8 us (35%)
  starting transfers between devices  13.5 us (23%)
  blocking collectives  13.4 us (23%)
  Pallas kernels  3.47 us (6%)
  local copies, waits for them, and re-layouts  2.9 us (5%)
  other arithmetic  2.54 us (4%)
  matrix products  1.22 us (2%)
  between operations  0.69 us (1%)
    all_to_all x1, blocking collectives, all_reduce_a2a(): owned = lax.all_to_all(chunks, axes, 0, 0, tiled=True).sum(0)  13.4 us
    all_to_all x1, waiting for transfers between devices, per_device(): arrived = lax.all_to_all(terms, 'grp', 0, 0, tiled=True)  9.63 us
    all_to_all x1, waiting for transfers between devices, all_reduce_a2a(): return lax.all_to_all(spread, axes, 0, 0, tiled=True).reshape(w.shape)  9.23 us
    ppermute x3, starting transfers between devices, per_device(): lax.ppermute(scaled_grad, 'rep', [((i + shift) % reps, i) for i in range(...  7.01 us
    all_to_all x1, starting transfers between devices, per_device(): arrived = lax.all_to_all(terms, 'grp', 0, 0, tiled=True)  3.77 us
    pallas_call x1, Pallas kernels, transposed_terms(): pl.pallas_call(kernel, out_shape=jax.ShapeDtypeStruct((col_tiles, edge, w...  3.47 us
    all_to_all x1, starting transfers between devices, all_reduce_a2a(): return lax.all_to_all(spread, axes, 0, 0, tiled=True).reshape(w.shape)  2.72 us
    ppermute x3, waiting for transfers between devices, per_device(): lax.ppermute(scaled_grad, 'rep', [((i + shift) % reps, i) for i in range(...  1.99 us
  transfers between devices with their start and end apart: 5, of which 4 were waited for; matrix products, arithmetic and copies ran while one was open for 3% of the time, Pallas kernels for 0%

profile of v7, /device:TPU:0, one launch (start us, length us, event | category | flops | bytes accessed | tf_op | source)
XLA Modules:
  0.0 58.5 jit_solution(5544265057434875768)
XLA Ops:
  0.6 0.0 copy-start
  0.6 0.7 %convert_rsqrt_fusion = f32[128]{0:T(128)S(1)} fusion(s32[128]{0:T(128)} %param.11), kind=kLoop, calls=%fused_computation.15 | loop fusion | flops 128 | bytes 1024 | tf_op jit(solution)/shard_map/rsqrt | solution.py:66
  1.3 1.0 %fusion.2 = (bf16[256,128]{0,1:T(8,128)(2,1)S(1)}, bf16[128,256]{1,0:T(8,128)(2,1)S(1)}) fusion(bf16[128,256]{1,0:T(8,128)(2,1)} %param.7, f32[128]{0:T(128)S(1)} %convert_rsqrt_fusion, bf16[128,256]{1,0:T(8,128)(2,1)} %param.10, bf16[128,256]{1,0:T(8,128)(2,1)} %param.9), kind=kLoop, calls=%fused_computation.8 | loop fusion | flops 262144 | bytes 328192 | tf_op jit(solution)/shard_map/dot_general | solution.py:88
  2.3 3.1 %collective-permute-start.2 = (bf16[128,256]{1,0:T(8,128)(2,1)S(1)}, bf16[128,256]{1,0:T(8,128)(2,1)S(1)}, u32[]{:S(2)}, u32[]{:S(2)}) collective-permute-start(bf16[128,256]{1,0:T(8,128)(2,1)S(1)} %get-tuple-element.3), channel_id=1, source_target_pairs={{3,0},{0,1},{1,2},{2,3},{7,4},{4,5},{5,6},{6,7},{11,8},{8,9},{9,10... | collective-permute-start | bytes 196616 | tf_op jit(solution)/shard_map/ppermute | solution.py:74
  5.4 2.6 %collective-permute-start.1 = (bf16[128,256]{1,0:T(8,128)(2,1)S(1)}, bf16[128,256]{1,0:T(8,128)(2,1)S(1)}, u32[]{:S(2)}, u32[]{:S(2)}) collective-permute-start(bf16[128,256]{1,0:T(8,128)(2,1)S(1)} %get-tuple-element.3), channel_id=1, source_target_pairs={{2,0},{3,1},{0,2},{1,3},{6,4},{7,5},{4,6},{5,7},{10,8},{11,9},{8,1... | collective-permute-start | bytes 196616 | tf_op jit(solution)/shard_map/ppermute | solution.py:74
  8.0 1.3 %collective-permute-start = (bf16[128,256]{1,0:T(8,128)(2,1)S(1)}, bf16[128,256]{1,0:T(8,128)(2,1)S(1)}, u32[]{:S(2)}, u32[]{:S(2)}) collective-permute-start(bf16[128,256]{1,0:T(8,128)(2,1)S(1)} %get-tuple-element.3), channel_id=1, source_target_pairs={{1,0},{2,1},{3,2},{0,3},{5,4},{6,5},{7,6},{4,7},{9,8},{10,9},{11,1... | collective-permute-start | bytes 196616 | tf_op jit(solution)/shard_map/ppermute | solution.py:74
  9.4 0.0 copy-start.1
  9.4 0.7 %copy-done.1 = s32[8,4]{0,1:T(4,128)S(1)} copy-done((s32[8,4]{0,1:T(4,128)S(1)}, s32[8,4]{0,1:T(4,128)}, u32[]{:S(2)}) %copy-start.1) | copy-done | bytes 152
  10.0 0.1 copy.11
  10.1 0.6 %reshape.14.rows_ref = s32[32]{0:T(128)} reshape(s32[8,4]{1,0:T(8,128)S(1)} %copy.11) | data formatting | bytes 256 | tf_op jit(solution)/shard_map/reshape | solution.py:58
  10.7 0.0 collective-permute-done.2
  10.7 1.8 %collective-permute-done.1 = bf16[128,256]{1,0:T(8,128)(2,1)S(1)} collective-permute-done((bf16[128,256]{1,0:T(8,128)(2,1)S(1)}, bf16[128,256]{1,0:T(8,128)(2,1)S(1)}, u32[]{:S(2)}, u32[]{:S(2)}) %collective-permute-start.1) | collective-permute-done | bytes 65568 | tf_op jit(solution)/shard_map/ppermute | solution.py:74
  12.5 0.2 collective-permute-done
  12.7 0.7 %pad_maximum_fusion.block_ref = bf16[4,128,256]{2,1,0:T(8,128)(2,1)} fusion(bf16[1,128,256]{2,1,0:T(8,128)(2,1)S(1)} %bitcast.17, bf16[1,128,256]{2,1,0:T(8,128)(2,1)S(1)} %bitcast.18, bf16[1,128,256]{2,1,0:T(8,128)(2,1)S(1)} %bitcast.19, bf16[1,128,256]{2,1,0:T(8,128)(2,1)S(1)} %bitcast.16), kind=kLoop, calls=%fused_computation.2 | loop fusion | flops 393216 | bytes 524288 | tf_op jit(solution)/shard_map/stack | solution.py:75
  13.5 3.5 %shard_map.86 = bf16[8,128,256]{2,1,0:T(8,128)(2,1)} custom-call(s32[32]{0:T(128)} %reshape.14.rows_ref, bf16[8,4,128,128]{3,2,1,0:T(8,128)(2,1)} %tiles_ref.1, bf16[4,128,256]{2,1,0:T(8,128)(2,1)} %pad_maximum_fusion.block_ref), custom_call_target="tpu_custom_call" | custom-call | flops 268435456 | bytes 1835008 | tf_op jit(solution)/shard_map/pallas_call | solution.py:49
  16.9 3.8 %all-to-all-start = ((bf16[8,128,256]{2,1,0:T(8,128)(2,1)}), bf16[8,128,256]{2,1,0:T(8,128)(2,1)S(1)}, u32[]{:S(2)}, u32[]{:S(2)}) async-start(bf16[8,128,256]{2,1,0:T(8,128)(2,1)} %shard_map.86), calls=%async_computation | async-start | bytes 1048576 | tf_op jit(solution)/shard_map/all_to_all | solution.py:81
  20.7 0.1 copy.12
  20.8 9.6 %all-to-all-done = bf16[8,128,256]{2,1,0:T(8,128)(2,1)S(1)} async-done(((bf16[8,128,256]{2,1,0:T(8,128)(2,1)}), bf16[8,128,256]{2,1,0:T(8,128)(2,1)S(1)}, u32[]{:S(2)}, u32[]{:S(2)}) %all-to-all-start) | async-done | bytes 524320 | tf_op jit(solution)/shard_map/all_to_all | solution.py:81
  30.4 0.1 convert_reduce_fusion
  30.5 0.3 fusion
  30.8 13.4 %all_to_all.15 = f32[32,8,256]{2,1,0:T(8,128)S(1)} all-to-all(f32[32,8,256]{2,1,0:T(8,128)S(1)} %fusion), channel_id=1, replica_groups=mesh['grp'=8,'rep'=4] {'grp','rep'}, dimensions={0} | all-to-all | bytes 524288 | tf_op jit(solution)/shard_map/all_to_all | solution.py:16
  44.2 0.7 %broadcast_in_dim.12 = f32[32,8,256]{2,1,0:T(8,128)} broadcast(f32[8,256]{1,0:T(8,128)S(1)} %reduce_sum.19), dimensions={1,2} | broadcast | bytes 270336 | tf_op jit(solution)/shard_map/broadcast_in_dim | solution.py:17
  44.9 2.7 %all-to-all-start.2 = ((f32[32,8,256]{2,1,0:T(8,128)}), f32[32,8,256]{2,1,0:T(8,128)S(1)}, u32[]{:S(2)}, u32[]{:S(2)}) async-start(f32[32,8,256]{2,1,0:T(8,128)} %broadcast_in_dim.12), calls=%async_computation.2 | async-start | bytes 524288 | tf_op jit(solution)/shard_map/all_to_all | solution.py:18
  47.6 0.0 copy-done
  47.7 1.0 %convolution_multiply_fusion = f32[128,256]{1,0:T(8,128)} fusion(f32[128,256]{1,0:T(8,128)S(1)} %convert_reduce_fusion, bf16[256,256]{1,0:T(8,128)(2,1)S(1)} %copy-done, f32[128]{0:T(128)S(1)} %convert_rsqrt_fusion), kind=kOutput, calls=%fused_computation | convolution fusion | flops 100696064 | bytes 393728 | tf_op jit(solution)/shard_map/dot_general | solution.py:84
  48.6 9.2 %all-to-all-done.2 = f32[32,8,256]{2,1,0:T(8,128)S(1)} async-done(((f32[32,8,256]{2,1,0:T(8,128)}), f32[32,8,256]{2,1,0:T(8,128)S(1)}, u32[]{:S(2)}, u32[]{:S(2)}) %all-to-all-start.2) | async-done | bytes 262176 | tf_op jit(solution)/shard_map/all_to_all | solution.py:18
  57.8 0.7 %copy.14 = f32[256,256]{1,0:T(8,128)} copy(f32[256,256]{1,0:T(8,128)S(1)} %bitcast.15) | data formatting | bytes 524288
  (2 shorter events, 0.0 us)
Async XLA Ops:
  0.6 47.0 %copy-start = (bf16[256,256]{1,0:T(8,128)(2,1)S(1)}, bf16[256,256]{1,0:T(8,128)(2,1)}, u32[]{:S(2)}) copy-start(bf16[256,256]{1,0:T(8,128)(2,1)} %param.8) | copy-start | bytes 393220
  2.3 8.4 %collective-permute-start.2 = (bf16[128,256]{1,0:T(8,128)(2,1)S(1)}, bf16[128,256]{1,0:T(8,128)(2,1)S(1)}, u32[]{:S(2)}, u32[]{:S(2)}) collective-permute-start(bf16[128,256]{1,0:T(8,128)(2,1)S(1)} %get-tuple-element.3), channel_id=1, source_target_pairs={{3,0},{0,1},{1,2},{2,3},{7,4},{4,5},{5,6},{6,7},{11,8},{8,9},{9,10... | collective-permute-start | bytes 196616 | tf_op jit(solution)/shard_map/ppermute | solution.py:74
  5.4 7.1 %collective-permute-start.1 = (bf16[128,256]{1,0:T(8,128)(2,1)S(1)}, bf16[128,256]{1,0:T(8,128)(2,1)S(1)}, u32[]{:S(2)}, u32[]{:S(2)}) collective-permute-start(bf16[128,256]{1,0:T(8,128)(2,1)S(1)} %get-tuple-element.3), channel_id=1, source_target_pairs={{2,0},{3,1},{0,2},{1,3},{6,4},{7,5},{4,6},{5,7},{10,8},{11,9},{8,1... | collective-permute-start | bytes 196616 | tf_op jit(solution)/shard_map/ppermute | solution.py:74
  8.0 4.7 %collective-permute-start = (bf16[128,256]{1,0:T(8,128)(2,1)S(1)}, bf16[128,256]{1,0:T(8,128)(2,1)S(1)}, u32[]{:S(2)}, u32[]{:S(2)}) collective-permute-start(bf16[128,256]{1,0:T(8,128)(2,1)S(1)} %get-tuple-element.3), channel_id=1, source_target_pairs={{1,0},{2,1},{3,2},{0,3},{5,4},{6,5},{7,6},{4,7},{9,8},{10,9},{11,1... | collective-permute-start | bytes 196616 | tf_op jit(solution)/shard_map/ppermute | solution.py:74
  9.4 0.7 %copy-start.1 = (s32[8,4]{0,1:T(4,128)S(1)}, s32[8,4]{0,1:T(4,128)}, u32[]{:S(2)}) copy-start(s32[8,4]{0,1:T(4,128)} %param.13) | copy-start | bytes 388
  16.9 13.5 %all-to-all-start = ((bf16[8,128,256]{2,1,0:T(8,128)(2,1)}), bf16[8,128,256]{2,1,0:T(8,128)(2,1)S(1)}, u32[]{:S(2)}, u32[]{:S(2)}) async-start(bf16[8,128,256]{2,1,0:T(8,128)(2,1)} %shard_map.86), calls=%async_computation | async-start | bytes 1048576 | tf_op jit(solution)/shard_map/all_to_all | solution.py:81
  44.9 12.9 %all-to-all-start.2 = ((f32[32,8,256]{2,1,0:T(8,128)}), f32[32,8,256]{2,1,0:T(8,128)S(1)}, u32[]{:S(2)}, u32[]{:S(2)}) async-start(f32[32,8,256]{2,1,0:T(8,128)} %broadcast_in_dim.12), calls=%async_computation.2 | async-start | bytes 524288 | tf_op jit(solution)/shard_map/all_to_all | solution.py:18

commit v8 on v7

v8 whole, which is shorter than its diff:
```python
import jax
import jax.numpy as jnp
from jax import lax
from jax.experimental import pallas as pl
from jax.experimental.pallas import tpu as pltpu
from jax.sharding import PartitionSpec as P

HIGHEST = lax.Precision.HIGHEST


def all_reduce_a2a(w, axes):
    count = 1
    for name in axes:
        count *= lax.axis_size(name)
    chunks = w.reshape(count, w.shape[0] // count, w.shape[1])
    owned = lax.all_to_all(chunks, axes, 0, 0, tiled=True).sum(0)
    spread = jnp.broadcast_to(owned[None], chunks.shape)
    return lax.all_to_all(spread, axes, 0, 0, tiled=True).reshape(w.shape)


def transposed_terms(tile_rows, tile_values, block_t):
    col_tiles, slots, edge, _ = tile_values.shape
    kinds, width, _ = block_t.shape
    reps = kinds - 1
    per_step = min(col_tiles, 4)

    def kernel(rows_ref, tiles_ref, block_ref, out_ref):
        step = pl.program_id(0)
        me = lax.axis_index("rep")
        for c in range(per_step):
            acc = jnp.zeros((width, edge), jnp.float32)
            for s in range(slots):
                row = rows_ref[step * per_step + c, s]
                k = jnp.where(row >= 0, (row - me + reps) % reps, reps)
                acc = acc + jnp.dot(
                    block_ref[k], tiles_ref[c, s], preferred_element_type=jnp.float32
                )
            out_ref[c] = acc.astype(out_ref.dtype)

    grid_spec = pltpu.PrefetchScalarGridSpec(
        num_scalar_prefetch=1,
        grid=(col_tiles // per_step,),
        in_specs=[
            pl.BlockSpec((per_step, slots, edge, edge), lambda b, rows: (b, 0, 0, 0)),
            pl.BlockSpec((kinds, width, edge), lambda b, rows: (0, 0, 0)),
        ],
        out_specs=pl.BlockSpec((per_step, width, edge), lambda b, rows: (b, 0, 0)),
    )
    return pl.pallas_call(
        kernel,
        out_shape=jax.ShapeDtypeStruct((col_tiles, width, edge), jnp.bfloat16),
        grid_spec=grid_spec,
        cost_estimate=pl.CostEstimate(
            flops=2 * col_tiles * slots * edge * edge * width,
            transcendentals=0,
            bytes_accessed=2 * (tile_values.size + block_t.size + col_tiles * edge * width),
        ),
    )(tile_rows, tile_values, block_t)


def per_device(features, weight, preact, grad_out, degree, tile_values, tile_rows):
    rows_here, width = features.shape
    col_tiles, slots, edge, _ = tile_values.shape
    reps = lax.axis_size("rep")
    row_tiles = reps * rows_here // edge
    inverse = lax.rsqrt(degree.astype(jnp.float32))[:, None]
    grad_pre = jnp.where(preact > 0, grad_out, jnp.zeros_like(grad_out))
    scaled = (features.astype(jnp.float32) * inverse).astype(jnp.bfloat16)

    scaled_grad_t = (grad_pre.astype(jnp.float32) * inverse).astype(jnp.bfloat16).T
    parts = [scaled_grad_t]
    for shift in range(1, reps):
        parts.append(lax.ppermute(scaled_grad_t, "rep", [((i + shift) % reps, i) for i in range(reps)]))
    parts.append(jnp.zeros_like(scaled_grad_t))
    block_t = jnp.stack(parts)
    terms_t = transposed_terms(tile_rows, tile_values, block_t)

    arrived = lax.all_to_all(terms_t, "grp", 0, 0, tiled=True)
    pulled_t = arrived.astype(jnp.float32).sum(0)

    input_grad = inverse * lax.dot_general(
        pulled_t, weight.astype(jnp.float32), (((0,), (1,)), ((), ())), precision=HIGHEST,
        preferred_element_type=jnp.float32,
    )
    weight_local = lax.dot_general(
        scaled.astype(jnp.float32), pulled_t, (((0,), (1,)), ((), ())), precision=HIGHEST,
        preferred_element_type=jnp.float32,
    )
    weight_grad = all_reduce_a2a(weight_local, ("grp", "rep"))
    return (input_grad, weight_grad)


def solution(mesh):
    return jax.shard_map(
        per_device,
        mesh=mesh,
        in_specs=(
            P(("grp", "rep"), None),
            P(),
            P(("grp", "rep"), None),
            P(("grp", "rep"), None),
            P(("grp", "rep")),
            P(("grp", "rep"), None, None, None),
            P(("grp", "rep"), None),
        ),
        out_specs=(P(("grp", "rep"), None), P()),
        check_vma=False,
    )
```

time: 58.9 us -> 59.3 us (level)
  waiting for transfers between devices: 20.8 us -> 23.5 us
  local copies, waits for them, and re-layouts: 2.9 us -> 4.85 us
  other arithmetic: 2.54 us -> 0.86 us
  blocking collectives: 13.4 us -> 12.3 us
  starting transfers between devices: 13.5 us -> 12.7 us
  matrix products: 1.22 us -> 0.57 us
    ppermute x3, waiting for transfers between devices: 1.99 us -> 4.73 us  [per_device(): lax.ppermute(scaled_grad_t, 'rep', [((i + shift) % reps, i) for i in rang...]
    unnamed x5 -> x19, local copies, waits for them, and re-layouts: 1.39 us -> 4.11 us
    all_to_all x1, blocking collectives: 13.4 us -> 12.3 us  [all_reduce_a2a(): owned = lax.all_to_all(chunks, axes, 0, 0, tiled=True).sum(0)]
    dot_general x1 -> x0, other arithmetic: 0.99 us -> none  [per_device(): lax.dot_general(scaled.astype(jnp.float32), pulled, (((0,), (0,)), ((), (...]
    ppermute x3, starting transfers between devices: 7.01 us -> 6.11 us  [per_device(): lax.ppermute(scaled_grad_t, 'rep', [((i + shift) % reps, i) for i in rang...]
    another operation x1 -> x0, other arithmetic: 0.74 us -> none  [per_device(): block_scaled_grad = jnp.stack(parts)]
    dot_general x2, matrix products: 1.22 us -> 0.57 us  [the longest x1 0.28 us: per_device(): lax.dot_general(scaled.astype(jnp.float32), pulled_t, (((0,), (1,)), ((),...]
    reshape x1 -> x0, local copies, waits for them, and re-layouts: 0.59 us -> none  [transposed_terms(): arrival.reshape(-1)]
where the time goes in v8:
time: 59.3 us; the launch traced here: 58.9 us
  waiting for transfers between devices  23.5 us (40%)
  starting transfers between devices  12.7 us (21%)
  blocking collectives  12.3 us (21%)
  local copies, waits for them, and re-layouts  4.85 us (8%)
  Pallas kernels  3.43 us (6%)
  other arithmetic  0.86 us (1%)
  between operations  0.77 us (1%)
    all_to_all x1, blocking collectives, all_reduce_a2a(): owned = lax.all_to_all(chunks, axes, 0, 0, tiled=True).sum(0)  12.3 us
    all_to_all x1, waiting for transfers between devices, per_device(): arrived = lax.all_to_all(terms_t, 'grp', 0, 0, tiled=True)  9.62 us
    all_to_all x1, waiting for transfers between devices, all_reduce_a2a(): return lax.all_to_all(spread, axes, 0, 0, tiled=True).reshape(w.shape)  9.14 us
    ppermute x3, starting transfers between devices, per_device(): lax.ppermute(scaled_grad_t, 'rep', [((i + shift) % reps, i) for i in rang...  6.11 us
    ppermute x3, waiting for transfers between devices, per_device(): lax.ppermute(scaled_grad_t, 'rep', [((i + shift) % reps, i) for i in rang...  4.73 us
    unnamed x19, local copies, waits for them, and re-layouts  4.11 us
    all_to_all x1, starting transfers between devices, per_device(): arrived = lax.all_to_all(terms_t, 'grp', 0, 0, tiled=True)  3.86 us
    pallas_call x1, Pallas kernels, transposed_terms(): pl.pallas_call(kernel, out_shape=jax.ShapeDtypeStruct((col_tiles, width,...  3.43 us
  transfers between devices with their start and end apart: 5, of which 4 were waited for; matrix products, arithmetic and copies ran while one was open for 3% of the time, Pallas kernels for 0%

profile of v8, /device:TPU:0, one launch (start us, length us, event | category | flops | bytes accessed | tf_op | source)
XLA Modules:
  0.0 58.9 jit_solution(6596190783299586484)
XLA Ops:
  0.6 0.0 copy-start
  0.6 0.7 %convert_rsqrt_fusion = f32[128]{0:T(128)S(1)} fusion(s32[128]{0:T(128)} %param.11), kind=kLoop, calls=%fused_computation.15 | loop fusion | flops 128 | bytes 1024 | tf_op jit(solution)/shard_map/rsqrt | solution.py:66
  1.3 0.0 copy-start.2
  1.3 1.0 %copy.10 = bf16[128,256]{0,1:T(8,128)(2,1)S(1)} copy(bf16[128,256]{1,0:T(8,128)(2,1)} %param.10) | data formatting | bytes 131072 | tf_op args[3]
  2.3 0.0 copy-done.2
  2.3 0.1 copy.9
  2.5 0.0 copy-start.4
  2.5 5.1 %collective-permute-start = (bf16[256,128]{1,0:T(8,128)(2,1)S(1)}, bf16[256,128]{1,0:T(8,128)(2,1)S(1)}, u32[]{:S(2)}, u32[]{:S(2)}) collective-permute-start(bf16[256,128]{1,0:T(8,128)(2,1)S(1)} %fusion.5), channel_id=1, source_target_pairs={{1,0},{2,1},{3,2},{0,3},{5,4},{6,5},{7,6},{4,7},{9,8},{10,9},{11,1... | collective-permute-start | bytes 196616 | tf_op jit(solution)/shard_map/ppermute | solution.py:73
  7.6 0.0 collective-permute-start.1
  7.6 1.0 %collective-permute-start.2 = (bf16[256,128]{1,0:T(8,128)(2,1)S(1)}, bf16[256,128]{1,0:T(8,128)(2,1)S(1)}, u32[]{:S(2)}, u32[]{:S(2)}) collective-permute-start(bf16[256,128]{1,0:T(8,128)(2,1)S(1)} %fusion.5), channel_id=1, source_target_pairs={{3,0},{0,1},{1,2},{2,3},{7,4},{4,5},{5,6},{6,7},{11,8},{8,9},{9,10... | collective-permute-start | bytes 196616 | tf_op jit(solution)/shard_map/ppermute | solution.py:73
  8.7 0.0 copy-done.4
  8.7 0.7 %copy.11.rows_ref = s32[8,4]{1,0:T(8,128)} copy(s32[8,4]{0,1:T(4,128)S(1)} %copy-done.4) | data formatting | bytes 256 | tf_op args[6]
  9.3 0.8 %collective-permute-done = bf16[256,128]{1,0:T(8,128)(2,1)S(1)} collective-permute-done((bf16[256,128]{1,0:T(8,128)(2,1)S(1)}, bf16[256,128]{1,0:T(8,128)(2,1)S(1)}, u32[]{:S(2)}, u32[]{:S(2)}) %collective-permute-start) | collective-permute-done | bytes 65568 | tf_op jit(solution)/shard_map/ppermute | solution.py:73
  10.1 4.0 %collective-permute-done.1 = bf16[256,128]{1,0:T(8,128)(2,1)S(1)} collective-permute-done((bf16[256,128]{1,0:T(8,128)(2,1)S(1)}, bf16[256,128]{1,0:T(8,128)(2,1)S(1)}, u32[]{:S(2)}, u32[]{:S(2)}) %collective-permute-start.1) | collective-permute-done | bytes 65568 | tf_op jit(solution)/shard_map/ppermute | solution.py:73
  14.1 0.0 collective-permute-done.2
  14.1 0.0 copy-start.1
  14.2 0.7 %copy-done.1 = bf16[5,256,128]{2,1,0:T(8,128)(2,1)} copy-done((bf16[5,256,128]{2,1,0:T(8,128)(2,1)}, bf16[5,256,128]{2,1,0:T(8,128)(2,1)S(1)}, u32[]{:S(2)}) %copy-start.1) | copy-done | bytes 327704
  14.9 3.4 %shard_map.86 = bf16[8,256,128]{2,1,0:T(8,128)(2,1)} custom-call(s32[8,4]{1,0:T(8,128)} %copy.11.rows_ref, bf16[8,4,128,128]{3,2,1,0:T(8,128)(2,1)} %tiles_ref.1, bf16[5,256,128]{2,1,0:T(8,128)(2,1)} %copy-done.1), custom_call_target="tpu_custom_call" | custom-call | flops 268435456 | bytes 1900544 | tf_op jit(solution)/shard_map/pallas_call | solution.py:49
  18.3 0.0 copy-start.3
  18.3 3.9 %all-to-all-start = ((bf16[8,256,128]{2,1,0:T(8,128)(2,1)}), bf16[8,256,128]{2,1,0:T(8,128)(2,1)S(1)}, u32[]{:S(2)}, u32[]{:S(2)}) async-start(bf16[8,256,128]{2,1,0:T(8,128)(2,1)} %shard_map.86), calls=%async_computation | async-start | bytes 1048576 | tf_op jit(solution)/shard_map/all_to_all | solution.py:78
  22.2 0.0 copy-done.3
  22.2 0.1 copy.13
  22.3 9.6 %all-to-all-done = bf16[8,256,128]{2,1,0:T(8,128)(2,1)S(1)} async-done(((bf16[8,256,128]{2,1,0:T(8,128)(2,1)}), bf16[8,256,128]{2,1,0:T(8,128)(2,1)S(1)}, u32[]{:S(2)}, u32[]{:S(2)}) %all-to-all-start) | async-done | bytes 524320 | tf_op jit(solution)/shard_map/all_to_all | solution.py:78
  31.9 0.1 convert_reduce_fusion
  32.0 0.3 fusion
  32.3 12.3 %all_to_all.15 = f32[32,8,256]{2,1,0:T(8,128)S(1)} all-to-all(f32[32,8,256]{2,1,0:T(8,128)S(1)} %fusion), channel_id=1, replica_groups=mesh['grp'=8,'rep'=4] {'grp','rep'}, dimensions={0} | all-to-all | bytes 524288 | tf_op jit(solution)/shard_map/all_to_all | solution.py:16
  44.6 0.7 %broadcast_in_dim.2 = f32[32,8,256]{2,1,0:T(8,128)} broadcast(f32[8,256]{1,0:T(8,128)S(1)} %reduce_sum.19), dimensions={1,2} | broadcast | bytes 270336 | tf_op jit(solution)/shard_map/broadcast_in_dim | solution.py:17
  45.3 2.7 %all-to-all-start.2 = ((f32[32,8,256]{2,1,0:T(8,128)}), f32[32,8,256]{2,1,0:T(8,128)S(1)}, u32[]{:S(2)}, u32[]{:S(2)}) async-start(f32[32,8,256]{2,1,0:T(8,128)} %broadcast_in_dim.2), calls=%async_computation.2 | async-start | bytes 524288 | tf_op jit(solution)/shard_map/all_to_all | solution.py:18
  48.0 0.0 copy-done
  48.0 0.3 convolution_multiply_fusion
  48.3 0.8 %copy.14 = f32[128,256]{1,0:T(8,128)} copy(f32[128,256]{0,1:T(8,128)S(1)} %convolution_multiply_fusion) | data formatting | bytes 262144
  49.1 9.1 %all-to-all-done.2 = f32[32,8,256]{2,1,0:T(8,128)S(1)} async-done(((f32[32,8,256]{2,1,0:T(8,128)}), f32[32,8,256]{2,1,0:T(8,128)S(1)}, u32[]{:S(2)}, u32[]{:S(2)}) %all-to-all-start.2) | async-done | bytes 262176 | tf_op jit(solution)/shard_map/all_to_all | solution.py:18
  58.2 0.7 %copy.21 = f32[256,256]{1,0:T(8,128)} copy(f32[256,256]{1,0:T(8,128)S(1)} %bitcast.22) | data formatting | bytes 524288
  (7 shorter events, 0.2 us)
Async XLA Ops:
  0.6 47.4 %copy-start = (bf16[256,256]{1,0:T(8,128)(2,1)S(1)}, bf16[256,256]{1,0:T(8,128)(2,1)}, u32[]{:S(2)}) copy-start(bf16[256,256]{1,0:T(8,128)(2,1)} %param.8) | copy-start | bytes 393220
  1.3 1.0 %copy-start.2 = (bf16[128,256]{1,0:T(8,128)(2,1)S(1)}, bf16[128,256]{1,0:T(8,128)(2,1)}, u32[]{:S(2)}) copy-start(bf16[128,256]{1,0:T(8,128)(2,1)} %param.9) | copy-start | bytes 196612
  2.5 6.2 %copy-start.4 = (s32[8,4]{0,1:T(4,128)S(1)}, s32[8,4]{0,1:T(4,128)}, u32[]{:S(2)}) copy-start(s32[8,4]{0,1:T(4,128)} %param.13) | copy-start | bytes 388
  2.5 7.6 %collective-permute-start = (bf16[256,128]{1,0:T(8,128)(2,1)S(1)}, bf16[256,128]{1,0:T(8,128)(2,1)S(1)}, u32[]{:S(2)}, u32[]{:S(2)}) collective-permute-start(bf16[256,128]{1,0:T(8,128)(2,1)S(1)} %fusion.5), channel_id=1, source_target_pairs={{1,0},{2,1},{3,2},{0,3},{5,4},{6,5},{7,6},{4,7},{9,8},{10,9},{11,1... | collective-permute-start | bytes 196616 | tf_op jit(solution)/shard_map/ppermute | solution.py:73
  7.6 6.5 %collective-permute-start.1 = (bf16[256,128]{1,0:T(8,128)(2,1)S(1)}, bf16[256,128]{1,0:T(8,128)(2,1)S(1)}, u32[]{:S(2)}, u32[]{:S(2)}) collective-permute-start(bf16[256,128]{1,0:T(8,128)(2,1)S(1)} %fusion.5), channel_id=1, source_target_pairs={{2,0},{3,1},{0,2},{1,3},{6,4},{7,5},{4,6},{5,7},{10,8},{11,9},{8,1... | collective-permute-start | bytes 196616 | tf_op jit(solution)/shard_map/ppermute | solution.py:73
  7.6 6.5 %collective-permute-start.2 = (bf16[256,128]{1,0:T(8,128)(2,1)S(1)}, bf16[256,128]{1,0:T(8,128)(2,1)S(1)}, u32[]{:S(2)}, u32[]{:S(2)}) collective-permute-start(bf16[256,128]{1,0:T(8,128)(2,1)S(1)} %fusion.5), channel_id=1, source_target_pairs={{3,0},{0,1},{1,2},{2,3},{7,4},{4,5},{5,6},{6,7},{11,8},{8,9},{9,10... | collective-permute-start | bytes 196616 | tf_op jit(solution)/shard_map/ppermute | solution.py:73
  14.1 0.7 %copy-start.1 = (bf16[5,256,128]{2,1,0:T(8,128)(2,1)}, bf16[5,256,128]{2,1,0:T(8,128)(2,1)S(1)}, u32[]{:S(2)}) copy-start(bf16[5,256,128]{2,1,0:T(8,128)(2,1)S(1)} %broadcast_dynamic-update-slice_fusion.block_ref) | copy-start | bytes 983044
  18.3 3.9 %copy-start.3 = (bf16[128,256]{1,0:T(8,128)(2,1)S(1)}, bf16[128,256]{1,0:T(8,128)(2,1)}, u32[]{:S(2)}) copy-start(bf16[128,256]{1,0:T(8,128)(2,1)} %param.7) | copy-start | bytes 196612
  18.3 13.6 %all-to-all-start = ((bf16[8,256,128]{2,1,0:T(8,128)(2,1)}), bf16[8,256,128]{2,1,0:T(8,128)(2,1)S(1)}, u32[]{:S(2)}, u32[]{:S(2)}) async-start(bf16[8,256,128]{2,1,0:T(8,128)(2,1)} %shard_map.86), calls=%async_computation | async-start | bytes 1048576 | tf_op jit(solution)/shard_map/all_to_all | solution.py:78
  45.3 12.9 %all-to-all-start.2 = ((f32[32,8,256]{2,1,0:T(8,128)}), f32[32,8,256]{2,1,0:T(8,128)S(1)}, u32[]{:S(2)}, u32[]{:S(2)}) async-start(f32[32,8,256]{2,1,0:T(8,128)} %broadcast_in_dim.2), calls=%async_computation.2 | async-start | bytes 524288 | tf_op jit(solution)/shard_map/all_to_all | solution.py:18

commit v9 on v6

--- a/solution.py
+++ b/solution.py
@@ -34,11 +34,11 @@
     block_scaled_grad = block_scaled_grad.reshape(row_tiles, edge, width)
 
     arrival = jnp.where(tile_rows >= 0, (tile_rows - me + reps) % reps, -1)
-    hit = arrival[None] == jnp.arange(row_tiles, dtype=jnp.int32)[:, None, None]
-    masked = jnp.where(hit[..., None, None], tile_values[None], jnp.zeros_like(tile_values[None]))
-    terms = jnp.einsum(
-        "hcsij,hif->cjf", masked, block_scaled_grad, preferred_element_type=jnp.float32
-    )
+    onehot = (arrival[..., None] == jnp.arange(row_tiles, dtype=jnp.int32)).astype(jnp.bfloat16)
+    picked = jnp.einsum(
+        "csh,hif->csif", onehot, block_scaled_grad, preferred_element_type=jnp.float32
+    ).astype(jnp.bfloat16)
+    terms = jnp.einsum("csij,csif->cjf", tile_values, picked, preferred_element_type=jnp.float32)
 
     arrived = lax.all_to_all(terms.astype(jnp.bfloat16), "grp", 0, 0, tiled=True)
     pulled = arrived.astype(jnp.float32).sum(0)

time: 56 us -> 58.2 us (1.039)
  other arithmetic: 5.01 us -> 2.54 us
  waiting for transfers between devices: 18.9 us -> 21.1 us
  matrix products: 2.49 us -> 4.26 us
    reduce_sum x1 -> x0, other arithmetic: 2.52 us -> none  [per_device(): jnp.einsum('hcsij,hif->cjf', masked, block_scaled_grad, preferred_element...]
    ppermute x3, waiting for transfers between devices: 0.04 us -> 2.26 us  [per_device(): lax.ppermute(scaled_grad, 'rep', [((i + shift) % reps, i) for i in range(...]
    dot_general x1 -> x2, matrix products: 1.27 us -> 3.02 us  [the longest x1 1.6 us: per_device(): jnp.einsum('csij,csif->cjf', tile_values, picked, preferred_element_type=...]
  transfers between devices with their start and end apart: 5 -> 5, of which waited for: 2 -> 4; matrix products, arithmetic and copies ran while one was open for 8% -> 4% of each run, Pallas kernels for 0% -> 0%
where the time goes in v9:
time: 58.2 us; the launch traced here: 57.8 us
  waiting for transfers between devices  21.1 us (36%)
  starting transfers between devices  13.8 us (24%)
  blocking collectives  13.4 us (23%)
  matrix products  4.26 us (7%)
  other arithmetic  2.54 us (4%)
  local copies, waits for them, and re-layouts  2.04 us (4%)
  between operations  0.73 us (1%)
    all_to_all x1, blocking collectives, all_reduce_a2a(): owned = lax.all_to_all(chunks, axes, 0, 0, tiled=True).sum(0)  13.4 us
    all_to_all x1, waiting for transfers between devices, per_device(): lax.all_to_all(terms.astype(jnp.bfloat16), 'grp', 0, 0, tiled=True)  9.63 us
    all_to_all x1, waiting for transfers between devices, all_reduce_a2a(): return lax.all_to_all(spread, axes, 0, 0, tiled=True).reshape(w.shape)  9.23 us
    ppermute x3, starting transfers between devices, per_device(): lax.ppermute(scaled_grad, 'rep', [((i + shift) % reps, i) for i in range(...  7.01 us
    all_to_all x1, starting transfers between devices, per_device(): lax.all_to_all(terms.astype(jnp.bfloat16), 'grp', 0, 0, tiled=True)  4.02 us
    all_to_all x1, starting transfers between devices, all_reduce_a2a(): return lax.all_to_all(spread, axes, 0, 0, tiled=True).reshape(w.shape)  2.72 us
    ppermute x3, waiting for transfers between devices, per_device(): lax.ppermute(scaled_grad, 'rep', [((i + shift) % reps, i) for i in range(...  2.26 us
    dot_general x1, matrix products, per_device(): jnp.einsum('csij,csif->cjf', tile_values, picked, preferred_element_type=...  1.6 us
  transfers between devices with their start and end apart: 5, of which 4 were waited for; matrix products, arithmetic and copies ran while one was open for 4% of the time, Pallas kernels for 0%

profile of v9, /device:TPU:0, one launch (start us, length us, event | category | flops | bytes accessed | tf_op | source)
XLA Modules:
  0.0 57.8 jit_solution(12381360066656639578)
XLA Ops:
  0.6 0.0 copy-start
  0.6 0.7 %convert_rsqrt_fusion = f32[128]{0:T(128)S(1)} fusion(s32[128]{0:T(128)} %param.11), kind=kLoop, calls=%fused_computation.30 | loop fusion | flops 128 | bytes 1024 | tf_op jit(solution)/shard_map/rsqrt | solution.py:24
  1.4 1.0 %fusion.19 = (bf16[256,128]{0,1:T(8,128)(2,1)S(1)}, bf16[128,256]{1,0:T(8,128)(2,1)S(1)}) fusion(bf16[128,256]{1,0:T(8,128)(2,1)} %param.7, f32[128]{0:T(128)S(1)} %convert_rsqrt_fusion, bf16[128,256]{1,0:T(8,128)(2,1)} %param.10, bf16[128,256]{1,0:T(8,128)(2,1)} %param.9), kind=kLoop, calls=%fused_computation.20 | loop fusion | flops 262144 | bytes 328192 | tf_op jit(solution)/shard_map/dot_general | solution.py:50
  2.4 3.1 %collective-permute-start.2 = (bf16[128,256]{1,0:T(8,128)(2,1)S(1)}, bf16[128,256]{1,0:T(8,128)(2,1)S(1)}, u32[]{:S(2)}, u32[]{:S(2)}) collective-permute-start(bf16[128,256]{1,0:T(8,128)(2,1)S(1)} %get-tuple-element.3), channel_id=1, source_target_pairs={{3,0},{0,1},{1,2},{2,3},{7,4},{4,5},{5,6},{6,7},{11,8},{8,9},{9,10... | collective-permute-start | bytes 196616 | tf_op jit(solution)/shard_map/ppermute | solution.py:32
  5.5 2.6 %collective-permute-start.1 = (bf16[128,256]{1,0:T(8,128)(2,1)S(1)}, bf16[128,256]{1,0:T(8,128)(2,1)S(1)}, u32[]{:S(2)}, u32[]{:S(2)}) collective-permute-start(bf16[128,256]{1,0:T(8,128)(2,1)S(1)} %get-tuple-element.3), channel_id=1, source_target_pairs={{2,0},{3,1},{0,2},{1,3},{6,4},{7,5},{4,6},{5,7},{10,8},{11,9},{8,1... | collective-permute-start | bytes 196616 | tf_op jit(solution)/shard_map/ppermute | solution.py:32
  8.1 1.3 %collective-permute-start = (bf16[128,256]{1,0:T(8,128)(2,1)S(1)}, bf16[128,256]{1,0:T(8,128)(2,1)S(1)}, u32[]{:S(2)}, u32[]{:S(2)}) collective-permute-start(bf16[128,256]{1,0:T(8,128)(2,1)S(1)} %get-tuple-element.3), channel_id=1, source_target_pairs={{1,0},{2,1},{3,2},{0,3},{5,4},{6,5},{7,6},{4,7},{9,8},{10,9},{11,1... | collective-permute-start | bytes 196616 | tf_op jit(solution)/shard_map/ppermute | solution.py:32
  9.4 0.7 %fusion.25 = s32[8,4]{0,1:T(4,128)S(1)} fusion(s32[8,4]{0,1:T(4,128)} %param.13, s32[]{:T(128)S(6)} %axis_index.12), kind=kLoop, calls=%fused_computation.29 | loop fusion | flops 480 | bytes 260 | tf_op jit(solution)/shard_map/jit(_where)/select_n | solution.py:36
  10.1 0.1 copy.41
  10.2 0.1 copy.42
  10.3 0.0 collective-permute-done.2
  10.3 0.1 copy.45
  10.4 2.1 %collective-permute-done.1 = bf16[128,256]{1,0:T(8,128)(2,1)S(1)} collective-permute-done((bf16[128,256]{1,0:T(8,128)(2,1)S(1)}, bf16[128,256]{1,0:T(8,128)(2,1)S(1)}, u32[]{:S(2)}, u32[]{:S(2)}) %collective-permute-start.1) | collective-permute-done | bytes 65568 | tf_op jit(solution)/shard_map/ppermute | solution.py:32
  12.5 0.1 copy.44
  12.6 0.1 collective-permute-done
  12.8 0.1 copy.43
  12.9 1.4 %convolution_convert_fusion = bf16[8,4,128,256]{3,1,2,0:T(4,128)(2,1)S(1)} fusion(bf16[1,128,256]{2,0,1:T(2,128)(2,1)S(1)} %copy.45, bf16[1,128,256]{2,0,1:T(2,128)(2,1)S(1)} %copy.44, bf16[1,128,256]{2,0,1:T(2,128)(2,1)S(1)} %copy.43, bf16[1,128,256]{2,0,1:T(2,128)(2,1)S(1)} %copy.42, s32[8,4]{1,0:T(8,128)S(1)} %copy.41), kind=kOutput, calls=%fused_computation.2 | convolution fusion | flops 10485888 | bytes 2359424 | tf_op jit(solution)/shard_map/csh,hif->csif/dot_general | solution.py:38
  14.3 0.0 copy-done
  14.3 1.6 %fusion.8 = bf16[8,128,256]{1,2,0:T(8,128)(2,1)} fusion(bf16[8,4,128,128]{3,2,1,0:T(8,128)(2,1)S(1)} %copy-done, bf16[8,4,128,256]{3,1,2,0:T(4,128)(2,1)S(1)} %convolution_convert_fusion), kind=kOutput, calls=%fused_computation.5 | convolution fusion | flops 268697600 | bytes 3670016 | tf_op jit(solution)/shard_map/csij,csif->cjf/dot_general | solution.py:41
  15.9 0.0 copy-start.1
  15.9 4.0 %all-to-all-start = ((bf16[8,128,256]{1,2,0:T(8,128)(2,1)}), bf16[8,128,256]{1,2,0:T(8,128)(2,1)S(1)}, u32[]{:S(2)}, u32[]{:S(2)}) async-start(bf16[8,128,256]{1,2,0:T(8,128)(2,1)} %fusion.8), calls=%async_computation | async-start | bytes 1048576 | tf_op jit(solution)/shard_map/all_to_all | solution.py:43
  19.9 0.1 copy.47
  20.1 9.6 %all-to-all-done = bf16[8,128,256]{1,2,0:T(8,128)(2,1)S(1)} async-done(((bf16[8,128,256]{1,2,0:T(8,128)(2,1)}), bf16[8,128,256]{1,2,0:T(8,128)(2,1)S(1)}, u32[]{:S(2)}, u32[]{:S(2)}) %all-to-all-start) | async-done | bytes 524320 | tf_op jit(solution)/shard_map/all_to_all | solution.py:43
  29.7 0.1 convert_reduce_fusion
  29.8 0.3 fusion.17
  30.0 13.4 %all_to_all.15 = f32[32,8,256]{2,1,0:T(8,128)S(1)} all-to-all(f32[32,8,256]{2,1,0:T(8,128)S(1)} %fusion.17), channel_id=1, replica_groups=mesh['grp'=8,'rep'=4] {'grp','rep'}, dimensions={0} | all-to-all | bytes 524288 | tf_op jit(solution)/shard_map/all_to_all | solution.py:14
  43.5 0.7 %broadcast_in_dim.7 = f32[32,8,256]{2,1,0:T(8,128)} broadcast(f32[8,256]{1,0:T(8,128)S(1)} %reduce_sum.19), dimensions={1,2} | broadcast | bytes 270336 | tf_op jit(solution)/shard_map/broadcast_in_dim | solution.py:15
  44.2 2.7 %all-to-all-start.2 = ((f32[32,8,256]{2,1,0:T(8,128)}), f32[32,8,256]{2,1,0:T(8,128)S(1)}, u32[]{:S(2)}, u32[]{:S(2)}) async-start(f32[32,8,256]{2,1,0:T(8,128)} %broadcast_in_dim.7), calls=%async_computation.2 | async-start | bytes 524288 | tf_op jit(solution)/shard_map/all_to_all | solution.py:16
  46.9 0.0 copy-done.1
  46.9 1.0 %convolution_multiply_fusion = f32[128,256]{1,0:T(8,128)} fusion(f32[128,256]{0,1:T(8,128)S(1)} %convert_reduce_fusion, bf16[256,256]{1,0:T(8,128)(2,1)S(1)} %copy-done.1, f32[128]{0:T(128)S(1)} %convert_rsqrt_fusion), kind=kOutput, calls=%fused_computation.6 | convolution fusion | flops 100696064 | bytes 393728 | tf_op jit(solution)/shard_map/dot_general | solution.py:46
  47.9 9.2 %all-to-all-done.2 = f32[32,8,256]{2,1,0:T(8,128)S(1)} async-done(((f32[32,8,256]{2,1,0:T(8,128)}), f32[32,8,256]{2,1,0:T(8,128)S(1)}, u32[]{:S(2)}, u32[]{:S(2)}) %all-to-all-start.2) | async-done | bytes 262176 | tf_op jit(solution)/shard_map/all_to_all | solution.py:16
  57.1 0.7 %copy.62 = f32[256,256]{1,0:T(8,128)} copy(f32[256,256]{1,0:T(8,128)S(1)} %bitcast.33) | data formatting | bytes 524288
  (1 shorter events, 0.0 us)
Async XLA Ops:
  0.6 13.7 %copy-start = (bf16[8,4,128,128]{3,2,1,0:T(8,128)(2,1)S(1)}, bf16[8,4,128,128]{3,2,1,0:T(8,128)(2,1)}, u32[]{:S(2)}) copy-start(bf16[8,4,128,128]{3,2,1,0:T(8,128)(2,1)} %param.12) | copy-start | bytes 3145732
  2.4 7.9 %collective-permute-start.2 = (bf16[128,256]{1,0:T(8,128)(2,1)S(1)}, bf16[128,256]{1,0:T(8,128)(2,1)S(1)}, u32[]{:S(2)}, u32[]{:S(2)}) collective-permute-start(bf16[128,256]{1,0:T(8,128)(2,1)S(1)} %get-tuple-element.3), channel_id=1, source_target_pairs={{3,0},{0,1},{1,2},{2,3},{7,4},{4,5},{5,6},{6,7},{11,8},{8,9},{9,10... | collective-permute-start | bytes 196616 | tf_op jit(solution)/shard_map/ppermute | solution.py:32
  5.5 7.1 %collective-permute-start.1 = (bf16[128,256]{1,0:T(8,128)(2,1)S(1)}, bf16[128,256]{1,0:T(8,128)(2,1)S(1)}, u32[]{:S(2)}, u32[]{:S(2)}) collective-permute-start(bf16[128,256]{1,0:T(8,128)(2,1)S(1)} %get-tuple-element.3), channel_id=1, source_target_pairs={{2,0},{3,1},{0,2},{1,3},{6,4},{7,5},{4,6},{5,7},{10,8},{11,9},{8,1... | collective-permute-start | bytes 196616 | tf_op jit(solution)/shard_map/ppermute | solution.py:32
  8.1 4.7 %collective-permute-start = (bf16[128,256]{1,0:T(8,128)(2,1)S(1)}, bf16[128,256]{1,0:T(8,128)(2,1)S(1)}, u32[]{:S(2)}, u32[]{:S(2)}) collective-permute-start(bf16[128,256]{1,0:T(8,128)(2,1)S(1)} %get-tuple-element.3), channel_id=1, source_target_pairs={{1,0},{2,1},{3,2},{0,3},{5,4},{6,5},{7,6},{4,7},{9,8},{10,9},{11,1... | collective-permute-start | bytes 196616 | tf_op jit(solution)/shard_map/ppermute | solution.py:32
  15.9 31.0 %copy-start.1 = (bf16[256,256]{1,0:T(8,128)(2,1)S(1)}, bf16[256,256]{1,0:T(8,128)(2,1)}, u32[]{:S(2)}) copy-start(bf16[256,256]{1,0:T(8,128)(2,1)} %param.8) | copy-start | bytes 393220
  15.9 13.8 %all-to-all-start = ((bf16[8,128,256]{1,2,0:T(8,128)(2,1)}), bf16[8,128,256]{1,2,0:T(8,128)(2,1)S(1)}, u32[]{:S(2)}, u32[]{:S(2)}) async-start(bf16[8,128,256]{1,2,0:T(8,128)(2,1)} %fusion.8), calls=%async_computation | async-start | bytes 1048576 | tf_op jit(solution)/shard_map/all_to_all | solution.py:43
  44.2 12.9 %all-to-all-start.2 = ((f32[32,8,256]{2,1,0:T(8,128)}), f32[32,8,256]{2,1,0:T(8,128)S(1)}, u32[]{:S(2)}, u32[]{:S(2)}) async-start(f32[32,8,256]{2,1,0:T(8,128)} %broadcast_in_dim.7), calls=%async_computation.2 | async-start | bytes 524288 | tf_op jit(solution)/shard_map/all_to_all | solution.py:16

commit v10 on v6

--- a/solution.py
+++ b/solution.py
@@ -6,14 +6,15 @@
 HIGHEST = lax.Precision.HIGHEST
 
 
-def all_reduce_a2a(w, axes):
+def all_reduce_a2a(w, axes, early):
     count = 1
     for name in axes:
         count *= lax.axis_size(name)
     chunks = w.reshape(count, w.shape[0] // count, w.shape[1])
     owned = lax.all_to_all(chunks, axes, 0, 0, tiled=True).sum(0)
     spread = jnp.broadcast_to(owned[None], chunks.shape)
-    return lax.all_to_all(spread, axes, 0, 0, tiled=True).reshape(w.shape)
+    spread, early = lax.optimization_barrier((spread, early))
+    return lax.all_to_all(spread, axes, 0, 0, tiled=True).reshape(w.shape), early
 
 
 def per_device(features, weight, preact, grad_out, degree, tile_values, tile_rows):
@@ -43,15 +44,20 @@
     arrived = lax.all_to_all(terms.astype(jnp.bfloat16), "grp", 0, 0, tiled=True)
     pulled = arrived.astype(jnp.float32).sum(0)
 
-    input_grad = inverse * lax.dot_general(
-        pulled, weight.astype(jnp.float32), (((1,), (1,)), ((), ())), precision=HIGHEST,
-        preferred_element_type=jnp.float32,
-    )
+    def input_rows(rows):
+        return inverse[rows] * lax.dot_general(
+            pulled[rows], weight.astype(jnp.float32), (((1,), (1,)), ((), ())), precision=HIGHEST,
+            preferred_element_type=jnp.float32,
+        )
+
+    half = rows_here // 2
+    first_rows = input_rows(slice(0, half))
     weight_local = lax.dot_general(
         scaled.astype(jnp.float32), pulled, (((0,), (0,)), ((), ())), precision=HIGHEST,
         preferred_element_type=jnp.float32,
     )
-    weight_grad = all_reduce_a2a(weight_local, ("grp", "rep"))
+    weight_grad, first_rows = all_reduce_a2a(weight_local, ("grp", "rep"), first_rows)
+    input_grad = jnp.concatenate([first_rows, input_rows(slice(half, rows_here))], axis=0)
     return (input_grad, weight_grad)
 
 

time: 56 us -> 57.3 us (1.023)
  blocking collectives: 13.4 us -> 0 us
  waiting for transfers between devices: 18.9 us -> 30.9 us
  starting transfers between devices: 13.5 us -> 15.1 us
  other arithmetic: 5.01 us -> 5.68 us
    all_to_all x1 -> x0, blocking collectives: 13.4 us -> none  [all_reduce_a2a(): owned = lax.all_to_all(chunks, axes, 0, 0, tiled=True).sum(0)]
    all_to_all x1 -> x2, waiting for transfers between devices: 9.23 us -> 19.1 us  [the longest x1 9.84 us: all_reduce_a2a(): owned = lax.all_to_all(chunks, axes, 0, 0, tiled=True).sum(0)]
    all_to_all x1 -> x2, starting transfers between devices: 2.72 us -> 5.27 us  [the longest x1 2.69 us: all_reduce_a2a(): lax.all_to_all(spread, axes, 0, 0, tiled=True).reshape(w.shape)]
    ppermute x3, waiting for transfers between devices: 0.04 us -> 2.14 us  [per_device(): lax.ppermute(scaled_grad, 'rep', [((i + shift) % reps, i) for i in range(...]
    ppermute x3, starting transfers between devices: 7.01 us -> 6.11 us  [per_device(): lax.ppermute(scaled_grad, 'rep', [((i + shift) % reps, i) for i in range(...]
    dot_general x1, matrix products: 0.26 us -> 0.97 us  [per_device(): lax.dot_general(scaled.astype(jnp.float32), pulled, (((0,), (0,)), ((), (...]
    concatenate x0 -> x1, other arithmetic: none -> 0.67 us  [per_device(): jnp.concatenate([first_rows, input_rows(slice(half, rows_here))], axis=0)]
  transfers between devices with their start and end apart: 5 -> 6, of which waited for: 2 -> 4; matrix products, arithmetic and copies ran while one was open for 8% -> 8% of each run, Pallas kernels for 0% -> 0%
where the time goes in v10:
time: 57.3 us; the launch traced here: 56.8 us
  waiting for transfers between devices  30.9 us (54%)
  starting transfers between devices  15.1 us (26%)
  other arithmetic  5.68 us (10%)
  matrix products  2.79 us (5%)
  local copies, waits for them, and re-layouts  1.7 us (3%)
  between operations  0.71 us (1%)
    all_to_all x1, waiting for transfers between devices, all_reduce_a2a(): owned = lax.all_to_all(chunks, axes, 0, 0, tiled=True).sum(0)  9.84 us
    all_to_all x1, waiting for transfers between devices, per_device(): lax.all_to_all(terms.astype(jnp.bfloat16), 'grp', 0, 0, tiled=True)  9.63 us
    all_to_all x1, waiting for transfers between devices, all_reduce_a2a(): lax.all_to_all(spread, axes, 0, 0, tiled=True).reshape(w.shape)  9.25 us
    ppermute x3, starting transfers between devices, per_device(): lax.ppermute(scaled_grad, 'rep', [((i + shift) % reps, i) for i in range(...  6.11 us
    all_to_all x1, starting transfers between devices, per_device(): lax.all_to_all(terms.astype(jnp.bfloat16), 'grp', 0, 0, tiled=True)  3.73 us
    all_to_all x1, starting transfers between devices, all_reduce_a2a(): lax.all_to_all(spread, axes, 0, 0, tiled=True).reshape(w.shape)  2.69 us
    all_to_all x1, starting transfers between devices, all_reduce_a2a(): owned = lax.all_to_all(chunks, axes, 0, 0, tiled=True).sum(0)  2.59 us
    reduce_sum x1, other arithmetic, per_device(): jnp.einsum('hcsij,hif->cjf', masked, block_scaled_grad, preferred_element...  2.52 us
  transfers between devices with their start and end apart: 6, of which 4 were waited for; matrix products, arithmetic and copies ran while one was open for 8% of the time, Pallas kernels for 0%

profile of v10, /device:TPU:0, one launch (start us, length us, event | category | flops | bytes accessed | tf_op | source)
XLA Modules:
  0.0 56.8 jit_solution(15993586592097895456)
XLA Ops:
  0.6 0.0 copy-start
  0.6 0.7 %convert_rsqrt_fusion = f32[128]{0:T(128)S(1)} fusion(s32[128]{0:T(128)} %param.11), kind=kLoop, calls=%fused_computation.29 | loop fusion | flops 128 | bytes 1024 | tf_op jit(solution)/shard_map/rsqrt | solution.py:25
  1.3 1.0 %fusion.9 = (bf16[256,128]{0,1:T(8,128)(2,1)S(1)}, bf16[128,256]{1,0:T(8,128)(2,1)S(1)}) fusion(bf16[128,256]{1,0:T(8,128)(2,1)} %param.7, f32[128]{0:T(128)S(1)} %convert_rsqrt_fusion, bf16[128,256]{1,0:T(8,128)(2,1)} %param.10, bf16[128,256]{1,0:T(8,128)(2,1)} %param.9), kind=kLoop, calls=%fused_computation.19 | loop fusion | flops 262144 | bytes 328192 | tf_op jit(solution)/shard_map/dot_general | solution.py:55
  2.3 5.1 %collective-permute-start = (bf16[128,256]{1,0:T(8,128)(2,1)S(1)}, bf16[128,256]{1,0:T(8,128)(2,1)S(1)}, u32[]{:S(2)}, u32[]{:S(2)}) collective-permute-start(bf16[128,256]{1,0:T(8,128)(2,1)S(1)} %get-tuple-element.9), channel_id=1, source_target_pairs={{1,0},{2,1},{3,2},{0,3},{5,4},{6,5},{7,6},{4,7},{9,8},{10,9},{11,1... | collective-permute-start | bytes 196616 | tf_op jit(solution)/shard_map/ppermute | solution.py:33
  7.4 0.0 collective-permute-start.1
  7.4 1.0 %collective-permute-start.2 = (bf16[128,256]{1,0:T(8,128)(2,1)S(1)}, bf16[128,256]{1,0:T(8,128)(2,1)S(1)}, u32[]{:S(2)}, u32[]{:S(2)}) collective-permute-start(bf16[128,256]{1,0:T(8,128)(2,1)S(1)} %get-tuple-element.9), channel_id=1, source_target_pairs={{3,0},{0,1},{1,2},{2,3},{7,4},{4,5},{5,6},{6,7},{11,8},{8,9},{9,10... | collective-permute-start | bytes 196616 | tf_op jit(solution)/shard_map/ppermute | solution.py:33
  8.5 0.7 %fusion.14 = s32[8,4]{0,1:T(4,128)S(1)} fusion(s32[8,4]{0,1:T(4,128)} %param.13, s32[]{:T(128)S(6)} %axis_index.12), kind=kLoop, calls=%fused_computation.28 | loop fusion | flops 480 | bytes 260 | tf_op jit(solution)/shard_map/jit(_where)/select_n | solution.py:37
  9.1 0.1 copy.14
  9.2 2.5 %convert_reduce_fusion = bf16[4,8,128,128]{3,2,1,0:T(8,128)(2,1)S(1)} fusion(pred[4,8,4]{2,1,0:T(8,128)(4,1)S(1)} %iota_compare_fusion, bf16[8,4,128,128]{3,2,1,0:T(8,128)(2,1)} %param.12), kind=kLoop, calls=%fused_computation | loop fusion | flops 5767168 | bytes 2097280 | tf_op jit(solution)/shard_map/hcsij,hif->cjf/reduce_sum | solution.py:40
  11.8 0.0 collective-permute-done
  11.8 2.1 %collective-permute-done.1 = bf16[128,256]{1,0:T(8,128)(2,1)S(1)} collective-permute-done((bf16[128,256]{1,0:T(8,128)(2,1)S(1)}, bf16[128,256]{1,0:T(8,128)(2,1)S(1)}, u32[]{:S(2)}, u32[]{:S(2)}) %collective-permute-start.1) | collective-permute-done | bytes 65568 | tf_op jit(solution)/shard_map/ppermute | solution.py:33
  13.9 0.0 collective-permute-done.2
  13.9 1.3 %fusion = bf16[8,128,256]{2,1,0:T(8,128)(2,1)} fusion(bf16[4,8,128,128]{3,2,1,0:T(8,128)(2,1)S(1)} %convert_reduce_fusion, bf16[1,128,256]{2,1,0:T(8,128)(2,1)S(1)} %bitcast.29, bf16[1,128,256]{2,1,0:T(8,128)(2,1)S(1)} %bitcast.28, bf16[1,128,256]{2,1,0:T(8,128)(2,1)S(1)} %bitcast.27, bf16[1,128,256]{2,1,0:T(8,128)(2,1)S(1)} %bitcast.26), kind=kOutput, calls=%fused_computation.2 | convolution fusion | flops 268828672 | bytes 1835008 | tf_op jit(solution)/shard_map/hcsij,hif->cjf/dot_general | solution.py:40
  15.2 3.7 %all-to-all-start = ((bf16[8,128,256]{2,1,0:T(8,128)(2,1)}), bf16[8,128,256]{2,1,0:T(8,128)(2,1)S(1)}, u32[]{:S(2)}, u32[]{:S(2)}) async-start(bf16[8,128,256]{2,1,0:T(8,128)(2,1)} %fusion), calls=%async_computation | async-start | bytes 1048576 | tf_op jit(solution)/shard_map/all_to_all | solution.py:44
  18.9 0.1 copy.13
  19.0 9.6 %all-to-all-done = bf16[8,128,256]{2,1,0:T(8,128)(2,1)S(1)} async-done(((bf16[8,128,256]{2,1,0:T(8,128)(2,1)}), bf16[8,128,256]{2,1,0:T(8,128)(2,1)S(1)}, u32[]{:S(2)}, u32[]{:S(2)}) %all-to-all-start) | async-done | bytes 524320 | tf_op jit(solution)/shard_map/all_to_all | solution.py:44
  28.7 0.1 convert_reduce_fusion.1
  28.7 1.0 %fusion.7 = f32[32,8,256]{2,1,0:T(8,128)} fusion(f32[128,256]{1,0:T(8,128)S(1)} %convert_reduce_fusion.1, bf16[256,128]{1,0:T(8,128)(2,1)S(1)} %copy.13), kind=kOutput, calls=%fused_computation.14 | convolution fusion | flops 100663296 | bytes 458752 | tf_op jit(solution)/shard_map/dot_general | solution.py:55
  29.7 2.6 %all-to-all-start.1 = ((f32[32,8,256]{2,1,0:T(8,128)}), f32[32,8,256]{2,1,0:T(8,128)S(1)}, u32[]{:S(2)}, u32[]{:S(2)}) async-start(f32[32,8,256]{2,1,0:T(8,128)} %fusion.7), calls=%async_computation.1 | async-start | bytes 524288 | tf_op jit(solution)/shard_map/all_to_all | solution.py:14
  32.3 0.1 fusion.16
  32.4 0.0 copy-done
  32.4 0.3 convolution_multiply_fusion.1
  32.7 9.8 %all-to-all-done.1 = f32[32,8,256]{2,1,0:T(8,128)S(1)} async-done(((f32[32,8,256]{2,1,0:T(8,128)}), f32[32,8,256]{2,1,0:T(8,128)S(1)}, u32[]{:S(2)}, u32[]{:S(2)}) %all-to-all-start.1) | async-done | bytes 262176 | tf_op jit(solution)/shard_map/all_to_all | solution.py:14
  42.5 0.7 %broadcast_in_dim.44 = f32[32,8,256]{2,1,0:T(8,128)} broadcast(f32[8,256]{1,0:T(8,128)S(1)} %reduce_sum.29), dimensions={1,2} | broadcast | bytes 270336 | tf_op jit(solution)/shard_map/broadcast_in_dim | solution.py:15
  43.3 2.7 %all-to-all-start.2 = ((f32[32,8,256]{2,1,0:T(8,128)}), f32[32,8,256]{2,1,0:T(8,128)S(1)}, u32[]{:S(2)}, u32[]{:S(2)}) async-start(f32[32,8,256]{2,1,0:T(8,128)} %broadcast_in_dim.44), calls=%async_computation.2 | async-start | bytes 524288 | tf_op jit(solution)/shard_map/all_to_all | solution.py:17
  45.9 0.3 convolution_multiply_fusion
  46.2 0.7 %pad_maximum_fusion = f32[128,256]{1,0:T(8,128)} fusion(f32[64,256]{1,0:T(8,128)S(1)} %convolution_multiply_fusion, f32[64,256]{1,0:T(8,128)S(1)} %convolution_multiply_fusion.1), kind=kLoop, calls=%fused_computation.13 | loop fusion | flops 32768 | bytes 262144 | tf_op jit(solution)/shard_map/concatenate | solution.py:60
  46.9 9.2 %all-to-all-done.2 = f32[32,8,256]{2,1,0:T(8,128)S(1)} async-done(((f32[32,8,256]{2,1,0:T(8,128)}), f32[32,8,256]{2,1,0:T(8,128)S(1)}, u32[]{:S(2)}, u32[]{:S(2)}) %all-to-all-start.2) | async-done | bytes 262176 | tf_op jit(solution)/shard_map/all_to_all | solution.py:17
  56.1 0.7 %copy.19 = f32[256,256]{1,0:T(8,128)} copy(f32[256,256]{1,0:T(8,128)S(1)} %bitcast.25) | data formatting | bytes 524288
  (2 shorter events, 0.0 us)
Async XLA Ops:
  0.6 31.7 %copy-start = (bf16[256,256]{1,0:T(8,128)(2,1)S(1)}, bf16[256,256]{1,0:T(8,128)(2,1)}, u32[]{:S(2)}) copy-start(bf16[256,256]{1,0:T(8,128)(2,1)} %param.8) | copy-start | bytes 393220
  2.3 9.4 %collective-permute-start = (bf16[128,256]{1,0:T(8,128)(2,1)S(1)}, bf16[128,256]{1,0:T(8,128)(2,1)S(1)}, u32[]{:S(2)}, u32[]{:S(2)}) collective-permute-start(bf16[128,256]{1,0:T(8,128)(2,1)S(1)} %get-tuple-element.9), channel_id=1, source_target_pairs={{1,0},{2,1},{3,2},{0,3},{5,4},{6,5},{7,6},{4,7},{9,8},{10,9},{11,1... | collective-permute-start | bytes 196616 | tf_op jit(solution)/shard_map/ppermute | solution.py:33
  7.4 6.5 %collective-permute-start.1 = (bf16[128,256]{1,0:T(8,128)(2,1)S(1)}, bf16[128,256]{1,0:T(8,128)(2,1)S(1)}, u32[]{:S(2)}, u32[]{:S(2)}) collective-permute-start(bf16[128,256]{1,0:T(8,128)(2,1)S(1)} %get-tuple-element.9), channel_id=1, source_target_pairs={{2,0},{3,1},{0,2},{1,3},{6,4},{7,5},{4,6},{5,7},{10,8},{11,9},{8,1... | collective-permute-start | bytes 196616 | tf_op jit(solution)/shard_map/ppermute | solution.py:33
  7.4 6.5 %collective-permute-start.2 = (bf16[128,256]{1,0:T(8,128)(2,1)S(1)}, bf16[128,256]{1,0:T(8,128)(2,1)S(1)}, u32[]{:S(2)}, u32[]{:S(2)}) collective-permute-start(bf16[128,256]{1,0:T(8,128)(2,1)S(1)} %get-tuple-element.9), channel_id=1, source_target_pairs={{3,0},{0,1},{1,2},{2,3},{7,4},{4,5},{5,6},{6,7},{11,8},{8,9},{9,10... | collective-permute-start | bytes 196616 | tf_op jit(solution)/shard_map/ppermute | solution.py:33
  15.2 13.5 %all-to-all-start = ((bf16[8,128,256]{2,1,0:T(8,128)(2,1)}), bf16[8,128,256]{2,1,0:T(8,128)(2,1)S(1)}, u32[]{:S(2)}, u32[]{:S(2)}) async-start(bf16[8,128,256]{2,1,0:T(8,128)(2,1)} %fusion), calls=%async_computation | async-start | bytes 1048576 | tf_op jit(solution)/shard_map/all_to_all | solution.py:44
  29.7 12.8 %all-to-all-start.1 = ((f32[32,8,256]{2,1,0:T(8,128)}), f32[32,8,256]{2,1,0:T(8,128)S(1)}, u32[]{:S(2)}, u32[]{:S(2)}) async-start(f32[32,8,256]{2,1,0:T(8,128)} %fusion.7), calls=%async_computation.1 | async-start | bytes 524288 | tf_op jit(solution)/shard_map/all_to_all | solution.py:14
  43.3 12.9 %all-to-all-start.2 = ((f32[32,8,256]{2,1,0:T(8,128)}), f32[32,8,256]{2,1,0:T(8,128)S(1)}, u32[]{:S(2)}, u32[]{:S(2)}) async-start(f32[32,8,256]{2,1,0:T(8,128)} %broadcast_in_dim.44), calls=%async_computation.2 | async-start | bytes 524288 | tf_op jit(solution)/shard_map/all_to_all | solution.py:17

commit v11 on v6

--- a/solution.py
+++ b/solution.py
@@ -30,14 +30,16 @@
     parts = [scaled_grad]
     for shift in range(1, reps):
         parts.append(lax.ppermute(scaled_grad, "rep", [((i + shift) % reps, i) for i in range(reps)]))
-    block_scaled_grad = jnp.stack(parts)
-    block_scaled_grad = block_scaled_grad.reshape(row_tiles, edge, width)
+    arrived_rows = jnp.stack(parts[1:])
 
     arrival = jnp.where(tile_rows >= 0, (tile_rows - me + reps) % reps, -1)
-    hit = arrival[None] == jnp.arange(row_tiles, dtype=jnp.int32)[:, None, None]
+    hit = arrival[None] == jnp.arange(reps, dtype=jnp.int32)[:, None, None]
     masked = jnp.where(hit[..., None, None], tile_values[None], jnp.zeros_like(tile_values[None]))
-    terms = jnp.einsum(
-        "hcsij,hif->cjf", masked, block_scaled_grad, preferred_element_type=jnp.float32
+    own_terms = jnp.einsum(
+        "csij,if->cjf", masked[0], scaled_grad, preferred_element_type=jnp.float32
+    )
+    terms = own_terms + jnp.einsum(
+        "hcsij,hif->cjf", masked[1:], arrived_rows, preferred_element_type=jnp.float32
     )
 
     arrived = lax.all_to_all(terms.astype(jnp.bfloat16), "grp", 0, 0, tiled=True)

time: 56 us -> 56 us (level)
    reduce_sum x1 -> x2, other arithmetic: 2.52 us -> 0.74 us  [the longest x1 0.59 us: per_device(): jnp.einsum('hcsij,hif->cjf', masked[1:], arrived_rows, preferred_element_...]
    select_n x0 -> x1, other arithmetic: none -> 1.59 us  [per_device(): jnp.where(hit[..., None, None], tile_values[None], jnp.zeros_like(tile_va...]
    dot_general x1 -> x2, matrix products: 1.27 us -> 1.59 us  [the longest x1 1.27 us: per_device(): jnp.einsum('hcsij,hif->cjf', masked[1:], arrived_rows, preferred_element_...]
where the time goes in v11:
time: 56 us; the launch traced here: 55.6 us
  waiting for transfers between devices  18.9 us (34%)
  starting transfers between devices  13.5 us (24%)
  blocking collectives  13.3 us (24%)
  other arithmetic  4.82 us (9%)
  matrix products  2.81 us (5%)
  local copies, waits for them, and re-layouts  1.63 us (3%)
  between operations  0.74 us (1%)
    all_to_all x1, blocking collectives, all_reduce_a2a(): owned = lax.all_to_all(chunks, axes, 0, 0, tiled=True).sum(0)  13.3 us
    all_to_all x1, waiting for transfers between devices, per_device(): lax.all_to_all(terms.astype(jnp.bfloat16), 'grp', 0, 0, tiled=True)  9.63 us
    all_to_all x1, waiting for transfers between devices, all_reduce_a2a(): return lax.all_to_all(spread, axes, 0, 0, tiled=True).reshape(w.shape)  9.23 us
    ppermute x3, starting transfers between devices, per_device(): lax.ppermute(scaled_grad, 'rep', [((i + shift) % reps, i) for i in range(...  7.01 us
    all_to_all x1, starting transfers between devices, per_device(): lax.all_to_all(terms.astype(jnp.bfloat16), 'grp', 0, 0, tiled=True)  3.72 us
    all_to_all x1, starting transfers between devices, all_reduce_a2a(): return lax.all_to_all(spread, axes, 0, 0, tiled=True).reshape(w.shape)  2.72 us
    select_n x1, other arithmetic, per_device(): jnp.where(hit[..., None, None], tile_values[None], jnp.zeros_like(tile_va...  1.59 us
    dot_general x1, matrix products, per_device(): jnp.einsum('hcsij,hif->cjf', masked[1:], arrived_rows, preferred_element_...  1.27 us
  transfers between devices with their start and end apart: 5, of which 2 were waited for; matrix products, arithmetic and copies ran while one was open for 8% of the time, Pallas kernels for 0%

profile of v11, /device:TPU:0, one launch (start us, length us, event | category | flops | bytes accessed | tf_op | source)
XLA Modules:
  0.0 55.6 jit_solution(16256035863556916304)
XLA Ops:
  0.6 0.0 copy-start
  0.6 0.7 %convert_rsqrt_fusion = f32[128]{0:T(128)S(1)} fusion(s32[128]{0:T(128)} %param.11), kind=kLoop, calls=%fused_computation.28 | loop fusion | flops 128 | bytes 1024 | tf_op jit(solution)/shard_map/rsqrt | solution.py:24
  1.3 1.0 %fusion.8 = (bf16[256,128]{0,1:T(8,128)(2,1)S(1)}, bf16[128,256]{1,0:T(8,128)(2,1)S(1)}) fusion(bf16[128,256]{1,0:T(8,128)(2,1)} %param.7, f32[128]{0:T(128)S(1)} %convert_rsqrt_fusion, bf16[128,256]{1,0:T(8,128)(2,1)} %param.10, bf16[128,256]{1,0:T(8,128)(2,1)} %param.9), kind=kLoop, calls=%fused_computation.18 | loop fusion | flops 262144 | bytes 328192 | tf_op jit(solution)/shard_map/dot_general | solution.py:52
  2.3 3.1 %collective-permute-start.2 = (bf16[128,256]{1,0:T(8,128)(2,1)S(1)}, bf16[128,256]{1,0:T(8,128)(2,1)S(1)}, u32[]{:S(2)}, u32[]{:S(2)}) collective-permute-start(bf16[128,256]{1,0:T(8,128)(2,1)S(1)} %get-tuple-element.3), channel_id=1, source_target_pairs={{3,0},{0,1},{1,2},{2,3},{7,4},{4,5},{5,6},{6,7},{11,8},{8,9},{9,10... | collective-permute-start | bytes 196616 | tf_op jit(solution)/shard_map/ppermute | solution.py:32
  5.4 2.6 %collective-permute-start.1 = (bf16[128,256]{1,0:T(8,128)(2,1)S(1)}, bf16[128,256]{1,0:T(8,128)(2,1)S(1)}, u32[]{:S(2)}, u32[]{:S(2)}) collective-permute-start(bf16[128,256]{1,0:T(8,128)(2,1)S(1)} %get-tuple-element.3), channel_id=1, source_target_pairs={{2,0},{3,1},{0,2},{1,3},{6,4},{7,5},{4,6},{5,7},{10,8},{11,9},{8,1... | collective-permute-start | bytes 196616 | tf_op jit(solution)/shard_map/ppermute | solution.py:32
  8.0 1.3 %collective-permute-start = (bf16[128,256]{1,0:T(8,128)(2,1)S(1)}, bf16[128,256]{1,0:T(8,128)(2,1)S(1)}, u32[]{:S(2)}, u32[]{:S(2)}) collective-permute-start(bf16[128,256]{1,0:T(8,128)(2,1)S(1)} %get-tuple-element.3), channel_id=1, source_target_pairs={{1,0},{2,1},{3,2},{0,3},{5,4},{6,5},{7,6},{4,7},{9,8},{10,9},{11,1... | collective-permute-start | bytes 196616 | tf_op jit(solution)/shard_map/ppermute | solution.py:32
  9.4 0.7 %fusion.13 = s32[8,4]{0,1:T(4,128)S(1)} fusion(s32[8,4]{0,1:T(4,128)} %param.13, s32[]{:T(128)S(6)} %axis_index.12), kind=kLoop, calls=%fused_computation.27 | loop fusion | flops 480 | bytes 260 | tf_op jit(solution)/shard_map/jit(_where)/select_n | solution.py:35
  10.0 0.1 copy.13
  10.1 1.6 %broadcast_select_fusion = bf16[4,8,4,128,128]{4,3,2,1,0:T(8,128)(2,1)S(1)} fusion(pred[4,8,4]{2,1,0:T(8,128)(4,1)S(1)} %iota_compare_fusion, bf16[8,4,128,128]{3,2,1,0:T(8,128)(2,1)} %param.12), kind=kLoop, calls=%fused_computation.1 | loop fusion | flops 2097152 | bytes 5243008 | tf_op jit(solution)/shard_map/jit(_where)/select_n | solution.py:37
  11.7 0.1 convert_reduce_fusion.1
  11.9 0.6 %convert_reduce_fusion = bf16[3,8,128,128]{3,2,1,0:T(8,128)(2,1)S(1)} fusion(bf16[4,8,4,128,128]{4,3,2,1,0:T(8,128)(2,1)S(1)} %broadcast_select_fusion), kind=kLoop, calls=%fused_computation | loop fusion | flops 2752512 | bytes 3932160 | tf_op jit(solution)/shard_map/hcsij,hif->cjf/reduce_sum | solution.py:41
  12.5 0.3 fusion.10
  12.8 0.0 collective-permute-done.2
  12.8 0.0 collective-permute-done.1
  12.8 0.0 collective-permute-done
  12.9 1.3 %fusion.1 = bf16[8,128,256]{2,1,0:T(8,128)(2,1)} fusion(f32[8,128,256]{2,1,0:T(8,128)S(1)} %fusion.10, bf16[3,8,128,128]{3,2,1,0:T(8,128)(2,1)S(1)} %convert_reduce_fusion, bf16[1,128,256]{2,1,0:T(8,128)(2,1)S(1)} %bitcast.31, bf16[1,128,256]{2,1,0:T(8,128)(2,1)S(1)} %bitcast.32, bf16[1,128,256]{2,1,0:T(8,128)(2,1)S(1)} %bitcast.33), kind=kOutput, calls=%fused_computation.5 | convolution fusion | flops 202047488 | bytes 2555904 | tf_op jit(solution)/shard_map/hcsij,hif->cjf/dot_general | solution.py:41
  14.1 3.7 %all-to-all-start = ((bf16[8,128,256]{2,1,0:T(8,128)(2,1)}), bf16[8,128,256]{2,1,0:T(8,128)(2,1)S(1)}, u32[]{:S(2)}, u32[]{:S(2)}) async-start(bf16[8,128,256]{2,1,0:T(8,128)(2,1)} %fusion.1), calls=%async_computation | async-start | bytes 1048576 | tf_op jit(solution)/shard_map/all_to_all | solution.py:45
  17.8 0.1 copy.16
  18.0 9.6 %all-to-all-done = bf16[8,128,256]{2,1,0:T(8,128)(2,1)S(1)} async-done(((bf16[8,128,256]{2,1,0:T(8,128)(2,1)}), bf16[8,128,256]{2,1,0:T(8,128)(2,1)S(1)}, u32[]{:S(2)}, u32[]{:S(2)}) %all-to-all-start) | async-done | bytes 524320 | tf_op jit(solution)/shard_map/all_to_all | solution.py:45
  27.6 0.1 convert_reduce_fusion.2
  27.7 0.3 fusion.6
  27.9 13.3 %all_to_all.15 = f32[32,8,256]{2,1,0:T(8,128)S(1)} all-to-all(f32[32,8,256]{2,1,0:T(8,128)S(1)} %fusion.6), channel_id=1, replica_groups=mesh['grp'=8,'rep'=4] {'grp','rep'}, dimensions={0} | all-to-all | bytes 524288 | tf_op jit(solution)/shard_map/all_to_all | solution.py:14
  41.3 0.7 %broadcast_in_dim.44 = f32[32,8,256]{2,1,0:T(8,128)} broadcast(f32[8,256]{1,0:T(8,128)S(1)} %reduce_sum.39), dimensions={1,2} | broadcast | bytes 270336 | tf_op jit(solution)/shard_map/broadcast_in_dim | solution.py:15
  42.0 2.7 %all-to-all-start.2 = ((f32[32,8,256]{2,1,0:T(8,128)}), f32[32,8,256]{2,1,0:T(8,128)S(1)}, u32[]{:S(2)}, u32[]{:S(2)}) async-start(f32[32,8,256]{2,1,0:T(8,128)} %broadcast_in_dim.44), calls=%async_computation.2 | async-start | bytes 524288 | tf_op jit(solution)/shard_map/all_to_all | solution.py:16
  44.7 0.0 copy-done
  44.7 1.0 %convolution_multiply_fusion = f32[128,256]{1,0:T(8,128)} fusion(f32[128,256]{1,0:T(8,128)S(1)} %convert_reduce_fusion.2, bf16[256,256]{1,0:T(8,128)(2,1)S(1)} %copy-done, f32[128]{0:T(128)S(1)} %convert_rsqrt_fusion), kind=kOutput, calls=%fused_computation.6 | convolution fusion | flops 100696064 | bytes 393728 | tf_op jit(solution)/shard_map/dot_general | solution.py:48
  45.7 9.2 %all-to-all-done.2 = f32[32,8,256]{2,1,0:T(8,128)S(1)} async-done(((f32[32,8,256]{2,1,0:T(8,128)}), f32[32,8,256]{2,1,0:T(8,128)S(1)}, u32[]{:S(2)}, u32[]{:S(2)}) %all-to-all-start.2) | async-done | bytes 262176 | tf_op jit(solution)/shard_map/all_to_all | solution.py:16
  54.9 0.7 %copy.21 = f32[256,256]{1,0:T(8,128)} copy(f32[256,256]{1,0:T(8,128)S(1)} %bitcast.30) | data formatting | bytes 524288
  (2 shorter events, 0.0 us)
Async XLA Ops:
  0.6 44.1 %copy-start = (bf16[256,256]{1,0:T(8,128)(2,1)S(1)}, bf16[256,256]{1,0:T(8,128)(2,1)}, u32[]{:S(2)}) copy-start(bf16[256,256]{1,0:T(8,128)(2,1)} %param.8) | copy-start | bytes 393220
  2.3 10.5 %collective-permute-start.2 = (bf16[128,256]{1,0:T(8,128)(2,1)S(1)}, bf16[128,256]{1,0:T(8,128)(2,1)S(1)}, u32[]{:S(2)}, u32[]{:S(2)}) collective-permute-start(bf16[128,256]{1,0:T(8,128)(2,1)S(1)} %get-tuple-element.3), channel_id=1, source_target_pairs={{3,0},{0,1},{1,2},{2,3},{7,4},{4,5},{5,6},{6,7},{11,8},{8,9},{9,10... | collective-permute-start | bytes 196616 | tf_op jit(solution)/shard_map/ppermute | solution.py:32
  5.4 7.4 %collective-permute-start.1 = (bf16[128,256]{1,0:T(8,128)(2,1)S(1)}, bf16[128,256]{1,0:T(8,128)(2,1)S(1)}, u32[]{:S(2)}, u32[]{:S(2)}) collective-permute-start(bf16[128,256]{1,0:T(8,128)(2,1)S(1)} %get-tuple-element.3), channel_id=1, source_target_pairs={{2,0},{3,1},{0,2},{1,3},{6,4},{7,5},{4,6},{5,7},{10,8},{11,9},{8,1... | collective-permute-start | bytes 196616 | tf_op jit(solution)/shard_map/ppermute | solution.py:32
  8.0 4.8 %collective-permute-start = (bf16[128,256]{1,0:T(8,128)(2,1)S(1)}, bf16[128,256]{1,0:T(8,128)(2,1)S(1)}, u32[]{:S(2)}, u32[]{:S(2)}) collective-permute-start(bf16[128,256]{1,0:T(8,128)(2,1)S(1)} %get-tuple-element.3), channel_id=1, source_target_pairs={{1,0},{2,1},{3,2},{0,3},{5,4},{6,5},{7,6},{4,7},{9,8},{10,9},{11,1... | collective-permute-start | bytes 196616 | tf_op jit(solution)/shard_map/ppermute | solution.py:32
  14.1 13.5 %all-to-all-start = ((bf16[8,128,256]{2,1,0:T(8,128)(2,1)}), bf16[8,128,256]{2,1,0:T(8,128)(2,1)S(1)}, u32[]{:S(2)}, u32[]{:S(2)}) async-start(bf16[8,128,256]{2,1,0:T(8,128)(2,1)} %fusion.1), calls=%async_computation | async-start | bytes 1048576 | tf_op jit(solution)/shard_map/all_to_all | solution.py:45
  42.0 12.9 %all-to-all-start.2 = ((f32[32,8,256]{2,1,0:T(8,128)}), f32[32,8,256]{2,1,0:T(8,128)S(1)}, u32[]{:S(2)}, u32[]{:S(2)}) async-start(f32[32,8,256]{2,1,0:T(8,128)} %broadcast_in_dim.44), calls=%async_computation.2 | async-start | bytes 524288 | tf_op jit(solution)/shard_map/all_to_all | solution.py:16

commit v12 on v6

--- a/solution.py
+++ b/solution.py
@@ -35,9 +35,13 @@
 
     arrival = jnp.where(tile_rows >= 0, (tile_rows - me + reps) % reps, -1)
     hit = arrival[None] == jnp.arange(row_tiles, dtype=jnp.int32)[:, None, None]
-    masked = jnp.where(hit[..., None, None], tile_values[None], jnp.zeros_like(tile_values[None]))
+    tiles = tile_values[None].astype(jnp.float32)
+    summed = jnp.where(hit[..., None, None], tiles, jnp.zeros_like(tiles)).sum(axis=2)
+    high = summed.astype(jnp.bfloat16)
+    low = (summed - high.astype(jnp.float32)).astype(jnp.bfloat16)
     terms = jnp.einsum(
-        "hcsij,hif->cjf", masked, block_scaled_grad, preferred_element_type=jnp.float32
+        "phcij,hif->cjf", jnp.stack([high, low]), block_scaled_grad,
+        preferred_element_type=jnp.float32,
     )
 
     arrived = lax.all_to_all(terms.astype(jnp.bfloat16), "grp", 0, 0, tiled=True)

time: 56 us -> 56 us (level)
    convert_element_type x0 -> x2, other arithmetic: none -> 1.98 us  [the longest x1 1.45 us: per_device(): tiles = tile_values[None].astype(jnp.float32)]
    reduce_sum x1 -> x2, other arithmetic: 2.52 us -> 1.4 us  [the longest x1 0.97 us: per_device(): jnp.where(hit[..., None, None], tiles, jnp.zeros_like(tiles)).sum(axis=2)]
    select_n x1, other arithmetic: 0.69 us -> 0.01 us  [per_device(): arrival = jnp.where(tile_rows >= 0, (tile_rows - me + reps) % reps, -1)]
where the time goes in v12:
time: 56 us; the launch traced here: 55.6 us
  waiting for transfers between devices  18.9 us (34%)
  starting transfers between devices  13.5 us (24%)
  blocking collectives  13.2 us (24%)
  other arithmetic  5.21 us (9%)
  matrix products  2.51 us (4%)
  local copies, waits for them, and re-layouts  1.63 us (3%)
  between operations  0.76 us (1%)
    all_to_all x1, blocking collectives, all_reduce_a2a(): owned = lax.all_to_all(chunks, axes, 0, 0, tiled=True).sum(0)  13.2 us
    all_to_all x1, waiting for transfers between devices, per_device(): lax.all_to_all(terms.astype(jnp.bfloat16), 'grp', 0, 0, tiled=True)  9.63 us
    all_to_all x1, waiting for transfers between devices, all_reduce_a2a(): return lax.all_to_all(spread, axes, 0, 0, tiled=True).reshape(w.shape)  9.23 us
    ppermute x3, starting transfers between devices, per_device(): lax.ppermute(scaled_grad, 'rep', [((i + shift) % reps, i) for i in range(...  7.01 us
    all_to_all x1, starting transfers between devices, per_device(): lax.all_to_all(terms.astype(jnp.bfloat16), 'grp', 0, 0, tiled=True)  3.72 us
    all_to_all x1, starting transfers between devices, all_reduce_a2a(): return lax.all_to_all(spread, axes, 0, 0, tiled=True).reshape(w.shape)  2.72 us
    convert_element_type x1, other arithmetic, per_device(): tiles = tile_values[None].astype(jnp.float32)  1.45 us
    dot_general x1, matrix products, per_device(): jnp.einsum('phcij,hif->cjf', jnp.stack([high, low]), block_scaled_grad, p...  1.29 us
  transfers between devices with their start and end apart: 5, of which 2 were waited for; matrix products, arithmetic and copies ran while one was open for 8% of the time, Pallas kernels for 0%

profile of v12, /device:TPU:0, one launch (start us, length us, event | category | flops | bytes accessed | tf_op | source)
XLA Modules:
  0.0 55.6 jit_solution(15783734761254726315)
XLA Ops:
  0.6 0.0 copy-start
  0.6 0.0 copy-start.1
  0.7 0.7 %convert_rsqrt_fusion = f32[128]{0:T(128)S(1)} fusion(s32[128]{0:T(128)} %param.11), kind=kLoop, calls=%fused_computation.29 | loop fusion | flops 128 | bytes 1024 | tf_op jit(solution)/shard_map/rsqrt | solution.py:24
  1.4 1.0 %fusion.10 = (bf16[256,128]{0,1:T(8,128)(2,1)S(1)}, bf16[128,256]{1,0:T(8,128)(2,1)S(1)}) fusion(bf16[128,256]{1,0:T(8,128)(2,1)} %param.7, f32[128]{0:T(128)S(1)} %convert_rsqrt_fusion, bf16[128,256]{1,0:T(8,128)(2,1)} %param.10, bf16[128,256]{1,0:T(8,128)(2,1)} %param.9), kind=kLoop, calls=%fused_computation.21 | loop fusion | flops 262144 | bytes 328192 | tf_op jit(solution)/shard_map/dot_general | solution.py:54
  2.4 3.1 %collective-permute-start.2 = (bf16[128,256]{1,0:T(8,128)(2,1)S(1)}, bf16[128,256]{1,0:T(8,128)(2,1)S(1)}, u32[]{:S(2)}, u32[]{:S(2)}) collective-permute-start(bf16[128,256]{1,0:T(8,128)(2,1)S(1)} %get-tuple-element.5), channel_id=1, source_target_pairs={{3,0},{0,1},{1,2},{2,3},{7,4},{4,5},{5,6},{6,7},{11,8},{8,9},{9,10... | collective-permute-start | bytes 196616 | tf_op jit(solution)/shard_map/ppermute | solution.py:32
  5.4 2.6 %collective-permute-start.1 = (bf16[128,256]{1,0:T(8,128)(2,1)S(1)}, bf16[128,256]{1,0:T(8,128)(2,1)S(1)}, u32[]{:S(2)}, u32[]{:S(2)}) collective-permute-start(bf16[128,256]{1,0:T(8,128)(2,1)S(1)} %get-tuple-element.5), channel_id=1, source_target_pairs={{2,0},{3,1},{0,2},{1,3},{6,4},{7,5},{4,6},{5,7},{10,8},{11,9},{8,1... | collective-permute-start | bytes 196616 | tf_op jit(solution)/shard_map/ppermute | solution.py:32
  8.0 1.3 %collective-permute-start = (bf16[128,256]{1,0:T(8,128)(2,1)S(1)}, bf16[128,256]{1,0:T(8,128)(2,1)S(1)}, u32[]{:S(2)}, u32[]{:S(2)}) collective-permute-start(bf16[128,256]{1,0:T(8,128)(2,1)S(1)} %get-tuple-element.5), channel_id=1, source_target_pairs={{1,0},{2,1},{3,2},{0,3},{5,4},{6,5},{7,6},{4,7},{9,8},{10,9},{11,1... | collective-permute-start | bytes 196616 | tf_op jit(solution)/shard_map/ppermute | solution.py:32
  9.4 1.5 %convert_element_type.65 = f32[8,4,128,128]{3,2,1,0:T(8,128)S(1)} convert(bf16[8,4,128,128]{3,2,1,0:T(8,128)(2,1)} %param.12) | non-fusion elementwise | flops 524288 | bytes 3145728 | tf_op jit(solution)/shard_map/convert_element_type | solution.py:38
  10.8 0.0 copy-done.1
  10.9 0.1 copy.13
  11.0 1.0 %select_reduce_fusion = f32[4,8,128,128]{3,2,1,0:T(8,128)S(1)} fusion(f32[8,4,128,128]{3,2,1,0:T(8,128)S(1)} %convert_element_type.65, pred[4,8,4]{2,1,0:T(8,128)(4,1)S(1)} %iota_compare_fusion), kind=kLoop, calls=%fused_computation | loop fusion | flops 3670016 | bytes 4194432 | tf_op jit(solution)/shard_map/reduce_sum | solution.py:39
  11.9 0.5 fusion
  12.5 0.4 convert_reduce_fusion
  12.9 0.0 collective-permute-done.2
  12.9 0.0 collective-permute-done.1
  12.9 0.0 collective-permute-done
  12.9 1.3 %fusion.1 = bf16[8,128,256]{2,1,0:T(8,128)(2,1)} fusion(bf16[4,8,128,128]{3,2,1,0:T(8,128)(2,1)S(1)} %convert_reduce_fusion, bf16[1,128,256]{2,1,0:T(8,128)(2,1)S(1)} %bitcast.33, bf16[1,128,256]{2,1,0:T(8,128)(2,1)S(1)} %bitcast.34, bf16[1,128,256]{2,1,0:T(8,128)(2,1)S(1)} %bitcast.35, bf16[1,128,256]{2,1,0:T(8,128)(2,1)S(1)} %bitcast.32), kind=kOutput, calls=%fused_computation.6 | convolution fusion | flops 268828672 | bytes 1835008 | tf_op jit(solution)/shard_map/phcij,hif->cjf/dot_general | solution.py:42
  14.2 3.7 %all-to-all-start = ((bf16[8,128,256]{2,1,0:T(8,128)(2,1)}), bf16[8,128,256]{2,1,0:T(8,128)(2,1)S(1)}, u32[]{:S(2)}, u32[]{:S(2)}) async-start(bf16[8,128,256]{2,1,0:T(8,128)(2,1)} %fusion.1), calls=%async_computation | async-start | bytes 1048576 | tf_op jit(solution)/shard_map/all_to_all | solution.py:47
  17.9 0.1 copy.15
  18.1 9.6 %all-to-all-done = bf16[8,128,256]{2,1,0:T(8,128)(2,1)S(1)} async-done(((bf16[8,128,256]{2,1,0:T(8,128)(2,1)}), bf16[8,128,256]{2,1,0:T(8,128)(2,1)S(1)}, u32[]{:S(2)}, u32[]{:S(2)}) %all-to-all-start) | async-done | bytes 524320 | tf_op jit(solution)/shard_map/all_to_all | solution.py:47
  27.7 0.1 convert_reduce_fusion.1
  27.8 0.3 fusion.8
  28.0 13.2 %all_to_all.15 = f32[32,8,256]{2,1,0:T(8,128)S(1)} all-to-all(f32[32,8,256]{2,1,0:T(8,128)S(1)} %fusion.8), channel_id=1, replica_groups=mesh['grp'=8,'rep'=4] {'grp','rep'}, dimensions={0} | all-to-all | bytes 524288 | tf_op jit(solution)/shard_map/all_to_all | solution.py:14
  41.3 0.7 %broadcast_in_dim.44 = f32[32,8,256]{2,1,0:T(8,128)} broadcast(f32[8,256]{1,0:T(8,128)S(1)} %reduce_sum.42), dimensions={1,2} | broadcast | bytes 270336 | tf_op jit(solution)/shard_map/broadcast_in_dim | solution.py:15
  42.0 2.7 %all-to-all-start.2 = ((f32[32,8,256]{2,1,0:T(8,128)}), f32[32,8,256]{2,1,0:T(8,128)S(1)}, u32[]{:S(2)}, u32[]{:S(2)}) async-start(f32[32,8,256]{2,1,0:T(8,128)} %broadcast_in_dim.44), calls=%async_computation.2 | async-start | bytes 524288 | tf_op jit(solution)/shard_map/all_to_all | solution.py:16
  44.7 0.0 copy-done
  44.7 1.0 %convolution_multiply_fusion = f32[128,256]{1,0:T(8,128)} fusion(f32[128,256]{1,0:T(8,128)S(1)} %convert_reduce_fusion.1, bf16[256,256]{1,0:T(8,128)(2,1)S(1)} %copy-done, f32[128]{0:T(128)S(1)} %convert_rsqrt_fusion), kind=kOutput, calls=%fused_computation.7 | convolution fusion | flops 100696064 | bytes 393728 | tf_op jit(solution)/shard_map/dot_general | solution.py:50
  45.7 9.2 %all-to-all-done.2 = f32[32,8,256]{2,1,0:T(8,128)S(1)} async-done(((f32[32,8,256]{2,1,0:T(8,128)}), f32[32,8,256]{2,1,0:T(8,128)S(1)}, u32[]{:S(2)}, u32[]{:S(2)}) %all-to-all-start.2) | async-done | bytes 262176 | tf_op jit(solution)/shard_map/all_to_all | solution.py:16
  54.9 0.7 %copy.19 = f32[256,256]{1,0:T(8,128)} copy(f32[256,256]{1,0:T(8,128)S(1)} %bitcast.31) | data formatting | bytes 524288
  (3 shorter events, 0.1 us)
Async XLA Ops:
  0.6 44.1 %copy-start = (bf16[256,256]{1,0:T(8,128)(2,1)S(1)}, bf16[256,256]{1,0:T(8,128)(2,1)}, u32[]{:S(2)}) copy-start(bf16[256,256]{1,0:T(8,128)(2,1)} %param.8) | copy-start | bytes 393220
  0.6 10.2 %copy-start.1 = (s32[8,4]{0,1:T(4,128)S(1)}, s32[8,4]{0,1:T(4,128)}, u32[]{:S(2)}) copy-start(s32[8,4]{0,1:T(4,128)} %param.13) | copy-start | bytes 388
  2.4 10.6 %collective-permute-start.2 = (bf16[128,256]{1,0:T(8,128)(2,1)S(1)}, bf16[128,256]{1,0:T(8,128)(2,1)S(1)}, u32[]{:S(2)}, u32[]{:S(2)}) collective-permute-start(bf16[128,256]{1,0:T(8,128)(2,1)S(1)} %get-tuple-element.5), channel_id=1, source_target_pairs={{3,0},{0,1},{1,2},{2,3},{7,4},{4,5},{5,6},{6,7},{11,8},{8,9},{9,10... | collective-permute-start | bytes 196616 | tf_op jit(solution)/shard_map/ppermute | solution.py:32
  5.4 7.5 %collective-permute-start.1 = (bf16[128,256]{1,0:T(8,128)(2,1)S(1)}, bf16[128,256]{1,0:T(8,128)(2,1)S(1)}, u32[]{:S(2)}, u32[]{:S(2)}) collective-permute-start(bf16[128,256]{1,0:T(8,128)(2,1)S(1)} %get-tuple-element.5), channel_id=1, source_target_pairs={{2,0},{3,1},{0,2},{1,3},{6,4},{7,5},{4,6},{5,7},{10,8},{11,9},{8,1... | collective-permute-start | bytes 196616 | tf_op jit(solution)/shard_map/ppermute | solution.py:32
  8.0 4.9 %collective-permute-start = (bf16[128,256]{1,0:T(8,128)(2,1)S(1)}, bf16[128,256]{1,0:T(8,128)(2,1)S(1)}, u32[]{:S(2)}, u32[]{:S(2)}) collective-permute-start(bf16[128,256]{1,0:T(8,128)(2,1)S(1)} %get-tuple-element.5), channel_id=1, source_target_pairs={{1,0},{2,1},{3,2},{0,3},{5,4},{6,5},{7,6},{4,7},{9,8},{10,9},{11,1... | collective-permute-start | bytes 196616 | tf_op jit(solution)/shard_map/ppermute | solution.py:32
  14.2 13.5 %all-to-all-start = ((bf16[8,128,256]{2,1,0:T(8,128)(2,1)}), bf16[8,128,256]{2,1,0:T(8,128)(2,1)S(1)}, u32[]{:S(2)}, u32[]{:S(2)}) async-start(bf16[8,128,256]{2,1,0:T(8,128)(2,1)} %fusion.1), calls=%async_computation | async-start | bytes 1048576 | tf_op jit(solution)/shard_map/all_to_all | solution.py:47
  42.0 12.9 %all-to-all-start.2 = ((f32[32,8,256]{2,1,0:T(8,128)}), f32[32,8,256]{2,1,0:T(8,128)S(1)}, u32[]{:S(2)}, u32[]{:S(2)}) async-start(f32[32,8,256]{2,1,0:T(8,128)} %broadcast_in_dim.44), calls=%async_computation.2 | async-start | bytes 524288 | tf_op jit(solution)/shard_map/all_to_all | solution.py:16

commit v13 on v6

--- a/solution.py
+++ b/solution.py
@@ -23,7 +23,6 @@
     row_tiles = reps * rows_here // edge
     inverse = lax.rsqrt(degree.astype(jnp.float32))[:, None]
     grad_pre = jnp.where(preact > 0, grad_out, jnp.zeros_like(grad_out))
-    scaled = (features.astype(jnp.float32) * inverse).astype(jnp.bfloat16)
 
     scaled_grad = (grad_pre.astype(jnp.float32) * inverse).astype(jnp.bfloat16)
     me = lax.axis_index("rep")
@@ -47,6 +46,8 @@
         pulled, weight.astype(jnp.float32), (((1,), (1,)), ((), ())), precision=HIGHEST,
         preferred_element_type=jnp.float32,
     )
+    late_features, pulled = lax.optimization_barrier((features, pulled))
+    scaled = (late_features.astype(jnp.float32) * inverse).astype(jnp.bfloat16)
     weight_local = lax.dot_general(
         scaled.astype(jnp.float32), pulled, (((0,), (0,)), ((), ())), precision=HIGHEST,
         preferred_element_type=jnp.float32,

time: 56 us -> 55.2 us (0.986)
  blocking collectives: 13.4 us -> 26.8 us
  waiting for transfers between devices: 18.9 us -> 9.27 us
  starting transfers between devices: 13.5 us -> 9.74 us
  matrix products: 2.49 us -> 1.82 us
    all_to_all x0 -> x1, blocking collectives: none -> 13.4 us  [per_device(): lax.all_to_all(terms.astype(jnp.bfloat16), 'grp', 0, 0, tiled=True)]
    all_to_all x1 -> x0, waiting for transfers between devices: 9.63 us -> none  [per_device(): lax.all_to_all(terms.astype(jnp.bfloat16), 'grp', 0, 0, tiled=True)]
    all_to_all x1 -> x0, starting transfers between devices: 3.77 us -> none  [per_device(): lax.all_to_all(terms.astype(jnp.bfloat16), 'grp', 0, 0, tiled=True)]
    dot_general x1 -> x0, other arithmetic: 0.99 us -> none  [per_device(): lax.dot_general(scaled.astype(jnp.float32), pulled, (((0,), (0,)), ((), (...]
    convert_element_type x0 -> x1, other arithmetic: none -> 0.96 us  [per_device(): scaled_grad = (grad_pre.astype(jnp.float32) * inverse).astype(jnp.bfloat16)]
    dot_general x1, matrix products: 1.27 us -> 0.49 us  [per_device(): jnp.einsum('hcsij,hif->cjf', masked, block_scaled_grad, preferred_element...]
  transfers between devices with their start and end apart: 5 -> 4, of which waited for: 2 -> 1; matrix products, arithmetic and copies ran while one was open for 8% -> 8% of each run, Pallas kernels for 0% -> 0%
where the time goes in v13:
time: 55.2 us; the launch traced here: 54.9 us
  blocking collectives  26.8 us (49%)
  starting transfers between devices  9.74 us (18%)
  waiting for transfers between devices  9.27 us (17%)
  other arithmetic  4.98 us (9%)
  matrix products  1.82 us (3%)
  local copies, waits for them, and re-layouts  1.52 us (3%)
  between operations  0.72 us (1%)
    all_to_all x1, blocking collectives, per_device(): lax.all_to_all(terms.astype(jnp.bfloat16), 'grp', 0, 0, tiled=True)  13.4 us
    all_to_all x1, blocking collectives, all_reduce_a2a(): owned = lax.all_to_all(chunks, axes, 0, 0, tiled=True).sum(0)  13.4 us
    all_to_all x1, waiting for transfers between devices, all_reduce_a2a(): return lax.all_to_all(spread, axes, 0, 0, tiled=True).reshape(w.shape)  9.23 us
    ppermute x3, starting transfers between devices, per_device(): lax.ppermute(scaled_grad, 'rep', [((i + shift) % reps, i) for i in range(...  7.01 us
    all_to_all x1, starting transfers between devices, all_reduce_a2a(): return lax.all_to_all(spread, axes, 0, 0, tiled=True).reshape(w.shape)  2.72 us
    reduce_sum x1, other arithmetic, per_device(): jnp.einsum('hcsij,hif->cjf', masked, block_scaled_grad, preferred_element...  2.52 us
  transfers between devices with their start and end apart: 4, of which 1 were waited for; matrix products, arithmetic and copies ran while one was open for 8% of the time, Pallas kernels for 0%

profile of v13, /device:TPU:0, one launch (start us, length us, event | category | flops | bytes accessed | tf_op | source)
XLA Modules:
  0.0 54.9 jit_solution(13898968462323519097)
XLA Ops:
  0.6 0.0 copy-start
  0.6 0.7 %convert_rsqrt_fusion = f32[128]{0:T(128)S(1)} fusion(s32[128]{0:T(128)} %param.11), kind=kLoop, calls=%fused_computation.23 | loop fusion | flops 128 | bytes 1024 | tf_op jit(solution)/shard_map/rsqrt | solution.py:24
  1.3 1.0 %multiply_convert_fusion.1 = bf16[128,256]{1,0:T(8,128)(2,1)S(1)} fusion(bf16[128,256]{1,0:T(8,128)(2,1)} %param.10, bf16[128,256]{1,0:T(8,128)(2,1)} %param.9, f32[128]{0:T(128)S(1)} %convert_rsqrt_fusion), kind=kLoop, calls=%fused_computation.14 | loop fusion | flops 163840 | bytes 197120 | tf_op jit(solution)/shard_map/convert_element_type | solution.py:27
  2.3 3.1 %collective-permute-start.2 = (bf16[128,256]{1,0:T(8,128)(2,1)S(1)}, bf16[128,256]{1,0:T(8,128)(2,1)S(1)}, u32[]{:S(2)}, u32[]{:S(2)}) collective-permute-start(bf16[128,256]{1,0:T(8,128)(2,1)S(1)} %multiply_convert_fusion.1), channel_id=1, source_target_pairs={{3,0},{0,1},{1,2},{2,3},{7,4},{4,5},{5,6},{6,7},{11,8},{8,9},{9,10... | collective-permute-start | bytes 196616 | tf_op jit(solution)/shard_map/ppermute | solution.py:31
  5.4 2.6 %collective-permute-start.1 = (bf16[128,256]{1,0:T(8,128)(2,1)S(1)}, bf16[128,256]{1,0:T(8,128)(2,1)S(1)}, u32[]{:S(2)}, u32[]{:S(2)}) collective-permute-start(bf16[128,256]{1,0:T(8,128)(2,1)S(1)} %multiply_convert_fusion.1), channel_id=1, source_target_pairs={{2,0},{3,1},{0,2},{1,3},{6,4},{7,5},{4,6},{5,7},{10,8},{11,9},{8,1... | collective-permute-start | bytes 196616 | tf_op jit(solution)/shard_map/ppermute | solution.py:31
  8.0 1.3 %collective-permute-start = (bf16[128,256]{1,0:T(8,128)(2,1)S(1)}, bf16[128,256]{1,0:T(8,128)(2,1)S(1)}, u32[]{:S(2)}, u32[]{:S(2)}) collective-permute-start(bf16[128,256]{1,0:T(8,128)(2,1)S(1)} %multiply_convert_fusion.1), channel_id=1, source_target_pairs={{1,0},{2,1},{3,2},{0,3},{5,4},{6,5},{7,6},{4,7},{9,8},{10,9},{11,1... | collective-permute-start | bytes 196616 | tf_op jit(solution)/shard_map/ppermute | solution.py:31
  9.3 0.7 %fusion.9 = s32[8,4]{0,1:T(4,128)S(1)} fusion(s32[8,4]{0,1:T(4,128)} %param.13, s32[]{:T(128)S(6)} %axis_index.12), kind=kLoop, calls=%fused_computation.22 | loop fusion | flops 480 | bytes 260 | tf_op jit(solution)/shard_map/jit(_where)/select_n | solution.py:35
  10.0 0.1 copy.10
  10.1 2.5 %convert_reduce_fusion = bf16[4,8,128,128]{3,2,1,0:T(8,128)(2,1)S(1)} fusion(pred[4,8,4]{2,1,0:T(8,128)(4,1)S(1)} %iota_compare_fusion, bf16[8,4,128,128]{3,2,1,0:T(8,128)(2,1)} %param.12), kind=kLoop, calls=%fused_computation | loop fusion | flops 5767168 | bytes 2097280 | tf_op jit(solution)/shard_map/hcsij,hif->cjf/reduce_sum | solution.py:38
  12.6 0.0 collective-permute-done.2
  12.6 0.0 collective-permute-done.1
  12.7 0.0 collective-permute-done
  12.7 0.5 fusion
  13.2 0.0 copy-start.1
  13.2 13.4 %all_to_all.15 = bf16[8,128,256]{2,1,0:T(8,128)(2,1)S(1)} all-to-all(bf16[8,128,256]{2,1,0:T(8,128)(2,1)S(1)} %fusion), channel_id=1, replica_groups=mesh['grp'=8,'rep'=4] {'grp'}, dimensions={0} | all-to-all | bytes 1048576 | tf_op jit(solution)/shard_map/all_to_all | solution.py:42
  26.6 0.1 convert_reduce_fusion.1
  26.7 0.0 copy-done.1
  26.7 0.4 convolution_bitcast_fusion.1
  27.1 13.4 %all_to_all.16 = f32[32,8,256]{2,1,0:T(8,128)S(1)} all-to-all(f32[32,8,256]{2,1,0:T(8,128)S(1)} %convolution_bitcast_fusion.1), channel_id=1, replica_groups=mesh['grp'=8,'rep'=4] {'grp','rep'}, dimensions={0} | all-to-all | bytes 524288 | tf_op jit(solution)/shard_map/all_to_all | solution.py:14
  40.5 0.7 %broadcast_in_dim.44 = f32[32,8,256]{2,1,0:T(8,128)} broadcast(f32[8,256]{1,0:T(8,128)S(1)} %reduce_sum.29), dimensions={1,2} | broadcast | bytes 270336 | tf_op jit(solution)/shard_map/broadcast_in_dim | solution.py:15
  41.2 2.7 %all-to-all-start.2 = ((f32[32,8,256]{2,1,0:T(8,128)}), f32[32,8,256]{2,1,0:T(8,128)S(1)}, u32[]{:S(2)}, u32[]{:S(2)}) async-start(f32[32,8,256]{2,1,0:T(8,128)} %broadcast_in_dim.44), calls=%async_computation.2 | async-start | bytes 524288 | tf_op jit(solution)/shard_map/all_to_all | solution.py:16
  44.0 0.0 copy-done
  44.0 1.0 %convolution_multiply_fusion = f32[128,256]{1,0:T(8,128)} fusion(f32[128,256]{1,0:T(8,128)S(1)} %convert_reduce_fusion.1, bf16[256,256]{1,0:T(8,128)(2,1)S(1)} %copy-done, f32[128]{0:T(128)S(1)} %convert_rsqrt_fusion), kind=kOutput, calls=%fused_computation.4 | convolution fusion | flops 100696064 | bytes 393728 | tf_op jit(solution)/shard_map/dot_general | solution.py:45
  44.9 9.2 %all-to-all-done.2 = f32[32,8,256]{2,1,0:T(8,128)S(1)} async-done(((f32[32,8,256]{2,1,0:T(8,128)}), f32[32,8,256]{2,1,0:T(8,128)S(1)}, u32[]{:S(2)}, u32[]{:S(2)}) %all-to-all-start.2) | async-done | bytes 262176 | tf_op jit(solution)/shard_map/all_to_all | solution.py:16
  54.2 0.7 %copy.15 = f32[256,256]{1,0:T(8,128)} copy(f32[256,256]{1,0:T(8,128)S(1)} %bitcast.20) | data formatting | bytes 524288
  (2 shorter events, 0.0 us)
Async XLA Ops:
  0.6 43.3 %copy-start = (bf16[256,256]{1,0:T(8,128)(2,1)S(1)}, bf16[256,256]{1,0:T(8,128)(2,1)}, u32[]{:S(2)}) copy-start(bf16[256,256]{1,0:T(8,128)(2,1)} %param.8) | copy-start | bytes 393220
  2.3 10.3 %collective-permute-start.2 = (bf16[128,256]{1,0:T(8,128)(2,1)S(1)}, bf16[128,256]{1,0:T(8,128)(2,1)S(1)}, u32[]{:S(2)}, u32[]{:S(2)}) collective-permute-start(bf16[128,256]{1,0:T(8,128)(2,1)S(1)} %multiply_convert_fusion.1), channel_id=1, source_target_pairs={{3,0},{0,1},{1,2},{2,3},{7,4},{4,5},{5,6},{6,7},{11,8},{8,9},{9,10... | collective-permute-start | bytes 196616 | tf_op jit(solution)/shard_map/ppermute | solution.py:31
  5.4 7.3 %collective-permute-start.1 = (bf16[128,256]{1,0:T(8,128)(2,1)S(1)}, bf16[128,256]{1,0:T(8,128)(2,1)S(1)}, u32[]{:S(2)}, u32[]{:S(2)}) collective-permute-start(bf16[128,256]{1,0:T(8,128)(2,1)S(1)} %multiply_convert_fusion.1), channel_id=1, source_target_pairs={{2,0},{3,1},{0,2},{1,3},{6,4},{7,5},{4,6},{5,7},{10,8},{11,9},{8,1... | collective-permute-start | bytes 196616 | tf_op jit(solution)/shard_map/ppermute | solution.py:31
  8.0 4.7 %collective-permute-start = (bf16[128,256]{1,0:T(8,128)(2,1)S(1)}, bf16[128,256]{1,0:T(8,128)(2,1)S(1)}, u32[]{:S(2)}, u32[]{:S(2)}) collective-permute-start(bf16[128,256]{1,0:T(8,128)(2,1)S(1)} %multiply_convert_fusion.1), channel_id=1, source_target_pairs={{1,0},{2,1},{3,2},{0,3},{5,4},{6,5},{7,6},{4,7},{9,8},{10,9},{11,1... | collective-permute-start | bytes 196616 | tf_op jit(solution)/shard_map/ppermute | solution.py:31
  13.2 13.5 %copy-start.1 = (bf16[128,256]{1,0:T(8,128)(2,1)S(1)}, bf16[128,256]{1,0:T(8,128)(2,1)}, u32[]{:S(2)}) copy-start(bf16[128,256]{1,0:T(8,128)(2,1)} %param.7) | copy-start | bytes 196612
  41.2 12.9 %all-to-all-start.2 = ((f32[32,8,256]{2,1,0:T(8,128)}), f32[32,8,256]{2,1,0:T(8,128)S(1)}, u32[]{:S(2)}, u32[]{:S(2)}) async-start(f32[32,8,256]{2,1,0:T(8,128)} %broadcast_in_dim.44), calls=%async_computation.2 | async-start | bytes 524288 | tf_op jit(solution)/shard_map/all_to_all | solution.py:16

commit v14 on v13

--- a/solution.py
+++ b/solution.py
@@ -48,9 +48,13 @@
     )
     late_features, pulled = lax.optimization_barrier((features, pulled))
     scaled = (late_features.astype(jnp.float32) * inverse).astype(jnp.bfloat16)
-    weight_local = lax.dot_general(
-        scaled.astype(jnp.float32), pulled, (((0,), (0,)), ((), ())), precision=HIGHEST,
-        preferred_element_type=jnp.float32,
+    pulled_high = pulled.astype(jnp.bfloat16)
+    pulled_low = (pulled - pulled_high.astype(jnp.float32)).astype(jnp.bfloat16)
+    weight_local = sum(
+        lax.dot_general(
+            scaled, part, (((0,), (0,)), ((), ())), preferred_element_type=jnp.float32
+        )
+        for part in (pulled_high, pulled_low)
     )
     weight_grad = all_reduce_a2a(weight_local, ("grp", "rep"))
     return (input_grad, weight_grad)

time: 55.2 us -> 55.4 us (level)
  no operation moved by 1% of the time
where the time goes in v14:
time: 55.4 us; the launch traced here: 55 us
  blocking collectives  26.8 us (48%)
  starting transfers between devices  9.74 us (18%)
  waiting for transfers between devices  9.27 us (17%)
  other arithmetic  4.98 us (9%)
  matrix products  2 us (4%)
  local copies, waits for them, and re-layouts  1.52 us (3%)
  between operations  0.73 us (1%)
    all_to_all x1, blocking collectives, per_device(): lax.all_to_all(terms.astype(jnp.bfloat16), 'grp', 0, 0, tiled=True)  13.4 us
    all_to_all x1, blocking collectives, all_reduce_a2a(): owned = lax.all_to_all(chunks, axes, 0, 0, tiled=True).sum(0)  13.4 us
    all_to_all x1, waiting for transfers between devices, all_reduce_a2a(): return lax.all_to_all(spread, axes, 0, 0, tiled=True).reshape(w.shape)  9.23 us
    ppermute x3, starting transfers between devices, per_device(): lax.ppermute(scaled_grad, 'rep', [((i + shift) % reps, i) for i in range(...  7.01 us
    all_to_all x1, starting transfers between devices, all_reduce_a2a(): return lax.all_to_all(spread, axes, 0, 0, tiled=True).reshape(w.shape)  2.72 us
    reduce_sum x1, other arithmetic, per_device(): jnp.einsum('hcsij,hif->cjf', masked, block_scaled_grad, preferred_element...  2.52 us
  transfers between devices with their start and end apart: 4, of which 1 were waited for; matrix products, arithmetic and copies ran while one was open for 8% of the time, Pallas kernels for 0%

profile of v14, /device:TPU:0, one launch (start us, length us, event | category | flops | bytes accessed | tf_op | source)
XLA Modules:
  0.0 55.0 jit_solution(6093060570722514221)
XLA Ops:
  0.6 0.0 copy-start
  0.6 0.7 %convert_rsqrt_fusion = f32[128]{0:T(128)S(1)} fusion(s32[128]{0:T(128)} %param.11), kind=kLoop, calls=%fused_computation.27 | loop fusion | flops 128 | bytes 1024 | tf_op jit(solution)/shard_map/rsqrt | solution.py:24
  1.3 1.0 %multiply_convert_fusion.1 = bf16[128,256]{1,0:T(8,128)(2,1)S(1)} fusion(bf16[128,256]{1,0:T(8,128)(2,1)} %param.10, bf16[128,256]{1,0:T(8,128)(2,1)} %param.9, f32[128]{0:T(128)S(1)} %convert_rsqrt_fusion), kind=kLoop, calls=%fused_computation.16 | loop fusion | flops 163840 | bytes 197120 | tf_op jit(solution)/shard_map/convert_element_type | solution.py:27
  2.3 3.1 %collective-permute-start.2 = (bf16[128,256]{1,0:T(8,128)(2,1)S(1)}, bf16[128,256]{1,0:T(8,128)(2,1)S(1)}, u32[]{:S(2)}, u32[]{:S(2)}) collective-permute-start(bf16[128,256]{1,0:T(8,128)(2,1)S(1)} %multiply_convert_fusion.1), channel_id=1, source_target_pairs={{3,0},{0,1},{1,2},{2,3},{7,4},{4,5},{5,6},{6,7},{11,8},{8,9},{9,10... | collective-permute-start | bytes 196616 | tf_op jit(solution)/shard_map/ppermute | solution.py:31
  5.4 2.6 %collective-permute-start.1 = (bf16[128,256]{1,0:T(8,128)(2,1)S(1)}, bf16[128,256]{1,0:T(8,128)(2,1)S(1)}, u32[]{:S(2)}, u32[]{:S(2)}) collective-permute-start(bf16[128,256]{1,0:T(8,128)(2,1)S(1)} %multiply_convert_fusion.1), channel_id=1, source_target_pairs={{2,0},{3,1},{0,2},{1,3},{6,4},{7,5},{4,6},{5,7},{10,8},{11,9},{8,1... | collective-permute-start | bytes 196616 | tf_op jit(solution)/shard_map/ppermute | solution.py:31
  8.0 1.3 %collective-permute-start = (bf16[128,256]{1,0:T(8,128)(2,1)S(1)}, bf16[128,256]{1,0:T(8,128)(2,1)S(1)}, u32[]{:S(2)}, u32[]{:S(2)}) collective-permute-start(bf16[128,256]{1,0:T(8,128)(2,1)S(1)} %multiply_convert_fusion.1), channel_id=1, source_target_pairs={{1,0},{2,1},{3,2},{0,3},{5,4},{6,5},{7,6},{4,7},{9,8},{10,9},{11,1... | collective-permute-start | bytes 196616 | tf_op jit(solution)/shard_map/ppermute | solution.py:31
  9.3 0.7 %fusion.12 = s32[8,4]{0,1:T(4,128)S(1)} fusion(s32[8,4]{0,1:T(4,128)} %param.13, s32[]{:T(128)S(6)} %axis_index.12), kind=kLoop, calls=%fused_computation.26 | loop fusion | flops 480 | bytes 260 | tf_op jit(solution)/shard_map/jit(_where)/select_n | solution.py:35
  10.0 0.1 copy.10
  10.1 2.5 %convert_reduce_fusion = bf16[4,8,128,128]{3,2,1,0:T(8,128)(2,1)S(1)} fusion(pred[4,8,4]{2,1,0:T(8,128)(4,1)S(1)} %iota_compare_fusion, bf16[8,4,128,128]{3,2,1,0:T(8,128)(2,1)} %param.12), kind=kLoop, calls=%fused_computation | loop fusion | flops 5767168 | bytes 2097280 | tf_op jit(solution)/shard_map/hcsij,hif->cjf/reduce_sum | solution.py:38
  12.6 0.0 collective-permute-done.2
  12.6 0.0 collective-permute-done.1
  12.7 0.0 collective-permute-done
  12.7 0.5 fusion
  13.2 0.0 copy-start.1
  13.2 13.4 %all_to_all.15 = bf16[8,128,256]{2,1,0:T(8,128)(2,1)S(1)} all-to-all(bf16[8,128,256]{2,1,0:T(8,128)(2,1)S(1)} %fusion), channel_id=1, replica_groups=mesh['grp'=8,'rep'=4] {'grp'}, dimensions={0} | all-to-all | bytes 1048576 | tf_op jit(solution)/shard_map/all_to_all | solution.py:42
  26.6 0.1 convert_reduce_fusion.1
  26.7 0.0 copy-done.1
  26.7 0.3 fusion.9
  27.0 0.3 fusion.1
  27.3 13.4 %all_to_all.16 = f32[32,8,256]{2,1,0:T(8,128)S(1)} all-to-all(f32[32,8,256]{2,1,0:T(8,128)S(1)} %fusion.1), channel_id=1, replica_groups=mesh['grp'=8,'rep'=4] {'grp','rep'}, dimensions={0} | all-to-all | bytes 524288 | tf_op jit(solution)/shard_map/all_to_all | solution.py:14
  40.7 0.7 %broadcast_in_dim.44 = f32[32,8,256]{2,1,0:T(8,128)} broadcast(f32[8,256]{1,0:T(8,128)S(1)} %reduce_sum.29), dimensions={1,2} | broadcast | bytes 270336 | tf_op jit(solution)/shard_map/broadcast_in_dim | solution.py:15
  41.4 2.7 %all-to-all-start.2 = ((f32[32,8,256]{2,1,0:T(8,128)}), f32[32,8,256]{2,1,0:T(8,128)S(1)}, u32[]{:S(2)}, u32[]{:S(2)}) async-start(f32[32,8,256]{2,1,0:T(8,128)} %broadcast_in_dim.44), calls=%async_computation.2 | async-start | bytes 524288 | tf_op jit(solution)/shard_map/all_to_all | solution.py:16
  44.1 0.0 copy-done
  44.2 1.0 %convolution_multiply_fusion = f32[128,256]{1,0:T(8,128)} fusion(f32[128,256]{1,0:T(8,128)S(1)} %convert_reduce_fusion.1, bf16[256,256]{1,0:T(8,128)(2,1)S(1)} %copy-done, f32[128]{0:T(128)S(1)} %convert_rsqrt_fusion), kind=kOutput, calls=%fused_computation.5 | convolution fusion | flops 100696064 | bytes 393728 | tf_op jit(solution)/shard_map/dot_general | solution.py:45
  45.1 9.2 %all-to-all-done.2 = f32[32,8,256]{2,1,0:T(8,128)S(1)} async-done(((f32[32,8,256]{2,1,0:T(8,128)}), f32[32,8,256]{2,1,0:T(8,128)S(1)}, u32[]{:S(2)}, u32[]{:S(2)}) %all-to-all-start.2) | async-done | bytes 262176 | tf_op jit(solution)/shard_map/all_to_all | solution.py:16
  54.3 0.7 %copy.15 = f32[256,256]{1,0:T(8,128)} copy(f32[256,256]{1,0:T(8,128)S(1)} %bitcast.19) | data formatting | bytes 524288
  (2 shorter events, 0.0 us)
Async XLA Ops:
  0.6 43.5 %copy-start = (bf16[256,256]{1,0:T(8,128)(2,1)S(1)}, bf16[256,256]{1,0:T(8,128)(2,1)}, u32[]{:S(2)}) copy-start(bf16[256,256]{1,0:T(8,128)(2,1)} %param.8) | copy-start | bytes 393220
  2.3 10.3 %collective-permute-start.2 = (bf16[128,256]{1,0:T(8,128)(2,1)S(1)}, bf16[128,256]{1,0:T(8,128)(2,1)S(1)}, u32[]{:S(2)}, u32[]{:S(2)}) collective-permute-start(bf16[128,256]{1,0:T(8,128)(2,1)S(1)} %multiply_convert_fusion.1), channel_id=1, source_target_pairs={{3,0},{0,1},{1,2},{2,3},{7,4},{4,5},{5,6},{6,7},{11,8},{8,9},{9,10... | collective-permute-start | bytes 196616 | tf_op jit(solution)/shard_map/ppermute | solution.py:31
  5.4 7.3 %collective-permute-start.1 = (bf16[128,256]{1,0:T(8,128)(2,1)S(1)}, bf16[128,256]{1,0:T(8,128)(2,1)S(1)}, u32[]{:S(2)}, u32[]{:S(2)}) collective-permute-start(bf16[128,256]{1,0:T(8,128)(2,1)S(1)} %multiply_convert_fusion.1), channel_id=1, source_target_pairs={{2,0},{3,1},{0,2},{1,3},{6,4},{7,5},{4,6},{5,7},{10,8},{11,9},{8,1... | collective-permute-start | bytes 196616 | tf_op jit(solution)/shard_map/ppermute | solution.py:31
  8.0 4.7 %collective-permute-start = (bf16[128,256]{1,0:T(8,128)(2,1)S(1)}, bf16[128,256]{1,0:T(8,128)(2,1)S(1)}, u32[]{:S(2)}, u32[]{:S(2)}) collective-permute-start(bf16[128,256]{1,0:T(8,128)(2,1)S(1)} %multiply_convert_fusion.1), channel_id=1, source_target_pairs={{1,0},{2,1},{3,2},{0,3},{5,4},{6,5},{7,6},{4,7},{9,8},{10,9},{11,1... | collective-permute-start | bytes 196616 | tf_op jit(solution)/shard_map/ppermute | solution.py:31
  13.2 13.5 %copy-start.1 = (bf16[128,256]{1,0:T(8,128)(2,1)S(1)}, bf16[128,256]{1,0:T(8,128)(2,1)}, u32[]{:S(2)}) copy-start(bf16[128,256]{1,0:T(8,128)(2,1)} %param.7) | copy-start | bytes 196612
  41.4 12.9 %all-to-all-start.2 = ((f32[32,8,256]{2,1,0:T(8,128)}), f32[32,8,256]{2,1,0:T(8,128)S(1)}, u32[]{:S(2)}, u32[]{:S(2)}) async-start(f32[32,8,256]{2,1,0:T(8,128)} %broadcast_in_dim.44), calls=%async_computation.2 | async-start | bytes 524288 | tf_op jit(solution)/shard_map/all_to_all | solution.py:16

commit v15 on v6

--- a/solution.py
+++ b/solution.py
@@ -23,7 +23,6 @@
     row_tiles = reps * rows_here // edge
     inverse = lax.rsqrt(degree.astype(jnp.float32))[:, None]
     grad_pre = jnp.where(preact > 0, grad_out, jnp.zeros_like(grad_out))
-    scaled = (features.astype(jnp.float32) * inverse).astype(jnp.bfloat16)
 
     scaled_grad = (grad_pre.astype(jnp.float32) * inverse).astype(jnp.bfloat16)
     me = lax.axis_index("rep")
@@ -39,6 +38,9 @@
     terms = jnp.einsum(
         "hcsij,hif->cjf", masked, block_scaled_grad, preferred_element_type=jnp.float32
     )
+
+    late_features, terms = lax.optimization_barrier((features, terms))
+    scaled = (late_features.astype(jnp.float32) * inverse).astype(jnp.bfloat16)
 
     arrived = lax.all_to_all(terms.astype(jnp.bfloat16), "grp", 0, 0, tiled=True)
     pulled = arrived.astype(jnp.float32).sum(0)

time: 56 us -> 56 us (level)
    convert_element_type x0 -> x1, other arithmetic: none -> 0.96 us  [per_device(): scaled_grad = (grad_pre.astype(jnp.float32) * inverse).astype(jnp.bfloat16)]
    dot_general x1, other arithmetic: 0.99 us -> 0.08 us  [per_device(): lax.dot_general(scaled.astype(jnp.float32), pulled, (((0,), (0,)), ((), (...]
where the time goes in v15:
time: 56 us; the launch traced here: 55.6 us
  waiting for transfers between devices  18.8 us (34%)
  starting transfers between devices  13.5 us (24%)
  blocking collectives  13.4 us (24%)
  other arithmetic  5.06 us (9%)
  matrix products  2.49 us (4%)
  local copies, waits for them, and re-layouts  1.63 us (3%)
  between operations  0.72 us (1%)
    all_to_all x1, blocking collectives, all_reduce_a2a(): owned = lax.all_to_all(chunks, axes, 0, 0, tiled=True).sum(0)  13.4 us
    all_to_all x1, waiting for transfers between devices, per_device(): lax.all_to_all(terms.astype(jnp.bfloat16), 'grp', 0, 0, tiled=True)  9.53 us
    all_to_all x1, waiting for transfers between devices, all_reduce_a2a(): return lax.all_to_all(spread, axes, 0, 0, tiled=True).reshape(w.shape)  9.23 us
    ppermute x3, starting transfers between devices, per_device(): lax.ppermute(scaled_grad, 'rep', [((i + shift) % reps, i) for i in range(...  7.01 us
    all_to_all x1, starting transfers between devices, per_device(): lax.all_to_all(terms.astype(jnp.bfloat16), 'grp', 0, 0, tiled=True)  3.77 us
    all_to_all x1, starting transfers between devices, all_reduce_a2a(): return lax.all_to_all(spread, axes, 0, 0, tiled=True).reshape(w.shape)  2.72 us
    reduce_sum x1, other arithmetic, per_device(): jnp.einsum('hcsij,hif->cjf', masked, block_scaled_grad, preferred_element...  2.52 us
    dot_general x1, matrix products, per_device(): jnp.einsum('hcsij,hif->cjf', masked, block_scaled_grad, preferred_element...  1.27 us
  transfers between devices with their start and end apart: 5, of which 2 were waited for; matrix products, arithmetic and copies ran while one was open for 8% of the time, Pallas kernels for 0%

profile of v15, /device:TPU:0, one launch (start us, length us, event | category | flops | bytes accessed | tf_op | source)
XLA Modules:
  0.0 55.6 jit_solution(6348498414244131825)
XLA Ops:
  0.6 0.0 copy-start
  0.6 0.7 %convert_rsqrt_fusion = f32[128]{0:T(128)S(1)} fusion(s32[128]{0:T(128)} %param.11), kind=kLoop, calls=%fused_computation.24 | loop fusion | flops 128 | bytes 1024 | tf_op jit(solution)/shard_map/rsqrt | solution.py:24
  1.3 1.0 %multiply_convert_fusion.1 = bf16[128,256]{1,0:T(8,128)(2,1)S(1)} fusion(bf16[128,256]{1,0:T(8,128)(2,1)} %param.10, bf16[128,256]{1,0:T(8,128)(2,1)} %param.9, f32[128]{0:T(128)S(1)} %convert_rsqrt_fusion), kind=kLoop, calls=%fused_computation.14 | loop fusion | flops 163840 | bytes 197120 | tf_op jit(solution)/shard_map/convert_element_type | solution.py:27
  2.3 3.1 %collective-permute-start.2 = (bf16[128,256]{1,0:T(8,128)(2,1)S(1)}, bf16[128,256]{1,0:T(8,128)(2,1)S(1)}, u32[]{:S(2)}, u32[]{:S(2)}) collective-permute-start(bf16[128,256]{1,0:T(8,128)(2,1)S(1)} %multiply_convert_fusion.1), channel_id=1, source_target_pairs={{3,0},{0,1},{1,2},{2,3},{7,4},{4,5},{5,6},{6,7},{11,8},{8,9},{9,10... | collective-permute-start | bytes 196616 | tf_op jit(solution)/shard_map/ppermute | solution.py:31
  5.4 2.6 %collective-permute-start.1 = (bf16[128,256]{1,0:T(8,128)(2,1)S(1)}, bf16[128,256]{1,0:T(8,128)(2,1)S(1)}, u32[]{:S(2)}, u32[]{:S(2)}) collective-permute-start(bf16[128,256]{1,0:T(8,128)(2,1)S(1)} %multiply_convert_fusion.1), channel_id=1, source_target_pairs={{2,0},{3,1},{0,2},{1,3},{6,4},{7,5},{4,6},{5,7},{10,8},{11,9},{8,1... | collective-permute-start | bytes 196616 | tf_op jit(solution)/shard_map/ppermute | solution.py:31
  8.0 1.3 %collective-permute-start = (bf16[128,256]{1,0:T(8,128)(2,1)S(1)}, bf16[128,256]{1,0:T(8,128)(2,1)S(1)}, u32[]{:S(2)}, u32[]{:S(2)}) collective-permute-start(bf16[128,256]{1,0:T(8,128)(2,1)S(1)} %multiply_convert_fusion.1), channel_id=1, source_target_pairs={{1,0},{2,1},{3,2},{0,3},{5,4},{6,5},{7,6},{4,7},{9,8},{10,9},{11,1... | collective-permute-start | bytes 196616 | tf_op jit(solution)/shard_map/ppermute | solution.py:31
  9.3 0.7 %fusion.11 = s32[8,4]{0,1:T(4,128)S(1)} fusion(s32[8,4]{0,1:T(4,128)} %param.13, s32[]{:T(128)S(6)} %axis_index.12), kind=kLoop, calls=%fused_computation.23 | loop fusion | flops 480 | bytes 260 | tf_op jit(solution)/shard_map/jit(_where)/select_n | solution.py:35
  10.0 0.1 copy.13
  10.1 2.5 %convert_reduce_fusion = bf16[4,8,128,128]{3,2,1,0:T(8,128)(2,1)S(1)} fusion(pred[4,8,4]{2,1,0:T(8,128)(4,1)S(1)} %iota_compare_fusion, bf16[8,4,128,128]{3,2,1,0:T(8,128)(2,1)} %param.12), kind=kLoop, calls=%fused_computation | loop fusion | flops 5767168 | bytes 2097280 | tf_op jit(solution)/shard_map/hcsij,hif->cjf/reduce_sum | solution.py:38
  12.6 0.0 collective-permute-done.2
  12.6 0.0 collective-permute-done.1
  12.7 0.0 collective-permute-done
  12.7 0.0 copy-start.1
  12.7 1.3 %convolution_bitcast_fusion = bf16[8,128,256]{2,1,0:T(8,128)(2,1)} fusion(bf16[4,8,128,128]{3,2,1,0:T(8,128)(2,1)S(1)} %convert_reduce_fusion, bf16[1,128,256]{2,1,0:T(8,128)(2,1)S(1)} %bitcast.25, bf16[1,128,256]{2,1,0:T(8,128)(2,1)S(1)} %bitcast.26, bf16[1,128,256]{2,1,0:T(8,128)(2,1)S(1)} %bitcast.27, bf16[1,128,256]{2,1,0:T(8,128)(2,1)S(1)} %bitcast.24), kind=kOutput, calls=%fused_computation.1 | convolution fusion | flops 268828672 | bytes 1835008 | tf_op jit(solution)/shard_map/hcsij,hif->cjf/dot_general | solution.py:38
  14.0 3.8 %all-to-all-start = ((bf16[8,128,256]{2,1,0:T(8,128)(2,1)}), bf16[8,128,256]{2,1,0:T(8,128)(2,1)S(1)}, u32[]{:S(2)}, u32[]{:S(2)}) async-start(bf16[8,128,256]{2,1,0:T(8,128)(2,1)} %convolution_bitcast_fusion), calls=%async_computation | async-start | bytes 1048576 | tf_op jit(solution)/shard_map/all_to_all | solution.py:45
  17.7 0.0 copy-done.1
  17.7 0.1 fusion.8
  17.8 0.1 copy.15
  17.9 9.5 %all-to-all-done = bf16[8,128,256]{2,1,0:T(8,128)(2,1)S(1)} async-done(((bf16[8,128,256]{2,1,0:T(8,128)(2,1)}), bf16[8,128,256]{2,1,0:T(8,128)(2,1)S(1)}, u32[]{:S(2)}, u32[]{:S(2)}) %all-to-all-start) | async-done | bytes 524320 | tf_op jit(solution)/shard_map/all_to_all | solution.py:45
  27.5 0.1 convert_reduce_fusion.1
  27.6 0.3 fusion.6
  27.8 13.4 %all_to_all.15 = f32[32,8,256]{2,1,0:T(8,128)S(1)} all-to-all(f32[32,8,256]{2,1,0:T(8,128)S(1)} %fusion.6), channel_id=1, replica_groups=mesh['grp'=8,'rep'=4] {'grp','rep'}, dimensions={0} | all-to-all | bytes 524288 | tf_op jit(solution)/shard_map/all_to_all | solution.py:14
  41.2 0.7 %broadcast_in_dim.44 = f32[32,8,256]{2,1,0:T(8,128)} broadcast(f32[8,256]{1,0:T(8,128)S(1)} %reduce_sum.29), dimensions={1,2} | broadcast | bytes 270336 | tf_op jit(solution)/shard_map/broadcast_in_dim | solution.py:15
  42.0 2.7 %all-to-all-start.2 = ((f32[32,8,256]{2,1,0:T(8,128)}), f32[32,8,256]{2,1,0:T(8,128)S(1)}, u32[]{:S(2)}, u32[]{:S(2)}) async-start(f32[32,8,256]{2,1,0:T(8,128)} %broadcast_in_dim.44), calls=%async_computation.2 | async-start | bytes 524288 | tf_op jit(solution)/shard_map/all_to_all | solution.py:16
  44.7 0.0 copy-done
  44.7 1.0 %convolution_multiply_fusion = f32[128,256]{1,0:T(8,128)} fusion(f32[128,256]{1,0:T(8,128)S(1)} %convert_reduce_fusion.1, bf16[256,256]{1,0:T(8,128)(2,1)S(1)} %copy-done, f32[128]{0:T(128)S(1)} %convert_rsqrt_fusion), kind=kOutput, calls=%fused_computation.2 | convolution fusion | flops 100696064 | bytes 393728 | tf_op jit(solution)/shard_map/dot_general | solution.py:48
  45.6 9.2 %all-to-all-done.2 = f32[32,8,256]{2,1,0:T(8,128)S(1)} async-done(((f32[32,8,256]{2,1,0:T(8,128)}), f32[32,8,256]{2,1,0:T(8,128)S(1)}, u32[]{:S(2)}, u32[]{:S(2)}) %all-to-all-start.2) | async-done | bytes 262176 | tf_op jit(solution)/shard_map/all_to_all | solution.py:16
  54.9 0.7 %copy.19 = f32[256,256]{1,0:T(8,128)} copy(f32[256,256]{1,0:T(8,128)S(1)} %bitcast.23) | data formatting | bytes 524288
  (2 shorter events, 0.0 us)
Async XLA Ops:
  0.6 44.1 %copy-start = (bf16[256,256]{1,0:T(8,128)(2,1)S(1)}, bf16[256,256]{1,0:T(8,128)(2,1)}, u32[]{:S(2)}) copy-start(bf16[256,256]{1,0:T(8,128)(2,1)} %param.8) | copy-start | bytes 393220
  2.3 10.3 %collective-permute-start.2 = (bf16[128,256]{1,0:T(8,128)(2,1)S(1)}, bf16[128,256]{1,0:T(8,128)(2,1)S(1)}, u32[]{:S(2)}, u32[]{:S(2)}) collective-permute-start(bf16[128,256]{1,0:T(8,128)(2,1)S(1)} %multiply_convert_fusion.1), channel_id=1, source_target_pairs={{3,0},{0,1},{1,2},{2,3},{7,4},{4,5},{5,6},{6,7},{11,8},{8,9},{9,10... | collective-permute-start | bytes 196616 | tf_op jit(solution)/shard_map/ppermute | solution.py:31
  5.4 7.3 %collective-permute-start.1 = (bf16[128,256]{1,0:T(8,128)(2,1)S(1)}, bf16[128,256]{1,0:T(8,128)(2,1)S(1)}, u32[]{:S(2)}, u32[]{:S(2)}) collective-permute-start(bf16[128,256]{1,0:T(8,128)(2,1)S(1)} %multiply_convert_fusion.1), channel_id=1, source_target_pairs={{2,0},{3,1},{0,2},{1,3},{6,4},{7,5},{4,6},{5,7},{10,8},{11,9},{8,1... | collective-permute-start | bytes 196616 | tf_op jit(solution)/shard_map/ppermute | solution.py:31
  8.0 4.7 %collective-permute-start = (bf16[128,256]{1,0:T(8,128)(2,1)S(1)}, bf16[128,256]{1,0:T(8,128)(2,1)S(1)}, u32[]{:S(2)}, u32[]{:S(2)}) collective-permute-start(bf16[128,256]{1,0:T(8,128)(2,1)S(1)} %multiply_convert_fusion.1), channel_id=1, source_target_pairs={{1,0},{2,1},{3,2},{0,3},{5,4},{6,5},{7,6},{4,7},{9,8},{10,9},{11,1... | collective-permute-start | bytes 196616 | tf_op jit(solution)/shard_map/ppermute | solution.py:31
  12.7 5.0 %copy-start.1 = (bf16[128,256]{1,0:T(8,128)(2,1)S(1)}, bf16[128,256]{1,0:T(8,128)(2,1)}, u32[]{:S(2)}) copy-start(bf16[128,256]{1,0:T(8,128)(2,1)} %param.7) | copy-start | bytes 196612
  14.0 13.5 %all-to-all-start = ((bf16[8,128,256]{2,1,0:T(8,128)(2,1)}), bf16[8,128,256]{2,1,0:T(8,128)(2,1)S(1)}, u32[]{:S(2)}, u32[]{:S(2)}) async-start(bf16[8,128,256]{2,1,0:T(8,128)(2,1)} %convolution_bitcast_fusion), calls=%async_computation | async-start | bytes 1048576 | tf_op jit(solution)/shard_map/all_to_all | solution.py:45
  42.0 12.9 %all-to-all-start.2 = ((f32[32,8,256]{2,1,0:T(8,128)}), f32[32,8,256]{2,1,0:T(8,128)S(1)}, u32[]{:S(2)}, u32[]{:S(2)}) async-start(f32[32,8,256]{2,1,0:T(8,128)} %broadcast_in_dim.44), calls=%async_computation.2 | async-start | bytes 524288 | tf_op jit(solution)/shard_map/all_to_all | solution.py:16

commit v16 on v13

--- a/solution.py
+++ b/solution.py
@@ -6,14 +6,15 @@
 HIGHEST = lax.Precision.HIGHEST
 
 
-def all_reduce_a2a(w, axes):
+def all_reduce_a2a(w, axes, early):
     count = 1
     for name in axes:
         count *= lax.axis_size(name)
     chunks = w.reshape(count, w.shape[0] // count, w.shape[1])
     owned = lax.all_to_all(chunks, axes, 0, 0, tiled=True).sum(0)
     spread = jnp.broadcast_to(owned[None], chunks.shape)
-    return lax.all_to_all(spread, axes, 0, 0, tiled=True).reshape(w.shape)
+    spread, early = lax.optimization_barrier((spread, early))
+    return lax.all_to_all(spread, axes, 0, 0, tiled=True).reshape(w.shape), early
 
 
 def per_device(features, weight, preact, grad_out, degree, tile_values, tile_rows):
@@ -42,17 +43,22 @@
     arrived = lax.all_to_all(terms.astype(jnp.bfloat16), "grp", 0, 0, tiled=True)
     pulled = arrived.astype(jnp.float32).sum(0)
 
-    input_grad = inverse * lax.dot_general(
-        pulled, weight.astype(jnp.float32), (((1,), (1,)), ((), ())), precision=HIGHEST,
-        preferred_element_type=jnp.float32,
-    )
+    def projected_part(cols):
+        return lax.dot_general(
+            pulled[:, cols], weight[:, cols].astype(jnp.float32), (((1,), (1,)), ((), ())),
+            precision=HIGHEST, preferred_element_type=jnp.float32,
+        )
+
+    half = width // 2
+    first_part = projected_part(slice(0, half))
     late_features, pulled = lax.optimization_barrier((features, pulled))
     scaled = (late_features.astype(jnp.float32) * inverse).astype(jnp.bfloat16)
     weight_local = lax.dot_general(
         scaled.astype(jnp.float32), pulled, (((0,), (0,)), ((), ())), precision=HIGHEST,
         preferred_element_type=jnp.float32,
     )
-    weight_grad = all_reduce_a2a(weight_local, ("grp", "rep"))
+    weight_grad, first_part = all_reduce_a2a(weight_local, ("grp", "rep"), first_part)
+    input_grad = inverse * (first_part + projected_part(slice(half, width)))
     return (input_grad, weight_grad)
 
 

time: 55.2 us -> 56.1 us (1.016)
  blocking collectives: 26.8 us -> 13.4 us
  waiting for transfers between devices: 9.27 us -> 19.3 us
  starting transfers between devices: 9.74 us -> 13.1 us
  matrix products: 1.82 us -> 2.69 us
    all_to_all x1 -> x0, blocking collectives: 13.4 us -> none  [all_reduce_a2a(): owned = lax.all_to_all(chunks, axes, 0, 0, tiled=True).sum(0)]
    all_to_all x1 -> x2, waiting for transfers between devices: 9.23 us -> 19.3 us  [the longest x1 9.95 us: all_reduce_a2a(): owned = lax.all_to_all(chunks, axes, 0, 0, tiled=True).sum(0)]
    all_to_all x1 -> x2, starting transfers between devices: 2.72 us -> 6.09 us  [the longest x1 3.37 us: all_reduce_a2a(): owned = lax.all_to_all(chunks, axes, 0, 0, tiled=True).sum(0)]
    dot_general x1, matrix products: 0.38 us -> 1.08 us  [per_device(): lax.dot_general(scaled.astype(jnp.float32), pulled, (((0,), (0,)), ((), (...]
    dot_general x1 -> x2, matrix products: 0.96 us -> 1.12 us  [projected_part(): lax.dot_general(pulled[:, cols], weight[:, cols].astype(jnp.float32), (((...]
  transfers between devices with their start and end apart: 4 -> 5, of which waited for: 1 -> 2; matrix products, arithmetic and copies ran while one was open for 8% -> 8% of each run, Pallas kernels for 0% -> 0%
where the time goes in v16:
time: 56.1 us; the launch traced here: 55.7 us
  waiting for transfers between devices  19.3 us (34%)
  blocking collectives  13.4 us (24%)
  starting transfers between devices  13.1 us (23%)
  other arithmetic  4.94 us (9%)
  matrix products  2.69 us (5%)
  local copies, waits for them, and re-layouts  1.52 us (3%)
  between operations  0.72 us (1%)
    all_to_all x1, blocking collectives, per_device(): lax.all_to_all(terms.astype(jnp.bfloat16), 'grp', 0, 0, tiled=True)  13.4 us
    all_to_all x1, waiting for transfers between devices, all_reduce_a2a(): owned = lax.all_to_all(chunks, axes, 0, 0, tiled=True).sum(0)  9.95 us
    all_to_all x1, waiting for transfers between devices, all_reduce_a2a(): lax.all_to_all(spread, axes, 0, 0, tiled=True).reshape(w.shape)  9.31 us
    ppermute x3, starting transfers between devices, per_device(): lax.ppermute(scaled_grad, 'rep', [((i + shift) % reps, i) for i in range(...  7.01 us
    all_to_all x1, starting transfers between devices, all_reduce_a2a(): owned = lax.all_to_all(chunks, axes, 0, 0, tiled=True).sum(0)  3.37 us
    all_to_all x1, starting transfers between devices, all_reduce_a2a(): lax.all_to_all(spread, axes, 0, 0, tiled=True).reshape(w.shape)  2.72 us
    reduce_sum x1, other arithmetic, per_device(): jnp.einsum('hcsij,hif->cjf', masked, block_scaled_grad, preferred_element...  2.52 us
    dot_general x2, matrix products, projected_part(): lax.dot_general(pulled[:, cols], weight[:, cols].astype(jnp.float32), (((...  1.12 us
  transfers between devices with their start and end apart: 5, of which 2 were waited for; matrix products, arithmetic and copies ran while one was open for 8% of the time, Pallas kernels for 0%

profile of v16, /device:TPU:0, one launch (start us, length us, event | category | flops | bytes accessed | tf_op | source)
XLA Modules:
  0.0 55.7 jit_solution(3662362331212024916)
XLA Ops:
  0.6 0.7 %convert_rsqrt_fusion = f32[128]{0:T(128)S(1)} fusion(s32[128]{0:T(128)} %param.11), kind=kLoop, calls=%fused_computation.29 | loop fusion | flops 128 | bytes 1024 | tf_op jit(solution)/shard_map/rsqrt | solution.py:25
  1.3 1.0 %multiply_convert_fusion.1 = bf16[128,256]{1,0:T(8,128)(2,1)S(1)} fusion(bf16[128,256]{1,0:T(8,128)(2,1)} %param.10, bf16[128,256]{1,0:T(8,128)(2,1)} %param.9, f32[128]{0:T(128)S(1)} %convert_rsqrt_fusion), kind=kLoop, calls=%fused_computation.15 | loop fusion | flops 163840 | bytes 197120 | tf_op jit(solution)/shard_map/convert_element_type | solution.py:28
  2.3 3.1 %collective-permute-start.2 = (bf16[128,256]{1,0:T(8,128)(2,1)S(1)}, bf16[128,256]{1,0:T(8,128)(2,1)S(1)}, u32[]{:S(2)}, u32[]{:S(2)}) collective-permute-start(bf16[128,256]{1,0:T(8,128)(2,1)S(1)} %multiply_convert_fusion.1), channel_id=1, source_target_pairs={{3,0},{0,1},{1,2},{2,3},{7,4},{4,5},{5,6},{6,7},{11,8},{8,9},{9,10... | collective-permute-start | bytes 196616 | tf_op jit(solution)/shard_map/ppermute | solution.py:32
  5.3 2.6 %collective-permute-start.1 = (bf16[128,256]{1,0:T(8,128)(2,1)S(1)}, bf16[128,256]{1,0:T(8,128)(2,1)S(1)}, u32[]{:S(2)}, u32[]{:S(2)}) collective-permute-start(bf16[128,256]{1,0:T(8,128)(2,1)S(1)} %multiply_convert_fusion.1), channel_id=1, source_target_pairs={{2,0},{3,1},{0,2},{1,3},{6,4},{7,5},{4,6},{5,7},{10,8},{11,9},{8,1... | collective-permute-start | bytes 196616 | tf_op jit(solution)/shard_map/ppermute | solution.py:32
  7.9 1.3 %collective-permute-start = (bf16[128,256]{1,0:T(8,128)(2,1)S(1)}, bf16[128,256]{1,0:T(8,128)(2,1)S(1)}, u32[]{:S(2)}, u32[]{:S(2)}) collective-permute-start(bf16[128,256]{1,0:T(8,128)(2,1)S(1)} %multiply_convert_fusion.1), channel_id=1, source_target_pairs={{1,0},{2,1},{3,2},{0,3},{5,4},{6,5},{7,6},{4,7},{9,8},{10,9},{11,1... | collective-permute-start | bytes 196616 | tf_op jit(solution)/shard_map/ppermute | solution.py:32
  9.3 0.7 %fusion.15 = s32[8,4]{0,1:T(4,128)S(1)} fusion(s32[8,4]{0,1:T(4,128)} %param.13, s32[]{:T(128)S(6)} %axis_index.12), kind=kLoop, calls=%fused_computation.28 | loop fusion | flops 480 | bytes 260 | tf_op jit(solution)/shard_map/jit(_where)/select_n | solution.py:36
  10.0 0.1 copy.10
  10.1 2.5 %convert_reduce_fusion = bf16[4,8,128,128]{3,2,1,0:T(8,128)(2,1)S(1)} fusion(pred[4,8,4]{2,1,0:T(8,128)(4,1)S(1)} %iota_compare_fusion, bf16[8,4,128,128]{3,2,1,0:T(8,128)(2,1)} %param.12), kind=kLoop, calls=%fused_computation | loop fusion | flops 5767168 | bytes 2097280 | tf_op jit(solution)/shard_map/hcsij,hif->cjf/reduce_sum | solution.py:39
  12.6 0.0 collective-permute-done.2
  12.6 0.0 collective-permute-done.1
  12.6 0.0 collective-permute-done
  12.6 0.5 fusion
  13.1 0.0 copy-start.1
  13.1 13.4 %all_to_all.15 = bf16[8,128,256]{2,1,0:T(8,128)(2,1)S(1)} all-to-all(bf16[8,128,256]{2,1,0:T(8,128)(2,1)S(1)} %fusion), channel_id=1, replica_groups=mesh['grp'=8,'rep'=4] {'grp'}, dimensions={0} | all-to-all | bytes 1048576 | tf_op jit(solution)/shard_map/all_to_all | solution.py:43
  26.6 0.0 copy-start
  26.6 0.1 convert_reduce_fusion.1
  26.7 0.0 copy-done.1
  26.7 1.1 %convolution_bitcast_fusion.1 = f32[32,8,256]{2,1,0:T(8,128)} fusion(f32[128,256]{1,0:T(8,128)S(1)} %convert_reduce_fusion.1, bf16[128,256]{1,0:T(8,128)(2,1)S(1)} %copy-done.1, f32[128]{0:T(128)S(1)} %convert_rsqrt_fusion), kind=kOutput, calls=%fused_computation.3 | convolution fusion | flops 100761600 | bytes 459264 | tf_op jit(solution)/shard_map/dot_general | solution.py:56
  27.8 3.4 %all-to-all-start.1 = ((f32[32,8,256]{2,1,0:T(8,128)}), f32[32,8,256]{2,1,0:T(8,128)S(1)}, u32[]{:S(2)}, u32[]{:S(2)}) async-start(f32[32,8,256]{2,1,0:T(8,128)} %convolution_bitcast_fusion.1), calls=%async_computation.1 | async-start | bytes 524288 | tf_op jit(solution)/shard_map/all_to_all | solution.py:14
  31.1 0.0 copy-done
  31.1 0.2 fusion.8
  31.4 9.9 %all-to-all-done.1 = f32[32,8,256]{2,1,0:T(8,128)S(1)} async-done(((f32[32,8,256]{2,1,0:T(8,128)}), f32[32,8,256]{2,1,0:T(8,128)S(1)}, u32[]{:S(2)}, u32[]{:S(2)}) %all-to-all-start.1) | async-done | bytes 262176 | tf_op jit(solution)/shard_map/all_to_all | solution.py:14
  41.4 0.7 %broadcast_in_dim.44 = f32[32,8,256]{2,1,0:T(8,128)} broadcast(f32[8,256]{1,0:T(8,128)S(1)} %reduce_sum.29), dimensions={1,2} | broadcast | bytes 270336 | tf_op jit(solution)/shard_map/broadcast_in_dim | solution.py:15
  42.1 2.7 %all-to-all-start.2 = ((f32[32,8,256]{2,1,0:T(8,128)}), f32[32,8,256]{2,1,0:T(8,128)S(1)}, u32[]{:S(2)}, u32[]{:S(2)}) async-start(f32[32,8,256]{2,1,0:T(8,128)} %broadcast_in_dim.44), calls=%async_computation.2 | async-start | bytes 524288 | tf_op jit(solution)/shard_map/all_to_all | solution.py:17
  44.8 0.9 %fusion.1 = f32[128,256]{1,0:T(8,128)} fusion(f32[128,256]{1,0:T(8,128)S(1)} %fusion.8, bf16[256,256]{1,0:T(8,128)(2,1)S(1)} %copy-done, f32[128,256]{1,0:T(8,128)S(1)} %convert_reduce_fusion.1, f32[128]{0:T(128)S(1)} %convert_rsqrt_fusion), kind=kOutput, calls=%fused_computation.5 | convolution fusion | flops 50397184 | bytes 393728 | tf_op jit(solution)/shard_map/dot_general | solution.py:47
  45.7 9.3 %all-to-all-done.2 = f32[32,8,256]{2,1,0:T(8,128)S(1)} async-done(((f32[32,8,256]{2,1,0:T(8,128)}), f32[32,8,256]{2,1,0:T(8,128)S(1)}, u32[]{:S(2)}, u32[]{:S(2)}) %all-to-all-start.2) | async-done | bytes 262176 | tf_op jit(solution)/shard_map/all_to_all | solution.py:17
  55.0 0.7 %copy.15 = f32[256,256]{1,0:T(8,128)} copy(f32[256,256]{1,0:T(8,128)S(1)} %bitcast.18) | data formatting | bytes 524288
  (2 shorter events, 0.0 us)
Async XLA Ops:
  2.3 10.3 %collective-permute-start.2 = (bf16[128,256]{1,0:T(8,128)(2,1)S(1)}, bf16[128,256]{1,0:T(8,128)(2,1)S(1)}, u32[]{:S(2)}, u32[]{:S(2)}) collective-permute-start(bf16[128,256]{1,0:T(8,128)(2,1)S(1)} %multiply_convert_fusion.1), channel_id=1, source_target_pairs={{3,0},{0,1},{1,2},{2,3},{7,4},{4,5},{5,6},{6,7},{11,8},{8,9},{9,10... | collective-permute-start | bytes 196616 | tf_op jit(solution)/shard_map/ppermute | solution.py:32
  5.3 7.3 %collective-permute-start.1 = (bf16[128,256]{1,0:T(8,128)(2,1)S(1)}, bf16[128,256]{1,0:T(8,128)(2,1)S(1)}, u32[]{:S(2)}, u32[]{:S(2)}) collective-permute-start(bf16[128,256]{1,0:T(8,128)(2,1)S(1)} %multiply_convert_fusion.1), channel_id=1, source_target_pairs={{2,0},{3,1},{0,2},{1,3},{6,4},{7,5},{4,6},{5,7},{10,8},{11,9},{8,1... | collective-permute-start | bytes 196616 | tf_op jit(solution)/shard_map/ppermute | solution.py:32
  7.9 4.7 %collective-permute-start = (bf16[128,256]{1,0:T(8,128)(2,1)S(1)}, bf16[128,256]{1,0:T(8,128)(2,1)S(1)}, u32[]{:S(2)}, u32[]{:S(2)}) collective-permute-start(bf16[128,256]{1,0:T(8,128)(2,1)S(1)} %multiply_convert_fusion.1), channel_id=1, source_target_pairs={{1,0},{2,1},{3,2},{0,3},{5,4},{6,5},{7,6},{4,7},{9,8},{10,9},{11,1... | collective-permute-start | bytes 196616 | tf_op jit(solution)/shard_map/ppermute | solution.py:32
  13.1 13.5 %copy-start.1 = (bf16[128,256]{1,0:T(8,128)(2,1)S(1)}, bf16[128,256]{1,0:T(8,128)(2,1)}, u32[]{:S(2)}) copy-start(bf16[128,256]{1,0:T(8,128)(2,1)} %param.7) | copy-start | bytes 196612
  26.6 4.5 %copy-start = (bf16[256,256]{1,0:T(8,128)(2,1)S(1)}, bf16[256,256]{1,0:T(8,128)(2,1)}, u32[]{:S(2)}) copy-start(bf16[256,256]{1,0:T(8,128)(2,1)} %param.8) | copy-start | bytes 393220
  27.8 13.6 %all-to-all-start.1 = ((f32[32,8,256]{2,1,0:T(8,128)}), f32[32,8,256]{2,1,0:T(8,128)S(1)}, u32[]{:S(2)}, u32[]{:S(2)}) async-start(f32[32,8,256]{2,1,0:T(8,128)} %convolution_bitcast_fusion.1), calls=%async_computation.1 | async-start | bytes 524288 | tf_op jit(solution)/shard_map/all_to_all | solution.py:14
  42.1 12.9 %all-to-all-start.2 = ((f32[32,8,256]{2,1,0:T(8,128)}), f32[32,8,256]{2,1,0:T(8,128)S(1)}, u32[]{:S(2)}, u32[]{:S(2)}) async-start(f32[32,8,256]{2,1,0:T(8,128)} %broadcast_in_dim.44), calls=%async_computation.2 | async-start | bytes 524288 | tf_op jit(solution)/shard_map/all_to_all | solution.py:17
